TPU v7x, 128 devices: a whole 4x4x4 slice. The times are simulated.
128 devices in a mesh: seq: 16 (over y, x), grp: 8 (over z, core).
Axes of the slice: x: 4, y: 4, z: 4, core: 2. Of those that a mesh axis runs over, the one named last changes fastest.
Arguments:
- patches: bfloat16 [16384, 1664], P(('grp', 'seq')), may hold values from -6 to 6
- vis_gain: float32 [1664], replicated, may hold values from 0.25 to 1.75
- vis_qkv: bfloat16 [3, 1664, 1664], P(None, None, 'seq')
- vis_out: bfloat16 [1664, 1664], P('seq'), may hold values from -0.15625 to 0.15625
- merge_gain: float32 [1664], replicated, may hold values from 0.25 to 1.75
- merge_w: bfloat16 [6656, 1664], P('seq'), may hold values from -0.078125 to 0.078125
- image_blocks: int32 [8, 4], P('grp'), may hold values from 1 to 256, 512 in all within a row
- dest_group: int32 [4096, 1], P(('grp', 'seq')), may hold values from 0 to 7; in each aligned block of 32 rows (0 to 31, 32 to 63, ...) at most 8 rows name the same one
- slot_rows: int32 [8, 16, 128], P('grp', 'seq'), may hold values from 0 to 127, each once within a row
- prompt_len: int32 [8], P('grp'), may hold values from 512 to 2048
- text_emb: bfloat16 [16384, 1664], P(('grp', 'seq')), may hold values from -6 to 6
- txt_gain: float32 [1664], replicated, may hold values from 0.25 to 1.75
- txt_qkv: bfloat16 [3, 1664, 1664], P(None, None, 'seq')
- txt_out: bfloat16 [1664, 1664], P('seq'), may hold values from -0.15625 to 0.15625
Outputs:
- text_out: float32 [16384, 1664], P(('grp', 'seq'))
Inputs may be any that keep to these rules, and one draw needn't show every extreme that they name: image_blocks[g] sum to 512; one image of every group has the most. `dest_group`: of the 32 merged tokens of one device (aligned blocks of rows), at most 8 name one group. slot_rows[q, s] is a permutation of 0 to 127.
All inputs are finite; a program needn't handle non-finite values.
Results may differ from a plain program's by a relative error of at most 0.012.
Values may be sent and summed in bfloat16 or wider, within the bound.
No kernel may reach another device: no remote copies, remote signals or barrier semaphores. Data moves between devices by JAX's collectives and lax.ppermute only.
A program may use at most 64 MiB of HBM per device.

v0:
```python
import jax
import jax.numpy as jnp
from jax import lax
from jax.sharding import PartitionSpec as P

HEAD_DIM = 104


def layer_norm(row_block, scale_gain):
    values_f = row_block.astype(jnp.float32)
    row_mean = jnp.mean(values_f, axis=-1, keepdims=True)
    centred = values_f - row_mean
    variance = jnp.mean(centred * centred, axis=-1, keepdims=True)
    return centred * lax.rsqrt(variance + 1e-06) * scale_gain


def rms_norm(row_block, scale_gain):
    values_f = row_block.astype(jnp.float32)
    return (
        values_f
        * lax.rsqrt(jnp.mean(values_f * values_f, axis=-1, keepdims=True) + 1e-06)
        * scale_gain
    )


def projector(weights, shard_piece):
    return jnp.einsum(
        "rd,kde->kre", shard_piece, weights, preferred_element_type=jnp.float32
    ).astype(jnp.bfloat16)


def attend_local(queries, key_rows, value_rows, allowed_fn):
    length = queries.shape[0]
    head_width = queries.shape[1]
    head_count = head_width // HEAD_DIM
    block_rows = min(512, length)
    block_count = length // block_rows
    query_blocks = queries.reshape(block_count, block_rows, head_count, HEAD_DIM)
    key_heads = key_rows.reshape(length, head_count, HEAD_DIM)
    value_heads = value_rows.reshape(length, head_count, HEAD_DIM)

    def one_block(block_item):
        query_part, first_row = block_item
        scores = jnp.einsum(
            "qhe,khe->hqk", query_part, key_heads, preferred_element_type=jnp.float32
        ) * HEAD_DIM ** (-0.5)
        allowed = allowed_fn(first_row + jnp.arange(block_rows, dtype=jnp.int32))
        scores = jnp.where(allowed[None], scores, -1e30)
        row_max = jnp.max(scores, axis=-1, keepdims=True)
        expo = jnp.exp(scores - row_max)
        probabilities = (expo / jnp.sum(expo, axis=-1, keepdims=True)).astype(jnp.bfloat16)
        return jnp.einsum(
            "hqk,khe->qhe", probabilities, value_heads, preferred_element_type=jnp.float32
        ).astype(jnp.bfloat16)

    starts = jnp.arange(block_count, dtype=jnp.int32) * block_rows
    joined = lax.map(one_block, (query_blocks, starts))
    return joined.reshape(length, head_width)


def per_device(
    patches,
    vis_gain,
    vis_qkv,
    vis_out,
    merge_gain,
    merge_w,
    image_blocks,
    dest_group,
    slot_rows,
    prompt_len,
    text_emb,
    txt_gain,
    txt_qkv,
    txt_out,
):
    seq_count = lax.axis_size("seq")
    groups = lax.axis_size("grp")
    token_count = patches.shape[0]
    model_width = patches.shape[1]
    group_patches = token_count * seq_count
    vis_normed = layer_norm(patches, vis_gain).astype(jnp.bfloat16)
    vis_proj = projector(vis_qkv, lax.all_gather(vis_normed, "seq", axis=0, tiled=True))
    bounds = jnp.cumsum(image_blocks[0])[:-1]

    def segment(indices):
        return jnp.sum(((indices // 4)[:, None] >= bounds[None, :]).astype(jnp.int32), axis=1)

    key_segments = segment(jnp.arange(group_patches, dtype=jnp.int32))

    def vis_allowed(row_indices):
        return segment(row_indices)[:, None] == key_segments[None, :]

    vis_heads = attend_local(vis_proj[0], vis_proj[1], vis_proj[2], vis_allowed)
    picked = vis_heads
    vis_attn = lax.psum_scatter(
        jnp.dot(picked, vis_out, preferred_element_type=jnp.float32),
        "seq",
        scatter_dimension=0,
        tiled=True,
    )
    residual_sum = patches.astype(jnp.float32) + vis_attn
    merged_in = (
        layer_norm(residual_sum, merge_gain)
        .astype(jnp.bfloat16)
        .reshape(token_count // 4, 4 * model_width)
    )
    feature_slices = lax.all_to_all(merged_in, "seq", split_axis=1, concat_axis=0, tiled=True)
    picked = feature_slices
    visual = lax.psum_scatter(
        jnp.dot(picked, merge_w, preferred_element_type=jnp.float32),
        "seq",
        scatter_dimension=0,
        tiled=True,
    ).astype(jnp.bfloat16)
    dest_rows = dest_group[:, 0]
    merged_rows = dest_rows.shape[0]
    capacity = max(2, 2 * merged_rows // groups)
    onehot = (dest_rows[:, None] == jnp.arange(groups, dtype=jnp.int32)[None, :]).astype(jnp.int32)
    slot_rank = jnp.sum((jnp.cumsum(onehot, axis=0) - 1) * onehot, axis=1)
    selector = (
        (dest_rows[None, None, :] == jnp.arange(groups, dtype=jnp.int32)[:, None, None])
        & (slot_rank[None, None, :] == jnp.arange(capacity, dtype=jnp.int32)[None, :, None])
    ).astype(jnp.bfloat16)
    outgoing = jnp.einsum(
        "gct,td->gcd", selector, visual, preferred_element_type=jnp.float32
    ).astype(jnp.bfloat16)
    arrived_flags = jnp.sum(selector.astype(jnp.float32), axis=2).astype(jnp.bfloat16)
    incoming, arrived = (
        lax.all_to_all(outgoing, "grp", split_axis=0, concat_axis=0, tiled=True),
        lax.all_to_all(arrived_flags, "grp", split_axis=0, concat_axis=0, tiled=True),
    )
    prompt_rows = text_emb.shape[0]
    slot_targets = slot_rows[0, 0, : groups * capacity]
    placement_map = (
        slot_targets[None, :] == jnp.arange(prompt_rows, dtype=jnp.int32)[:, None]
    ).astype(jnp.bfloat16)
    placement_map = placement_map * arrived.reshape(1, groups * capacity)
    replaced = jnp.sum(placement_map.astype(jnp.float32), axis=1, keepdims=True)
    placed = jnp.dot(
        placement_map,
        incoming.reshape(groups * capacity, model_width),
        preferred_element_type=jnp.float32,
    )
    hidden = (text_emb.astype(jnp.float32) * (1.0 - replaced) + placed).astype(jnp.bfloat16)
    txt_normed = rms_norm(hidden, txt_gain).astype(jnp.bfloat16)
    txt_proj = projector(txt_qkv, lax.all_gather(txt_normed, "seq", axis=0, tiled=True))
    length = prompt_len[0]
    key_positions = jnp.arange(prompt_rows * seq_count, dtype=jnp.int32)

    def txt_allowed(row_indices):
        return (key_positions[None, :] <= row_indices[:, None]) & (key_positions[None, :] < length)

    txt_heads = attend_local(txt_proj[0], txt_proj[1], txt_proj[2], txt_allowed)
    picked = txt_heads
    txt_attn = lax.psum_scatter(
        jnp.dot(picked, txt_out, preferred_element_type=jnp.float32),
        "seq",
        scatter_dimension=0,
        tiled=True,
    )
    return hidden.astype(jnp.float32) + txt_attn


def solution(mesh):
    in_specs = (
        P(("grp", "seq"), None),
        P(),
        P(None, None, "seq"),
        P("seq", None),
        P(),
        P("seq", None),
        P("grp", None),
        P(("grp", "seq"), None),
        P("grp", "seq", None),
        P("grp"),
        P(("grp", "seq"), None),
        P(),
        P(None, None, "seq"),
        P("seq", None),
    )
    out_specs = P(("grp", "seq"), None)
    return jax.shard_map(
        per_device, mesh=mesh, in_specs=in_specs, out_specs=out_specs, check_vma=False
    )
```

profile of v0, /device:TPU:0, one launch (start us, length us, event | category | flops | bytes accessed | tf_op | source)
XLA Modules:
  0.0 519.2 jit_solution(14875809928823326263)
XLA Ops:
  6.5 1.3 convert_reduce_fusion.1
  7.8 1.3 fusion.30
  9.1 2.1 fusion.32
  11.2 0.8 reduce-window.4
  12.2 65.2 %all-gather.3.cloned.1.call-done = bf16[2048,1664]{1,0:T(8,128)(2,1)} async-done(((bf16[128,1664]{1,0:T(8,128)(2,1)}), bf16[2048,1664]{1,0:T(8,128)(2,1)}) %all-gather.3.cloned.1.call-update) | async-done | bytes 6815760 | tf_op jit(solution)/shard_map/all_gather | solution.py:83
  77.4 5.7 %fusion.53 = f32[2048,312]{0,1:S(1)} fusion(bf16[2048,1664]{1,0:T(8,128)(2,1)} %all-gather.3.cloned.1.call-done, bf16[1664,312]{0,1:T(8,128)(2,1)} %bitcast.142), kind=kOutput, calls=%fused_computation.103 | convolution fusion | flops 2126512128 | bytes 10409984
  83.8 16.5 %while.24 = (s32[]{:T(128)}, bf16[4,512,1,104]{1,3,2,0:T(8,128)(2,1)S(1)}, s32[4]{0:T(128)S(1)}, s32[3]{0:T(128)S(1)}, s32[2048]{0:T(1024)S(1)}, /*index=5*/bf16...) while((s32[]{:T(128)}, ...), condition=%wide.region_12.13_spmd, body=%wide.region_8.12_spmd.sunk | while | flops 445709312 | bytes 13674633 | solution.py:57
  84.4 0.7 add_select_fusion.3
  85.1 1.0 fusion.77
  86.1 0.7 fusion.78
  86.8 1.1 fusion.79
  88.5 0.7 add_select_fusion.3
  89.2 1.0 fusion.77
  90.2 0.7 fusion.78
  90.9 1.1 fusion.79
  92.6 0.7 add_select_fusion.3
  93.4 1.0 fusion.77
  94.3 0.7 fusion.78
  95.0 1.1 fusion.79
  96.7 0.7 add_select_fusion.3
  97.5 1.0 fusion.77
  98.5 0.7 fusion.78
  99.2 1.1 fusion.79
  100.6 6.9 %fusion.54 = f32[2048,1664]{1,0:T(8,128)} fusion(bf16[2048,104]{0,1:T(8,128)(2,1)S(1)} %bitcast.134, bf16[104,1664]{1,0:T(8,128)(2,1)S(1)} %copy-done.4), kind=kOutput, calls=%fused_computation.104 | convolution fusion | flops 708837376 | bytes 14403584 | tf_op jit(solution)/shard_map/dot_general | solution.py:97
  107.6 97.6 %reduce-scatter.4.cloned.1.call-done = f32[128,1664]{1,0:T(8,128)} async-done(((f32[2048,1664]{1,0:T(8,128)}), f32[128,1664]{1,0:T(8,128)}) %reduce-scatter.4.cloned.1.call-update) | async-done | bytes 851984 | tf_op jit(solution)/shard_map/reduce_scatter | solution.py:96
  205.1 1.3 fusion.33
  206.5 1.4 multiply_reduce_fusion.1
  207.9 1.4 multiply_convert_fusion.1
  210.2 15.3 %all_to_all.33 = bf16[32,16,416]{2,0,1:T(8,128)(2,1)S(1)} all-to-all(bf16[32,16,416]{2,0,1:T(8,128)(2,1)S(1)} %copy.41), channel_id=1, replica_groups=mesh['seq'=16,'grp'=8] {'seq'}, dimensions={1} | all-to-all | bytes 851968 | tf_op jit(solution)/shard_map/all_to_all | solution.py:108
  225.6 2.8 fusion.55
  228.8 0.6 copy.38
  229.5 4.4 all-to-all-start
  233.9 5.2 %all-to-all-done = bf16[8,1,8]{2,1,0:T(2,128)(2,1)S(1)} async-done(((bf16[8,1,8]{2,1,0:T(2,128)(2,1)}), bf16[8,1,8]{2,1,0:T(2,128)(2,1)S(1)}, u32[]{:S(2)}, u32[]{:S(2)}) %all-to-all-start) | async-done | bytes 160 | tf_op jit(solution)/shard_map/all_to_all | solution.py:131
  239.3 63.7 %reduce-scatter.6.cloned.1.call-done = f32[32,1664]{1,0:T(8,128)} async-done(((f32[512,1664]{1,0:T(8,128)}), f32[32,1664]{1,0:T(8,128)}) %reduce-scatter.6.cloned.1.call-update) | async-done | bytes 213008 | tf_op jit(solution)/shard_map/reduce_scatter | solution.py:110
  303.0 1.8 convolution_convert_fusion
  304.8 4.4 all-to-all-start.2
  309.3 6.9 %all-to-all-done.2 = bf16[8,8,1664]{2,1,0:T(8,128)(2,1)S(1)} async-done(((bf16[8,8,1664]{2,1,0:T(8,128)(2,1)}), bf16[8,8,1664]{2,1,0:T(8,128)(2,1)S(1)}, u32[]{:S(2)}, u32[]{:S(2)}) %all-to-all-start.2) | async-done | bytes 213024 | tf_op jit(solution)/shard_map/all_to_all | solution.py:130
  316.7 0.9 multiply_convert_fusion
  317.8 60.8 %all-gather.5.cloned.1.call-done = bf16[2048,1664]{1,0:T(8,128)(2,1)} async-done(((bf16[128,1664]{1,0:T(8,128)(2,1)}), bf16[2048,1664]{1,0:T(8,128)(2,1)}) %all-gather.5.cloned.1.call-update) | async-done | bytes 6815760 | tf_op jit(solution)/shard_map/all_gather | solution.py:147
  378.7 5.5 %fusion.56 = f32[2048,312]{0,1:S(1)} fusion(bf16[2048,1664]{1,0:T(8,128)(2,1)} %all-gather.5.cloned.1.call-done, bf16[1664,312]{0,1:T(8,128)(2,1)S(1)} %bitcast.143), kind=kOutput, calls=%fused_computation.106 | convolution fusion | flops 2126512128 | bytes 10409984
  384.9 20.8 %while.25 = (s32[]{:T(128)}, bf16[4,512,1,104]{1,3,2,0:T(8,128)(2,1)S(1)}, s32[4]{0:T(128)S(1)}, s32[]{:T(128)}, bf16[4,512,1,104]{1,3,2,0:T(8,128)(2,1)S(1)}, /...) while((s32[]{:T(128)}, ...), condition=%wide.region_21.22_spmd.clone.clone, body=%wide.region_18.21_spmd.clone.clone.sunk | while | flops 446748160 | bytes 13666425 | solution.py:57
  385.5 0.6 iota_add_fusion.3
  386.1 0.7 iota_compare_fusion.7
  386.8 1.5 fusion.81
  388.3 0.7 fusion.82
  389.0 1.1 fusion.83
  390.7 0.6 iota_add_fusion.3
  391.3 0.7 iota_compare_fusion.7
  392.0 1.5 fusion.81
  393.5 0.7 fusion.82
  394.2 1.1 fusion.83
  395.9 0.6 iota_add_fusion.3
  396.5 0.7 iota_compare_fusion.7
  397.2 1.5 fusion.81
  398.7 0.7 fusion.82
  399.4 1.1 fusion.83
  401.1 0.6 iota_add_fusion.3
  401.7 0.7 iota_compare_fusion.7
  402.4 1.5 fusion.81
  403.9 0.7 fusion.82
  404.6 1.1 fusion.83
  406.0 6.9 %fusion.57 = f32[2048,1664]{1,0:T(8,128)} fusion(bf16[2048,104]{0,1:T(8,128)(2,1)S(1)} %bitcast.135, bf16[104,1664]{1,0:T(8,128)(2,1)S(1)} %copy-done.5), kind=kOutput, calls=%fused_computation.107 | convolution fusion | flops 708837376 | bytes 14403584 | tf_op jit(solution)/shard_map/dot_general | solution.py:157
  412.9 97.5 %reduce-scatter.8.cloned.1.call-done = f32[128,1664]{1,0:T(8,128)} async-done(((f32[2048,1664]{1,0:T(8,128)}), f32[128,1664]{1,0:T(8,128)}) %reduce-scatter.8.cloned.1.call-update) | async-done | bytes 851984 | tf_op jit(solution)/shard_map/reduce_scatter | solution.py:156
  510.4 2.2 add.90
  (80 shorter events, 9.6 us)
Async XLA Ops:
  6.5 219.0 %copy-start = (bf16[416,1664]{1,0:T(8,128)(2,1)S(1)}, bf16[416,1664]{1,0:T(8,128)(2,1)}, u32[]{:S(2)}) copy-start(bf16[416,1664]{1,0:T(8,128)(2,1)} %param.23) | copy-start | bytes 4153348
  6.5 70.8 %all-gather.3.cloned.1.call-start = ((), (), s32[]{:S(2)}) async-start(), calls=%async_computation.6 | async-start | bytes 7241728 | tf_op jit(solution)/shard_map/all_gather | solution.py:83
  11.2 194.0 %reduce-scatter.4.cloned.1.call-start = ((), (), s32[]{:S(2)}) async-start(), calls=%async_computation.7 | async-start | bytes 14483456 | tf_op jit(solution)/shard_map/reduce_scatter | solution.py:96
  83.8 16.8 %copy-start.4 = (bf16[104,1664]{1,0:T(8,128)(2,1)S(1)}, bf16[104,1664]{1,0:T(8,128)(2,1)}, u32[]{:S(2)}) copy-start(bf16[104,1664]{1,0:T(8,128)(2,1)} %param.21) | copy-start | bytes 1038340
  107.5 97.6 %copy-start.2 = (bf16[128,1664]{1,0:T(8,128)(2,1)S(1)}, bf16[128,1664]{1,0:T(8,128)(2,1)}, u32[]{:S(2)}) copy-start(bf16[128,1664]{1,0:T(8,128)(2,1)} %param.18) | copy-start | bytes 1277956
  107.5 100.4 %copy-start.6 = (f32[1664]{0:T(1024)S(1)}, f32[1664]{0:T(1024)}, u32[]{:S(2)}) copy-start(f32[1664]{0:T(1024)} %param.22) | copy-start | bytes 19972
  107.5 195.4 %reduce-scatter.6.cloned.1.call-start = ((), (), s32[]{:S(2)}) async-start(), calls=%async_computation.8 | async-start | bytes 3620864 | tf_op jit(solution)/shard_map/reduce_scatter | solution.py:110
  225.5 2.9 copy-start.8
  225.5 8.3 %copy-start.10 = (s32[1,1,128]{2,1,0:T(1,128)S(1)}, s32[1,1,128]{2,1,0:T(1,128)}, u32[]{:S(2)}) copy-start(s32[1,1,128]{2,1,0:T(1,128)} %param.26) | copy-start | bytes 1540
  225.5 90.7 %copy-start.3 = (bf16[128,1664]{1,0:T(8,128)(2,1)S(1)}, bf16[128,1664]{1,0:T(8,128)(2,1)}, u32[]{:S(2)}) copy-start(bf16[128,1664]{1,0:T(8,128)(2,1)} %param.28) | copy-start | bytes 1277956
  228.4 88.3 %copy-start.7 = (f32[1664]{0:T(1024)S(1)}, f32[1664]{0:T(1024)}, u32[]{:S(2)}) copy-start(f32[1664]{0:T(1024)} %param.29) | copy-start | bytes 19972
  228.4 150.3 %copy-start.9 = (bf16[3,1664,104]{1,2,0:T(8,128)(2,1)S(1)}, bf16[3,1664,104]{1,2,0:T(8,128)(2,1)}, u32[]{:S(2)}) copy-start(bf16[3,1664,104]{1,2,0:T(8,128)(2,1)} %param.30) | copy-start | bytes 3115012
  229.5 9.6 %all-to-all-start = ((bf16[8,1,8]{2,1,0:T(2,128)(2,1)}), bf16[8,1,8]{2,1,0:T(2,128)(2,1)S(1)}, u32[]{:S(2)}, u32[]{:S(2)}) async-start(bf16[8,1,8]{2,1,0:T(2,128)(2,1)} %copy.38), calls=%async_computation | async-start | bytes 8192 | tf_op jit(solution)/shard_map/all_to_all | solution.py:131
  304.8 11.4 %all-to-all-start.2 = ((bf16[8,8,1664]{2,1,0:T(8,128)(2,1)}), bf16[8,8,1664]{2,1,0:T(8,128)(2,1)S(1)}, u32[]{:S(2)}, u32[]{:S(2)}) async-start(bf16[8,8,1664]{2,1,0:T(8,128)(2,1)} %convolution_convert_fusion), calls=%async_computation.4 | async-start | bytes 425984 | tf_op jit(solution)/shard_map/all_to_all | solution.py:130
  309.2 69.4 %all-gather.5.cloned.1.call-start = ((), (), s32[]{:S(2)}) async-start(), calls=%async_computation.9 | async-start | bytes 7241728 | tf_op jit(solution)/shard_map/all_gather | solution.py:147
  317.6 192.8 %reduce-scatter.8.cloned.1.call-start = ((), (), s32[]{:S(2)}) async-start(), calls=%async_computation.10 | async-start | bytes 14483456 | tf_op jit(solution)/shard_map/reduce_scatter | solution.py:156
  384.9 21.1 %copy-start.5 = (bf16[104,1664]{1,0:T(8,128)(2,1)S(1)}, bf16[104,1664]{1,0:T(8,128)(2,1)}, u32[]{:S(2)}) copy-start(bf16[104,1664]{1,0:T(8,128)(2,1)} %param.31) | copy-start | bytes 1038340
  412.9 99.7 %copy-start.1 = (bf16[416,1664]{1,0:T(8,128)(2,1)S(1)}, bf16[416,1664]{1,0:T(8,128)(2,1)}, u32[]{:S(2)}) copy-start(bf16[416,1664]{1,0:T(8,128)(2,1)} %param.23) | copy-start | bytes 4153348
Sparse Core Ops, SparseCore 0:
  11.3 66.0 all-gather.2
  107.7 97.4 reduce-scatter.3
  228.5 74.3 reduce-scatter.5
  317.7 60.8 all-gather.4
  413.0 97.3 reduce-scatter.7
where the time goes:
time: 520 us; the launch traced here: 519 us
  waiting for transfers between devices  397 us (76%)
  matrix products  48.6 us (9%)
  other arithmetic  27.5 us (5%)
  blocking collectives  15.3 us (3%)
  between operations  13.4 us (3%)
  starting transfers between devices  9.2 us (2%)
  local copies, waits for them, and re-layouts  7.97 us (2%)
    reduce_scatter x1, waiting for transfers between devices, per_device(): lax.psum_scatter(jnp.dot(picked, vis_out, preferred_element_type=jnp.floa...  97.6 us
    reduce_scatter x1, waiting for transfers between devices, per_device(): lax.psum_scatter(jnp.dot(picked, txt_out, preferred_element_type=jnp.floa...  97.5 us
    all_gather x1, waiting for transfers between devices, per_device(): lax.all_gather(vis_normed, 'seq', axis=0, tiled=True)  65.2 us
    reduce_scatter x1, waiting for transfers between devices, per_device(): lax.psum_scatter(jnp.dot(picked, merge_w, preferred_element_type=jnp.floa...  63.7 us
    all_gather x1, waiting for transfers between devices, per_device(): lax.all_gather(txt_normed, 'seq', axis=0, tiled=True)  60.8 us
    all_to_all x1, blocking collectives, per_device(): lax.all_to_all(merged_in, 'seq', split_axis=1, concat_axis=0, tiled=True)  15.3 us
    unnamed x2, matrix products  11.1 us
  transfers between devices with their start and end apart: 7, of which 7 were waited for; matrix products, arithmetic and copies ran while one was open for 0% of the time, Pallas kernels for 0%

commit v1 on v0

--- a/solution.py
+++ b/solution.py
@@ -58,6 +58,14 @@
     return joined.reshape(length, head_width)
 
 
+def heads_to_rows(heads, seq_count):
+    length, width = heads.shape
+    rows = length // seq_count
+    blocks = heads.reshape(seq_count, rows, width)
+    swapped = lax.all_to_all(blocks, "seq", split_axis=0, concat_axis=0, tiled=True)
+    return swapped.transpose(1, 0, 2).reshape(rows, seq_count * width)
+
+
 def per_device(
     patches,
     vis_gain,
@@ -79,6 +87,8 @@
     token_count = patches.shape[0]
     model_width = patches.shape[1]
     group_patches = token_count * seq_count
+    vis_out_full = lax.all_gather(vis_out, "seq", axis=0, tiled=True)
+    txt_out_full = lax.all_gather(txt_out, "seq", axis=0, tiled=True)
     vis_normed = layer_norm(patches, vis_gain).astype(jnp.bfloat16)
     vis_proj = projector(vis_qkv, lax.all_gather(vis_normed, "seq", axis=0, tiled=True))
     bounds = jnp.cumsum(image_blocks[0])[:-1]
@@ -92,12 +102,8 @@
         return segment(row_indices)[:, None] == key_segments[None, :]
 
     vis_heads = attend_local(vis_proj[0], vis_proj[1], vis_proj[2], vis_allowed)
-    picked = vis_heads
-    vis_attn = lax.psum_scatter(
-        jnp.dot(picked, vis_out, preferred_element_type=jnp.float32),
-        "seq",
-        scatter_dimension=0,
-        tiled=True,
+    vis_attn = jnp.dot(
+        heads_to_rows(vis_heads, seq_count), vis_out_full, preferred_element_type=jnp.float32
     )
     residual_sum = patches.astype(jnp.float32) + vis_attn
     merged_in = (
@@ -152,12 +158,8 @@
         return (key_positions[None, :] <= row_indices[:, None]) & (key_positions[None, :] < length)
 
     txt_heads = attend_local(txt_proj[0], txt_proj[1], txt_proj[2], txt_allowed)
-    picked = txt_heads
-    txt_attn = lax.psum_scatter(
-        jnp.dot(picked, txt_out, preferred_element_type=jnp.float32),
-        "seq",
-        scatter_dimension=0,
-        tiled=True,
+    txt_attn = jnp.dot(
+        heads_to_rows(txt_heads, seq_count), txt_out_full, preferred_element_type=jnp.float32
     )
     return hidden.astype(jnp.float32) + txt_attn
 

time: 520 us -> 389 us (0.75)
  waiting for transfers between devices: 397 us -> 258 us
  starting transfers between devices: 9.2 us -> 19.6 us
  other arithmetic: 27.5 us -> 21.8 us
    reduce_scatter x2 -> x0, waiting for transfers between devices: 195 us -> none  [the longest x1 97.6 us: per_device(): lax.psum_scatter(jnp.dot(picked, vis_out, preferred_element_type=jnp.floa...]
    all_gather x0 -> x2, waiting for transfers between devices: none -> 55.6 us  [the longest x1 31.8 us: per_device(): vis_out_full = lax.all_gather(vis_out, 'seq', axis=0, tiled=True)]
    all_to_all x0 -> x2, starting transfers between devices: none -> 10.5 us  [heads_to_rows(): lax.all_to_all(blocks, 'seq', split_axis=0, concat_axis=0, tiled=True)]
    dot_general x2, matrix products: 13.8 us -> 8.2 us  [the longest x1 4.51 us: per_device(): jnp.dot(heads_to_rows(txt_heads, seq_count), txt_out_full, preferred_elem...]
  transfers between devices with their start and end apart: 7 -> 9, of which waited for: 7 -> 7; matrix products, arithmetic and copies ran while one was open for 0% -> 16% of each run, Pallas kernels for 0% -> 0%
where the time goes in v1:
time: 389 us; the launch traced here: 388 us
  waiting for transfers between devices  258 us (66%)
  matrix products  47.6 us (12%)
  other arithmetic  21.8 us (6%)
  starting transfers between devices  19.6 us (5%)
  blocking collectives  15.7 us (4%)
  between operations  13.4 us (3%)
  local copies, waits for them, and re-layouts  11.7 us (3%)
    all_gather x1, waiting for transfers between devices, per_device(): lax.all_gather(vis_normed, 'seq', axis=0, tiled=True)  64.5 us
    reduce_scatter x1, waiting for transfers between devices, per_device(): lax.psum_scatter(jnp.dot(picked, merge_w, preferred_element_type=jnp.floa...  63.9 us
    all_gather x1, waiting for transfers between devices, per_device(): lax.all_gather(txt_normed, 'seq', axis=0, tiled=True)  60.5 us
    all_gather x1, waiting for transfers between devices, per_device(): vis_out_full = lax.all_gather(vis_out, 'seq', axis=0, tiled=True)  31.8 us
    all_gather x1, waiting for transfers between devices, per_device(): txt_out_full = lax.all_gather(txt_out, 'seq', axis=0, tiled=True)  23.8 us
    all_to_all x1, blocking collectives, per_device(): lax.all_to_all(merged_in, 'seq', split_axis=1, concat_axis=0, tiled=True)  15.7 us
    dot_general x8, matrix products, one_block(): jnp.einsum('qhe,khe->hqk', query_part, key_heads, preferred_element_type=...  14.2 us
    unnamed x2, matrix products  11.3 us
  transfers between devices with their start and end apart: 9, of which 7 were waited for; matrix products, arithmetic and copies ran while one was open for 16% of the time, Pallas kernels for 0%

profile of v1, /device:TPU:0, one launch (start us, length us, event | category | flops | bytes accessed | tf_op | source)
XLA Modules:
  0.0 387.7 jit_solution(5486208225228897463)
XLA Ops:
  6.5 1.3 convert_reduce_fusion.1
  7.8 1.3 fusion.30
  9.1 2.1 fusion.32
  11.2 0.7 all-gather.7.cloned.1.call-update
  11.9 0.8 reduce-window.4
  12.9 64.5 %all-gather.5.cloned.1.call-done = bf16[2048,1664]{1,0:T(8,128)(2,1)} async-done(((bf16[128,1664]{1,0:T(8,128)(2,1)}), bf16[2048,1664]{1,0:T(8,128)(2,1)}) %all-gather.5.cloned.1.call-update) | async-done | bytes 6815760 | tf_op jit(solution)/shard_map/all_gather | solution.py:93
  77.4 5.7 %fusion.53 = f32[2048,312]{0,1:S(1)} fusion(bf16[2048,1664]{1,0:T(8,128)(2,1)} %all-gather.5.cloned.1.call-done, bf16[1664,312]{0,1:T(8,128)(2,1)} %bitcast.140), kind=kOutput, calls=%fused_computation.104 | convolution fusion | flops 2126512128 | bytes 10409984
  83.8 16.5 %while.24 = (s32[]{:T(128)}, bf16[4,512,1,104]{1,3,2,0:T(8,128)(2,1)S(1)}, s32[4]{0:T(128)S(1)}, s32[3]{0:T(128)S(1)}, s32[2048]{0:T(1024)S(1)}, /*index=5*/bf16...) while((s32[]{:T(128)}, ...), condition=%wide.region_12.13_spmd, body=%wide.region_8.12_spmd.sunk | while | flops 445709312 | bytes 13674625 | solution.py:57
  85.1 1.0 fusion.75
  86.1 0.7 fusion.76
  86.8 1.1 fusion.77
  88.5 0.7 add_select_fusion.3
  89.2 1.0 fusion.75
  90.2 0.7 fusion.76
  90.9 1.1 fusion.77
  93.4 1.0 fusion.75
  94.4 0.7 fusion.76
  95.1 1.1 fusion.77
  97.5 1.0 fusion.75
  98.5 0.7 fusion.76
  99.2 1.1 fusion.77
  100.7 0.9 copy.47
  101.6 5.2 %all-to-all-start.1 = ((bf16[16,128,104]{1,2,0:T(8,128)(2,1)}), bf16[16,128,104]{1,2,0:T(8,128)(2,1)S(1)}, u32[]{:S(2)}, u32[]{:S(2)}) async-start(bf16[16,128,104]{1,2,0:T(8,128)(2,1)} %copy.47), calls=%async_computation.1 | async-start | bytes 851968 | tf_op jit(solution)/shard_map/all_to_all | solution.py:65
  106.9 31.8 %all-gather.7.cloned.1.call-done = bf16[1664,1664]{1,0:T(8,128)(2,1)} async-done(((bf16[104,1664]{1,0:T(8,128)(2,1)}), bf16[1664,1664]{1,0:T(8,128)(2,1)}) %all-gather.7.cloned.1.call-update) | async-done | bytes 5537808 | tf_op jit(solution)/shard_map/all_gather | solution.py:90
  138.7 3.7 fusion.52
  143.8 15.7 %all_to_all.43 = bf16[32,16,416]{2,0,1:T(8,128)(2,1)S(1)} all-to-all(bf16[32,16,416]{2,0,1:T(8,128)(2,1)S(1)} %copy.48), channel_id=1, replica_groups=mesh['seq'=16,'grp'=8] {'seq'}, dimensions={1} | all-to-all | bytes 851968 | tf_op jit(solution)/shard_map/all_to_all | solution.py:114
  159.5 2.8 fusion.54
  163.4 4.4 %all-to-all-start = ((bf16[8,1,8]{2,1,0:T(2,128)(2,1)}), bf16[8,1,8]{2,1,0:T(2,128)(2,1)S(1)}, u32[]{:S(2)}, u32[]{:S(2)}) async-start(bf16[8,1,8]{2,1,0:T(2,128)(2,1)} %copy.44), calls=%async_computation | async-start | bytes 8192 | tf_op jit(solution)/shard_map/all_to_all | solution.py:137
  167.9 5.2 %all-to-all-done = bf16[8,1,8]{2,1,0:T(2,128)(2,1)S(1)} async-done(((bf16[8,1,8]{2,1,0:T(2,128)(2,1)}), bf16[8,1,8]{2,1,0:T(2,128)(2,1)S(1)}, u32[]{:S(2)}, u32[]{:S(2)}) %all-to-all-start) | async-done | bytes 160 | tf_op jit(solution)/shard_map/all_to_all | solution.py:137
  173.3 63.9 %reduce-scatter.2.cloned.1.call-done = f32[32,1664]{1,0:T(8,128)} async-done(((f32[512,1664]{1,0:T(8,128)}), f32[32,1664]{1,0:T(8,128)}) %reduce-scatter.2.cloned.1.call-update) | async-done | bytes 213008 | tf_op jit(solution)/shard_map/reduce_scatter | solution.py:116
  237.2 1.8 convolution_convert_fusion
  239.0 4.4 %all-to-all-start.3 = ((bf16[8,8,1664]{2,1,0:T(8,128)(2,1)}), bf16[8,8,1664]{2,1,0:T(8,128)(2,1)S(1)}, u32[]{:S(2)}, u32[]{:S(2)}) async-start(bf16[8,8,1664]{2,1,0:T(8,128)(2,1)} %convolution_convert_fusion), calls=%async_computation.4 | async-start | bytes 425984 | tf_op jit(solution)/shard_map/all_to_all | solution.py:136
  243.4 6.9 %all-to-all-done.3 = bf16[8,8,1664]{2,1,0:T(8,128)(2,1)S(1)} async-done(((bf16[8,8,1664]{2,1,0:T(8,128)(2,1)}), bf16[8,8,1664]{2,1,0:T(8,128)(2,1)S(1)}, u32[]{:S(2)}, u32[]{:S(2)}) %all-to-all-start.3) | async-done | bytes 213024 | tf_op jit(solution)/shard_map/all_to_all | solution.py:136
  250.9 0.9 multiply_convert_fusion
  252.4 60.5 %all-gather.9.cloned.1.call-done = bf16[2048,1664]{1,0:T(8,128)(2,1)} async-done(((bf16[128,1664]{1,0:T(8,128)(2,1)}), bf16[2048,1664]{1,0:T(8,128)(2,1)}) %all-gather.9.cloned.1.call-update) | async-done | bytes 6815760 | tf_op jit(solution)/shard_map/all_gather | solution.py:153
  312.8 5.7 %fusion.55 = f32[2048,312]{0,1:S(1)} fusion(bf16[2048,1664]{1,0:T(8,128)(2,1)} %all-gather.9.cloned.1.call-done, bf16[1664,312]{0,1:T(8,128)(2,1)} %bitcast.141), kind=kOutput, calls=%fused_computation.106 | convolution fusion | flops 2126512128 | bytes 10409984
  318.7 0.8 slice_bitcast_fusion
  319.9 0.8 copy.49
  320.7 25.7 %while.25 = (s32[]{:T(128)}, bf16[4,512,1,104]{1,3,2,0:T(8,128)(2,1)S(1)}, s32[4]{0:T(128)S(1)}, s32[]{:T(128)}, bf16[4,512,1,104]{1,3,2,0:T(8,128)(2,1)}, /*ind...) while((s32[]{:T(128)}, ...), condition=%wide.region_20.21_spmd.clone.clone, body=%wide.region_17.20_spmd.clone.clone.sunk | while | flops 446748160 | bytes 13666925 | solution.py:57
  320.7 0.7 dynamic_slice.43
  321.4 0.7 iota_add_fusion.3
  322.8 2.6 fusion.79
  325.3 0.7 fusion.80
  326.0 1.1 fusion.81
  327.2 0.7 dynamic_slice.43
  327.8 0.7 iota_add_fusion.3
  329.2 2.6 fusion.79
  331.7 0.7 fusion.80
  332.5 1.1 fusion.81
  333.6 0.7 dynamic_slice.43
  334.2 0.7 iota_add_fusion.3
  334.9 0.7 iota_compare_fusion.7
  335.6 2.6 fusion.79
  338.2 0.7 fusion.80
  338.9 1.1 fusion.81
  340.0 0.7 dynamic_slice.43
  340.7 0.7 iota_add_fusion.3
  342.0 2.6 fusion.79
  344.6 0.7 fusion.80
  345.3 1.1 fusion.81
  346.8 0.9 copy.51
  347.7 5.2 %all-to-all-start.4 = ((bf16[16,128,104]{1,2,0:T(8,128)(2,1)}), bf16[16,128,104]{1,2,0:T(8,128)(2,1)S(1)}, u32[]{:S(2)}, u32[]{:S(2)}) async-start(bf16[16,128,104]{1,2,0:T(8,128)(2,1)} %copy.51), calls=%async_computation.5 | async-start | bytes 851968 | tf_op jit(solution)/shard_map/all_to_all | solution.py:65
  352.9 23.8 %all-gather.11.cloned.1.call-done = bf16[1664,1664]{1,0:T(8,128)(2,1)} async-done(((bf16[104,1664]{1,0:T(8,128)(2,1)}), bf16[1664,1664]{1,0:T(8,128)(2,1)}) %all-gather.11.cloned.1.call-update) | async-done | bytes 5537808 | tf_op jit(solution)/shard_map/all_gather | solution.py:91
  376.7 4.5 %convolution_add_fusion = f32[128,1664]{1,0:T(8,128)} fusion(f32[128,1664]{1,0:T(8,128)S(1)} %get-tuple-element.308, bf16[128,1664]{0,1:T(8,128)(2,1)S(1)} %bitcast.135, bf16[1664,1664]{1,0:T(8,128)(2,1)} %all-gather.11.cloned.1.call-done), kind=kOutput, calls=%fused_computation.41 | convolution fusion | flops 709050368 | bytes 7667712 | tf_op jit(solution)/shard_map/dot_general | solution.py:161
  (76 shorter events, 12.5 us)
Async XLA Ops:
  6.5 153.0 %copy-start = (bf16[416,1664]{1,0:T(8,128)(2,1)S(1)}, bf16[416,1664]{1,0:T(8,128)(2,1)}, u32[]{:S(2)}) copy-start(bf16[416,1664]{1,0:T(8,128)(2,1)} %param.23) | copy-start | bytes 4153348
  6.5 70.8 %all-gather.5.cloned.1.call-start = ((), (), s32[]{:S(2)}) async-start(), calls=%async_computation.6 | async-start | bytes 7241728 | tf_op jit(solution)/shard_map/all_gather | solution.py:93
  11.2 127.5 %all-gather.7.cloned.1.call-start = ((), (), s32[]{:S(2)}) async-start(), calls=%async_computation.7 | async-start | bytes 5883904 | tf_op jit(solution)/shard_map/all_gather | solution.py:90
  83.8 55.0 %copy-start.1 = (bf16[128,1664]{1,0:T(8,128)(2,1)S(1)}, bf16[128,1664]{1,0:T(8,128)(2,1)}, u32[]{:S(2)}) copy-start(bf16[128,1664]{1,0:T(8,128)(2,1)} %param.18) | copy-start | bytes 1277956
  101.6 37.2 %all-to-all-start.1 = ((bf16[16,128,104]{1,2,0:T(8,128)(2,1)}), bf16[16,128,104]{1,2,0:T(8,128)(2,1)S(1)}, u32[]{:S(2)}, u32[]{:S(2)}) async-start(bf16[16,128,104]{1,2,0:T(8,128)(2,1)} %copy.47), calls=%async_computation.1 | async-start | bytes 851968 | tf_op jit(solution)/shard_map/all_to_all | solution.py:65
  106.8 35.9 %copy-start.3 = (f32[1664]{0:T(1024)S(1)}, f32[1664]{0:T(1024)}, u32[]{:S(2)}) copy-start(f32[1664]{0:T(1024)} %param.22) | copy-start | bytes 19972
  106.8 130.3 %reduce-scatter.2.cloned.1.call-start = ((), (), s32[]{:S(2)}) async-start(), calls=%async_computation.8 | async-start | bytes 3620864 | tf_op jit(solution)/shard_map/reduce_scatter | solution.py:116
  159.5 2.9 copy-start.5
  159.5 8.3 %copy-start.6 = (s32[1,1,128]{2,1,0:T(1,128)S(1)}, s32[1,1,128]{2,1,0:T(1,128)}, u32[]{:S(2)}) copy-start(s32[1,1,128]{2,1,0:T(1,128)} %param.26) | copy-start | bytes 1540
  159.5 90.8 %copy-start.2 = (bf16[128,1664]{1,0:T(8,128)(2,1)S(1)}, bf16[128,1664]{1,0:T(8,128)(2,1)}, u32[]{:S(2)}) copy-start(bf16[128,1664]{1,0:T(8,128)(2,1)} %param.28) | copy-start | bytes 1277956
  162.4 88.5 %copy-start.4 = (f32[1664]{0:T(1024)S(1)}, f32[1664]{0:T(1024)}, u32[]{:S(2)}) copy-start(f32[1664]{0:T(1024)} %param.29) | copy-start | bytes 19972
  163.4 9.6 %all-to-all-start = ((bf16[8,1,8]{2,1,0:T(2,128)(2,1)}), bf16[8,1,8]{2,1,0:T(2,128)(2,1)S(1)}, u32[]{:S(2)}, u32[]{:S(2)}) async-start(bf16[8,1,8]{2,1,0:T(2,128)(2,1)} %copy.44), calls=%async_computation | async-start | bytes 8192 | tf_op jit(solution)/shard_map/all_to_all | solution.py:137
  239.0 11.4 %all-to-all-start.3 = ((bf16[8,8,1664]{2,1,0:T(8,128)(2,1)}), bf16[8,8,1664]{2,1,0:T(8,128)(2,1)S(1)}, u32[]{:S(2)}, u32[]{:S(2)}) async-start(bf16[8,8,1664]{2,1,0:T(8,128)(2,1)} %convolution_convert_fusion), calls=%async_computation.4 | async-start | bytes 425984 | tf_op jit(solution)/shard_map/all_to_all | solution.py:136
  243.4 69.5 %all-gather.9.cloned.1.call-start = ((), (), s32[]{:S(2)}) async-start(), calls=%async_computation.9 | async-start | bytes 7241728 | tf_op jit(solution)/shard_map/all_gather | solution.py:153
  251.8 124.9 %all-gather.11.cloned.1.call-start = ((), (), s32[]{:S(2)}) async-start(), calls=%async_computation.10 | async-start | bytes 5883904 | tf_op jit(solution)/shard_map/all_gather | solution.py:91
  347.7 29.0 %all-to-all-start.4 = ((bf16[16,128,104]{1,2,0:T(8,128)(2,1)}), bf16[16,128,104]{1,2,0:T(8,128)(2,1)S(1)}, u32[]{:S(2)}, u32[]{:S(2)}) async-start(bf16[16,128,104]{1,2,0:T(8,128)(2,1)} %copy.51), calls=%async_computation.5 | async-start | bytes 851968 | tf_op jit(solution)/shard_map/all_to_all | solution.py:65
Sparse Core Ops, SparseCore 0:
  11.3 66.0 all-gather.4
  79.5 59.1 all-gather.6
  162.5 74.5 reduce-scatter.1
  251.9 60.8 all-gather.8
  314.8 61.7 all-gather.10

commit v2 on v1

--- a/solution.py
+++ b/solution.py
@@ -64,6 +64,25 @@
     blocks = heads.reshape(seq_count, rows, width)
     swapped = lax.all_to_all(blocks, "seq", split_axis=0, concat_axis=0, tiled=True)
     return swapped.transpose(1, 0, 2).reshape(rows, seq_count * width)
+
+
+def gather_shared(w_local):
+    half = w_local.shape[1] // 2
+    groups = lax.axis_size("grp")
+    core = lax.axis_index("grp") % 2
+    mine = lax.dynamic_slice_in_dim(w_local, core * half, half, axis=1)
+    mine_full = lax.all_gather(mine, "seq", axis=0, tiled=True)
+    other_full = lax.ppermute(mine_full, "grp", [(g, g ^ 1) for g in range(groups)])
+    return mine_full, other_full, core
+
+
+def project_shared(rows, shared):
+    mine_full, other_full, core = shared
+    out_mine = jnp.dot(rows, mine_full, preferred_element_type=jnp.float32)
+    out_other = jnp.dot(rows, other_full, preferred_element_type=jnp.float32)
+    first = jnp.where(core == 0, out_mine, out_other)
+    second = jnp.where(core == 0, out_other, out_mine)
+    return jnp.concatenate([first, second], axis=1)
 
 
 def per_device(
@@ -87,10 +106,11 @@
     token_count = patches.shape[0]
     model_width = patches.shape[1]
     group_patches = token_count * seq_count
-    vis_out_full = lax.all_gather(vis_out, "seq", axis=0, tiled=True)
-    txt_out_full = lax.all_gather(txt_out, "seq", axis=0, tiled=True)
     vis_normed = layer_norm(patches, vis_gain).astype(jnp.bfloat16)
-    vis_proj = projector(vis_qkv, lax.all_gather(vis_normed, "seq", axis=0, tiled=True))
+    vis_gathered = lax.all_gather(vis_normed, "seq", axis=0, tiled=True)
+    vis_gathered, vis_out, txt_out = lax.optimization_barrier((vis_gathered, vis_out, txt_out))
+    vis_out_full = gather_shared(vis_out)
+    vis_proj = projector(vis_qkv, vis_gathered)
     bounds = jnp.cumsum(image_blocks[0])[:-1]
 
     def segment(indices):
@@ -102,9 +122,9 @@
         return segment(row_indices)[:, None] == key_segments[None, :]
 
     vis_heads = attend_local(vis_proj[0], vis_proj[1], vis_proj[2], vis_allowed)
-    vis_attn = jnp.dot(
-        heads_to_rows(vis_heads, seq_count), vis_out_full, preferred_element_type=jnp.float32
-    )
+    vis_heads, txt_out = lax.optimization_barrier((vis_heads, txt_out))
+    txt_out_full = gather_shared(txt_out)
+    vis_attn = project_shared(heads_to_rows(vis_heads, seq_count), vis_out_full)
     residual_sum = patches.astype(jnp.float32) + vis_attn
     merged_in = (
         layer_norm(residual_sum, merge_gain)
@@ -112,9 +132,10 @@
         .reshape(token_count // 4, 4 * model_width)
     )
     feature_slices = lax.all_to_all(merged_in, "seq", split_axis=1, concat_axis=0, tiled=True)
-    picked = feature_slices
+    merge_partial = jnp.dot(feature_slices, merge_w, preferred_element_type=jnp.float32)
+    merge_partial = lax.optimization_barrier((merge_partial, txt_out_full[0]))[0]
     visual = lax.psum_scatter(
-        jnp.dot(picked, merge_w, preferred_element_type=jnp.float32),
+        merge_partial,
         "seq",
         scatter_dimension=0,
         tiled=True,
@@ -132,10 +153,12 @@
         "gct,td->gcd", selector, visual, preferred_element_type=jnp.float32
     ).astype(jnp.bfloat16)
     arrived_flags = jnp.sum(selector.astype(jnp.float32), axis=2).astype(jnp.bfloat16)
-    incoming, arrived = (
-        lax.all_to_all(outgoing, "grp", split_axis=0, concat_axis=0, tiled=True),
-        lax.all_to_all(arrived_flags, "grp", split_axis=0, concat_axis=0, tiled=True),
-    )
+    flag_row = jnp.pad(arrived_flags, ((0, 0), (0, model_width - capacity)))[:, None, :]
+    payload = lax.all_to_all(
+        jnp.concatenate([outgoing, flag_row], axis=1), "grp", split_axis=0, concat_axis=0, tiled=True
+    )
+    incoming = payload[:, :capacity, :]
+    arrived = payload[:, capacity, :capacity]
     prompt_rows = text_emb.shape[0]
     slot_targets = slot_rows[0, 0, : groups * capacity]
     placement_map = (
@@ -158,9 +181,7 @@
         return (key_positions[None, :] <= row_indices[:, None]) & (key_positions[None, :] < length)
 
     txt_heads = attend_local(txt_proj[0], txt_proj[1], txt_proj[2], txt_allowed)
-    txt_attn = jnp.dot(
-        heads_to_rows(txt_heads, seq_count), txt_out_full, preferred_element_type=jnp.float32
-    )
+    txt_attn = project_shared(heads_to_rows(txt_heads, seq_count), txt_out_full)
     return hidden.astype(jnp.float32) + txt_attn
 
 

time: 389 us -> 408 us (1.049)
  blocking collectives: 15.7 us -> 35 us
  local copies, waits for them, and re-layouts: 11.7 us -> 25.7 us
  starting transfers between devices: 19.6 us -> 9.06 us
  waiting for transfers between devices: 258 us -> 253 us
    all_gather x3, waiting for transfers between devices: 120 us -> 91.7 us  [the longest x1 71 us: per_device(): vis_gathered = lax.all_gather(vis_normed, 'seq', axis=0, tiled=True)]
    all_to_all x0 -> x1, blocking collectives: none -> 14.3 us  [heads_to_rows(): lax.all_to_all(blocks, 'seq', split_axis=0, concat_axis=0, tiled=True)]
    reduce_scatter x1, waiting for transfers between devices: 63.9 us -> 77.9 us  [per_device(): lax.psum_scatter(merge_partial, 'seq', scatter_dimension=0, tiled=True)]
    all_to_all x2 -> x1, waiting for transfers between devices: 0.01 us -> 13.1 us  [heads_to_rows(): lax.all_to_all(blocks, 'seq', split_axis=0, concat_axis=0, tiled=True)]
    all_gather x0 -> x2, local copies, waits for them, and re-layouts: none -> 10.7 us  [gather_shared(): mine_full = lax.all_gather(mine, 'seq', axis=0, tiled=True)]
    all_to_all x2 -> x1, starting transfers between devices: 10.5 us -> 4.46 us  [heads_to_rows(): lax.all_to_all(blocks, 'seq', split_axis=0, concat_axis=0, tiled=True)]
    all_to_all x1, blocking collectives: 15.7 us -> 20.7 us  [per_device(): lax.all_to_all(merged_in, 'seq', split_axis=1, concat_axis=0, tiled=True)]
    all_to_all x2 -> x1, starting transfers between devices: 8.84 us -> 4.43 us  [per_device(): lax.all_to_all(jnp.concatenate([outgoing, flag_row], axis=1), 'grp', spli...]
  transfers between devices with their start and end apart: 9 -> 9, of which waited for: 7 -> 7; matrix products, arithmetic and copies ran while one was open for 16% -> 20% of each run, Pallas kernels for 0% -> 0%
where the time goes in v2:
time: 408 us; the launch traced here: 407 us
  waiting for transfers between devices  253 us (62%)
  matrix products  49.5 us (12%)
  blocking collectives  35 us (9%)
  local copies, waits for them, and re-layouts  25.7 us (6%)
  other arithmetic  20.5 us (5%)
  between operations  13.5 us (3%)
  starting transfers between devices  9.06 us (2%)
    reduce_scatter x1, waiting for transfers between devices, per_device(): lax.psum_scatter(merge_partial, 'seq', scatter_dimension=0, tiled=True)  77.9 us
    all_gather x1, waiting for transfers between devices, per_device(): vis_gathered = lax.all_gather(vis_normed, 'seq', axis=0, tiled=True)  71 us
    all_gather x1, waiting for transfers between devices, per_device(): lax.all_gather(txt_normed, 'seq', axis=0, tiled=True)  61.4 us
    all_gather x2, waiting for transfers between devices, gather_shared(): mine_full = lax.all_gather(mine, 'seq', axis=0, tiled=True)  20.7 us
    all_to_all x1, blocking collectives, per_device(): lax.all_to_all(merged_in, 'seq', split_axis=1, concat_axis=0, tiled=True)  20.7 us
    all_to_all x1, blocking collectives, heads_to_rows(): lax.all_to_all(blocks, 'seq', split_axis=0, concat_axis=0, tiled=True)  14.3 us
    dot_general x8, matrix products, one_block(): jnp.einsum('qhe,khe->hqk', query_part, key_heads, preferred_element_type=...  13.5 us
    all_to_all x1, waiting for transfers between devices, heads_to_rows(): lax.all_to_all(blocks, 'seq', split_axis=0, concat_axis=0, tiled=True)  13.1 us
  transfers between devices with their start and end apart: 9, of which 7 were waited for; matrix products, arithmetic and copies ran while one was open for 20% of the time, Pallas kernels for 0%

profile of v2, /device:TPU:0, one launch (start us, length us, event | category | flops | bytes accessed | tf_op | source)
XLA Modules:
  0.0 406.7 jit_solution(1949332091740989229)
XLA Ops:
  6.5 1.4 copy.77
  8.4 1.7 fusion.32
  10.2 0.8 reduce-window.4
  11.2 71.0 %all-gather.5.cloned.1.call-done = bf16[2048,1664]{0,1:T(8,128)(2,1)} async-done(((bf16[128,1664]{0,1:T(8,128)(2,1)}), bf16[2048,1664]{0,1:T(8,128)(2,1)}) %all-gather.5.cloned.1.call-update) | async-done | bytes 6815760 | tf_op jit(solution)/shard_map/all_gather | solution.py:110
  82.2 1.7 constant_dynamic-slice_fusion.1
  84.0 5.7 %fusion.52 = f32[2048,312]{0,1:S(1)} fusion(bf16[2048,1664]{0,1:T(8,128)(2,1)} %all-gather.5.cloned.1.call-done, bf16[1664,312]{0,1:T(8,128)(2,1)} %bitcast.156), kind=kOutput, calls=%fused_computation.114 | convolution fusion | flops 2126512128 | bytes 10409984
  90.3 0.8 copy.79
  91.1 20.1 %while.24 = (s32[]{:T(128)}, bf16[4,512,1,104]{1,3,2,0:T(8,128)(2,1)S(1)}, s32[4]{0:T(128)S(1)}, s32[3]{0:T(128)S(1)}, s32[2048]{0:T(1024)S(1)}, /*index=5*/bf16...) while((s32[]{:T(128)}, ...), condition=%wide.region_10.11_spmd, body=%wide.region_6.10_spmd.sunk | while | flops 445709312 | bytes 13675133 | solution.py:57
  92.5 1.9 fusion.81
  94.4 0.7 fusion.82
  95.1 1.1 fusion.83
  97.5 1.9 fusion.81
  99.4 0.7 fusion.82
  100.1 1.1 fusion.83
  102.5 1.9 fusion.81
  104.4 0.7 fusion.82
  105.1 1.1 fusion.83
  107.6 1.9 fusion.81
  109.5 0.7 fusion.82
  110.2 1.1 fusion.83
  111.6 0.8 constant_dynamic-slice_fusion
  112.4 18.5 %all-gather.7.cloned.1.call-done = bf16[1664,832]{1,0:T(8,128)(2,1)} async-done(((bf16[104,832]{1,0:T(8,128)(2,1)}), bf16[1664,832]{1,0:T(8,128)(2,1)}) %all-gather.7.cloned.1.call-update) | async-done | bytes 2768912 | tf_op jit(solution)/shard_map/all_gather | solution.py:74
  131.0 5.3 %copy.82 = bf16[1664,832]{0,1:T(8,128)(2,1)} copy(bf16[1664,832]{1,0:T(8,128)(2,1)} %all-gather.7.cloned.1.call-done) | data formatting | bytes 5537792 | tf_op jit(solution)/shard_map/all_gather | solution.py:74
  136.3 0.8 copy_bitcast_fusion
  137.1 4.5 %all-to-all-start = ((bf16[16,128,104]{1,2,0:T(8,128)(2,1)}), bf16[16,128,104]{1,2,0:T(8,128)(2,1)S(1)}, u32[]{:S(2)}, u32[]{:S(2)}) async-start(bf16[16,128,104]{1,2,0:T(8,128)(2,1)} %copy_bitcast_fusion), calls=%async_computation | async-start | bytes 851968 | tf_op jit(solution)/shard_map/all_to_all | solution.py:65
  141.7 13.1 %all-to-all-done = bf16[16,128,104]{1,2,0:T(8,128)(2,1)S(1)} async-done(((bf16[16,128,104]{1,2,0:T(8,128)(2,1)}), bf16[16,128,104]{1,2,0:T(8,128)(2,1)S(1)}, u32[]{:S(2)}, u32[]{:S(2)}) %all-to-all-start) | async-done | bytes 426016 | tf_op jit(solution)/shard_map/all_to_all | solution.py:65
  154.7 3.1 fusion.53
  157.8 2.7 broadcast_select_fusion.3
  162.5 20.7 %all_to_all.34 = bf16[32,16,416]{2,0,1:T(8,128)(2,1)S(1)} all-to-all(bf16[32,16,416]{2,0,1:T(8,128)(2,1)S(1)} %copy.84), channel_id=1, replica_groups=mesh['seq'=16,'grp'=8] {'seq'}, dimensions={1} | all-to-all | bytes 851968 | tf_op jit(solution)/shard_map/all_to_all | solution.py:134
  183.2 2.8 fusion.54
  186.0 2.2 all-gather.9.cloned.1.call-done
  189.0 77.9 %reduce-scatter.2.cloned.1.call-done = f32[32,1664]{1,0:T(8,128)} async-done(((f32[512,1664]{1,0:T(8,128)}), f32[32,1664]{1,0:T(8,128)}) %reduce-scatter.2.cloned.1.call-update) | async-done | bytes 213008 | tf_op jit(solution)/shard_map/reduce_scatter | solution.py:137
  266.9 1.1 convolution_convert_fusion
  268.0 0.8 pad_maximum_fusion
  268.8 4.4 %all-to-all-start.2 = ((bf16[8,9,1664]{2,1,0:T(8,128)(2,1)}), bf16[8,9,1664]{2,1,0:T(8,128)(2,1)S(1)}, u32[]{:S(2)}, u32[]{:S(2)}) async-start(bf16[8,9,1664]{2,1,0:T(8,128)(2,1)} %pad_maximum_fusion), calls=%async_computation.3 | async-start | bytes 851968 | tf_op jit(solution)/shard_map/all_to_all | solution.py:157
  273.3 9.2 %all-to-all-done.2 = bf16[8,9,1664]{2,1,0:T(8,128)(2,1)S(1)} async-done(((bf16[8,9,1664]{2,1,0:T(8,128)(2,1)}), bf16[8,9,1664]{2,1,0:T(8,128)(2,1)S(1)}, u32[]{:S(2)}, u32[]{:S(2)}) %all-to-all-start.2) | async-done | bytes 239648 | tf_op jit(solution)/shard_map/all_to_all | solution.py:157
  283.2 1.0 multiply_convert_fusion
  284.3 5.4 %copy.91 = bf16[1664,832]{0,1:T(8,128)(2,1)} copy(bf16[1664,832]{1,0:T(8,128)(2,1)} %all-gather.9.cloned.1.call-done) | data formatting | bytes 5537792 | tf_op jit(solution)/shard_map/all_gather | solution.py:74
  289.7 61.4 %all-gather.11.cloned.1.call-done = bf16[2048,1664]{0,1:T(8,128)(2,1)} async-done(((bf16[128,1664]{0,1:T(8,128)(2,1)}), bf16[2048,1664]{0,1:T(8,128)(2,1)}) %all-gather.11.cloned.1.call-update) | async-done | bytes 6815760 | tf_op jit(solution)/shard_map/all_gather | solution.py:176
  351.2 5.5 %fusion.55 = f32[2048,312]{0,1:S(1)} fusion(bf16[2048,1664]{0,1:T(8,128)(2,1)} %all-gather.11.cloned.1.call-done, bf16[1664,312]{0,1:T(8,128)(2,1)S(1)} %bitcast.157), kind=kOutput, calls=%fused_computation.117 | convolution fusion | flops 2126512128 | bytes 10409984
  357.4 20.8 %while.25 = (s32[]{:T(128)}, bf16[4,512,1,104]{1,3,2,0:T(8,128)(2,1)S(1)}, s32[4]{0:T(128)S(1)}, s32[]{:T(128)}, bf16[4,512,1,104]{1,3,2,0:T(8,128)(2,1)S(1)}, /...) while((s32[]{:T(128)}, ...), condition=%wide.region_20.21_spmd.clone.clone, body=%wide.region_17.20_spmd.clone.clone.sunk | while | flops 446748160 | bytes 13666417 | solution.py:57
  358.0 0.6 iota_add_fusion.3
  358.6 0.7 iota_compare_fusion.7
  359.3 1.5 fusion.85
  360.8 0.7 fusion.86
  361.5 1.1 fusion.87
  363.2 0.6 iota_add_fusion.3
  363.8 0.7 iota_compare_fusion.7
  364.5 1.5 fusion.85
  366.0 0.7 fusion.86
  366.7 1.1 fusion.87
  368.4 0.6 iota_add_fusion.3
  369.0 0.7 iota_compare_fusion.7
  369.7 1.5 fusion.85
  371.2 0.7 fusion.86
  371.9 1.1 fusion.87
  374.2 0.7 iota_compare_fusion.7
  374.9 1.5 fusion.85
  376.4 0.7 fusion.86
  377.1 1.1 fusion.87
  378.7 14.3 %all_to_all.35 = bf16[16,128,104]{1,2,0:T(8,128)(2,1)S(1)} all-to-all(bf16[16,128,104]{1,2,0:T(8,128)(2,1)S(1)} %copy.90), channel_id=1, replica_groups=mesh['seq'=16,'grp'=8] {'seq'}, dimensions={0} | all-to-all | bytes 851968 | tf_op jit(solution)/shard_map/all_to_all | solution.py:65
  393.0 3.2 fusion.56
  396.2 2.7 broadcast_select_fusion.1
  399.0 1.2 copy.92
  (95 shorter events, 14.7 us)
Async XLA Ops:
  6.5 176.6 %copy-start = (bf16[416,1664]{1,0:T(8,128)(2,1)S(1)}, bf16[416,1664]{1,0:T(8,128)(2,1)}, u32[]{:S(2)}) copy-start(bf16[416,1664]{1,0:T(8,128)(2,1)} %param.23) | copy-start | bytes 4153348
  6.5 75.6 %all-gather.5.cloned.1.call-start = ((), (), s32[]{:S(2)}) async-start(), calls=%async_computation.5 | async-start | bytes 7241728 | tf_op jit(solution)/shard_map/all_gather | solution.py:110
  10.2 120.8 %all-gather.7.cloned.1.call-start = ((), (), s32[]{:S(2)}) async-start(), calls=%async_computation.6 | async-start | bytes 3168256 | tf_op jit(solution)/shard_map/all_gather | solution.py:74
  83.9 104.2 %all-gather.9.cloned.1.call-start = ((), (), s32[]{:S(2)}) async-start(), calls=%async_computation.7 | async-start | bytes 3168256 | tf_op jit(solution)/shard_map/all_gather | solution.py:74
  91.1 20.5 %copy-start.3 = (bf16[104,1664]{1,0:T(8,128)(2,1)S(1)}, bf16[104,1664]{1,0:T(8,128)(2,1)}, u32[]{:S(2)}) copy-start(bf16[104,1664]{1,0:T(8,128)(2,1)} %param.31) | copy-start | bytes 1038340
  136.3 21.5 %collective-permute-start = (bf16[1664,832]{0,1:T(8,128)(2,1)}, bf16[1664,832]{0,1:T(8,128)(2,1)}, u32[]{:S(2)}, u32[]{:S(2)}) collective-permute-start(bf16[1664,832]{0,1:T(8,128)(2,1)} %copy.82), channel_id=1, source_target_pairs={{0,1},{1,0},{2,3},{3,2},{4,5},{5,4},{6,7},{7,6},{8,9},{9,8},{10,11... | collective-permute-start | bytes 8306696 | tf_op jit(solution)/shard_map/ppermute | solution.py:75
  137.1 17.6 %all-to-all-start = ((bf16[16,128,104]{1,2,0:T(8,128)(2,1)}), bf16[16,128,104]{1,2,0:T(8,128)(2,1)S(1)}, u32[]{:S(2)}, u32[]{:S(2)}) async-start(bf16[16,128,104]{1,2,0:T(8,128)(2,1)} %copy_bitcast_fusion), calls=%async_computation | async-start | bytes 851968 | tf_op jit(solution)/shard_map/all_to_all | solution.py:65
  141.6 125.3 %reduce-scatter.2.cloned.1.call-start = ((), (), s32[]{:S(2)}) async-start(), calls=%async_computation.8 | async-start | bytes 3620864 | tf_op jit(solution)/shard_map/reduce_scatter | solution.py:137
  157.8 3.2 copy-start.4
  183.1 5.0 %copy-start.6 = (s32[32,1]{0,1:T(1,128)S(1)}, s32[32,1]{0,1:T(1,128)}, u32[]{:S(2)}) copy-start(s32[32,1]{0,1:T(1,128)} %param.25) | copy-start | bytes 388
  183.2 5.5 %copy-start.2 = (bf16[128,1664]{1,0:T(8,128)(2,1)S(1)}, bf16[128,1664]{1,0:T(8,128)(2,1)}, u32[]{:S(2)}) copy-start(bf16[128,1664]{1,0:T(8,128)(2,1)} %param.28) | copy-start | bytes 1277956
  186.0 87.3 %copy-start.8 = (s32[1,1,128]{2,1,0:T(1,128)S(1)}, s32[1,1,128]{2,1,0:T(1,128)}, u32[]{:S(2)}) copy-start(s32[1,1,128]{2,1,0:T(1,128)} %param.26) | copy-start | bytes 1540
  186.0 97.2 %copy-start.5 = (f32[1664]{0:T(1024)S(1)}, f32[1664]{0:T(1024)}, u32[]{:S(2)}) copy-start(f32[1664]{0:T(1024)} %param.29) | copy-start | bytes 19972
  268.8 13.7 %all-to-all-start.2 = ((bf16[8,9,1664]{2,1,0:T(8,128)(2,1)}), bf16[8,9,1664]{2,1,0:T(8,128)(2,1)S(1)}, u32[]{:S(2)}, u32[]{:S(2)}) async-start(bf16[8,9,1664]{2,1,0:T(8,128)(2,1)} %pad_maximum_fusion), calls=%async_computation.3 | async-start | bytes 851968 | tf_op jit(solution)/shard_map/all_to_all | solution.py:157
  273.2 77.9 %all-gather.11.cloned.1.call-start = ((), (), s32[]{:S(2)}) async-start(), calls=%async_computation.9 | async-start | bytes 7241728 | tf_op jit(solution)/shard_map/all_gather | solution.py:176
  282.7 68.4 %copy-start.7 = (bf16[3,1664,104]{1,2,0:T(8,128)(2,1)S(1)}, bf16[3,1664,104]{1,2,0:T(8,128)(2,1)}, u32[]{:S(2)}) copy-start(bf16[3,1664,104]{1,2,0:T(8,128)(2,1)} %param.30) | copy-start | bytes 3115012
  289.7 106.5 %collective-permute-start.1 = (bf16[1664,832]{0,1:T(8,128)(2,1)}, bf16[1664,832]{0,1:T(8,128)(2,1)}, u32[]{:S(2)}, u32[]{:S(2)}) collective-permute-start(bf16[1664,832]{0,1:T(8,128)(2,1)} %copy.91), channel_id=1, source_target_pairs={{0,1},{1,0},{2,3},{3,2},{4,5},{5,4},{6,7},{7,6},{8,9},{9,8},{10,11... | collective-permute-start | bytes 8306696 | tf_op jit(solution)/shard_map/ppermute | solution.py:75
  393.0 7.2 %copy-start.1 = (bf16[416,1664]{1,0:T(8,128)(2,1)S(1)}, bf16[416,1664]{1,0:T(8,128)(2,1)}, u32[]{:S(2)}) copy-start(bf16[416,1664]{1,0:T(8,128)(2,1)} %param.23) | copy-start | bytes 4153348
Sparse Core Ops, SparseCore 0:
  10.3 71.8 all-gather.4
  84.3 46.6 all-gather.6
  133.1 54.9 all-gather.8
  191.4 75.4 reduce-scatter.1
  284.4 66.6 all-gather.10

commit v3 on v2

--- a/solution.py
+++ b/solution.py
@@ -1,3 +1,5 @@
+import functools
+
 import jax
 import jax.numpy as jnp
 from jax import lax
@@ -66,12 +68,31 @@
     return swapped.transpose(1, 0, 2).reshape(rows, seq_count * width)
 
 
-def gather_shared(w_local):
+def permute_gather_seq(piece, grid):
+    ny, nx = grid
+    seq_index = lax.axis_index("seq")
+    y, x = seq_index // nx, seq_index % nx
+
+    def shift(dy, dx):
+        return [
+            (a * nx + b, ((a + dy) % ny) * nx + (b + dx) % nx)
+            for a in range(ny)
+            for b in range(nx)
+        ]
+
+    row = jnp.stack([piece] + [lax.ppermute(piece, "seq", shift(0, dx)) for dx in range(1, nx)])
+    full = jnp.stack([row] + [lax.ppermute(row, "seq", shift(dy, 0)) for dy in range(1, ny)])
+    full = jnp.take(full, (y - jnp.arange(ny)) % ny, axis=0)
+    full = jnp.take(full, (x - jnp.arange(nx)) % nx, axis=1)
+    return full.reshape(ny * nx * piece.shape[0], piece.shape[1])
+
+
+def gather_shared(w_local, grid):
     half = w_local.shape[1] // 2
     groups = lax.axis_size("grp")
     core = lax.axis_index("grp") % 2
     mine = lax.dynamic_slice_in_dim(w_local, core * half, half, axis=1)
-    mine_full = lax.all_gather(mine, "seq", axis=0, tiled=True)
+    mine_full = permute_gather_seq(mine, grid)
     other_full = lax.ppermute(mine_full, "grp", [(g, g ^ 1) for g in range(groups)])
     return mine_full, other_full, core
 
@@ -86,6 +107,7 @@
 
 
 def per_device(
+    grid,
     patches,
     vis_gain,
     vis_qkv,
@@ -108,8 +130,8 @@
     group_patches = token_count * seq_count
     vis_normed = layer_norm(patches, vis_gain).astype(jnp.bfloat16)
     vis_gathered = lax.all_gather(vis_normed, "seq", axis=0, tiled=True)
-    vis_gathered, vis_out, txt_out = lax.optimization_barrier((vis_gathered, vis_out, txt_out))
-    vis_out_full = gather_shared(vis_out)
+    vis_out_full = gather_shared(vis_out, grid)
+    txt_out_full = gather_shared(txt_out, grid)
     vis_proj = projector(vis_qkv, vis_gathered)
     bounds = jnp.cumsum(image_blocks[0])[:-1]
 
@@ -122,8 +144,6 @@
         return segment(row_indices)[:, None] == key_segments[None, :]
 
     vis_heads = attend_local(vis_proj[0], vis_proj[1], vis_proj[2], vis_allowed)
-    vis_heads, txt_out = lax.optimization_barrier((vis_heads, txt_out))
-    txt_out_full = gather_shared(txt_out)
     vis_attn = project_shared(heads_to_rows(vis_heads, seq_count), vis_out_full)
     residual_sum = patches.astype(jnp.float32) + vis_attn
     merged_in = (
@@ -133,7 +153,6 @@
     )
     feature_slices = lax.all_to_all(merged_in, "seq", split_axis=1, concat_axis=0, tiled=True)
     merge_partial = jnp.dot(feature_slices, merge_w, preferred_element_type=jnp.float32)
-    merge_partial = lax.optimization_barrier((merge_partial, txt_out_full[0]))[0]
     visual = lax.psum_scatter(
         merge_partial,
         "seq",
@@ -183,6 +202,18 @@
     txt_heads = attend_local(txt_proj[0], txt_proj[1], txt_proj[2], txt_allowed)
     txt_attn = project_shared(heads_to_rows(txt_heads, seq_count), txt_out_full)
     return hidden.astype(jnp.float32) + txt_attn
+
+
+def seq_grid(mesh):
+    count = mesh.shape["seq"]
+    try:
+        xs = {d.coords[0] for d in mesh.devices.reshape(count, -1)[:, 0]}
+        nx = len(xs)
+    except Exception:
+        nx = 1
+    if nx <= 1 or count % nx:
+        nx = max(d for d in range(1, count + 1) if count % d == 0 and d * d <= count)
+    return count // nx, nx
 
 
 def solution(mesh):
@@ -204,5 +235,5 @@
     )
     out_specs = P(("grp", "seq"), None)
     return jax.shard_map(
-        per_device, mesh=mesh, in_specs=in_specs, out_specs=out_specs, check_vma=False
-    )
+        functools.partial(per_device, seq_grid(mesh)), mesh=mesh, in_specs=in_specs, out_specs=out_specs, check_vma=False
+    )

time: 408 us -> 438 us (1.074)
  local copies, waits for them, and re-layouts: 25.7 us -> 45.5 us
  other arithmetic: 20.5 us -> 40.1 us
  starting transfers between devices: 9.06 us -> 27.2 us
  waiting for transfers between devices: 253 us -> 236 us
  blocking collectives: 35 us -> 29.4 us
  matrix products: 49.5 us -> 44.6 us
    ppermute x0 -> x12, waiting for transfers between devices: none -> 89.5 us  [the longest x6 77.9 us: permute_gather_seq(): lax.ppermute(row, 'seq', shift(dy, 0))]
    all_gather x1, waiting for transfers between devices: 71 us -> 0.01 us  [per_device(): vis_gathered = lax.all_gather(vis_normed, 'seq', axis=0, tiled=True)]
    all_gather x2 -> x0, waiting for transfers between devices: 20.7 us -> none  [gather_shared(): mine_full = lax.all_gather(mine, 'seq', axis=0, tiled=True)]
    gather x0 -> x4, local copies, waits for them, and re-layouts: none -> 17.5 us  [the longest x2 8.73 us: permute_gather_seq(): full = jnp.take(full, (y - jnp.arange(ny)) % ny, axis=0)]
    ppermute x0 -> x12, starting transfers between devices: none -> 16.9 us  [the longest x6 8.57 us: permute_gather_seq(): lax.ppermute(piece, 'seq', shift(0, dx))]
    select_n x0 -> x4, other arithmetic: none -> 11 us  [the longest x2 5.92 us: permute_gather_seq(): full = jnp.take(full, (y - jnp.arange(ny)) % ny, axis=0)]
    all_gather x2 -> x0, local copies, waits for them, and re-layouts: 10.7 us -> none  [gather_shared(): mine_full = lax.all_gather(mine, 'seq', axis=0, tiled=True)]
    reshape x1 -> x2, local copies, waits for them, and re-layouts: 0.83 us -> 10.9 us  [permute_gather_seq(): return full.reshape(ny * nx * piece.shape[0], piece.shape[1])]
  transfers between devices with their start and end apart: 9 -> 19, of which waited for: 7 -> 15; matrix products, arithmetic and copies ran while one was open for 20% -> 25% of each run, Pallas kernels for 0% -> 0%
where the time goes in v3:
time: 438 us; the launch traced here: 436 us
  waiting for transfers between devices  236 us (54%)
  local copies, waits for them, and re-layouts  45.5 us (10%)
  matrix products  44.6 us (10%)
  other arithmetic  40.1 us (9%)
  blocking collectives  29.4 us (7%)
  starting transfers between devices  27.2 us (6%)
  between operations  13.5 us (3%)
    ppermute x6, waiting for transfers between devices, permute_gather_seq(): lax.ppermute(row, 'seq', shift(dy, 0))  77.9 us
    reduce_scatter x1, waiting for transfers between devices, per_device(): lax.psum_scatter(merge_partial, 'seq', scatter_dimension=0, tiled=True)  74.1 us
    all_gather x1, waiting for transfers between devices, per_device(): lax.all_gather(txt_normed, 'seq', axis=0, tiled=True)  51.9 us
    all_to_all x1, blocking collectives, heads_to_rows(): lax.all_to_all(blocks, 'seq', split_axis=0, concat_axis=0, tiled=True)  15.3 us
    all_to_all x1, blocking collectives, per_device(): lax.all_to_all(merged_in, 'seq', split_axis=1, concat_axis=0, tiled=True)  14.1 us
    ppermute x6, waiting for transfers between devices, permute_gather_seq(): lax.ppermute(piece, 'seq', shift(0, dx))  11.6 us
    all_to_all x1, waiting for transfers between devices, heads_to_rows(): lax.all_to_all(blocks, 'seq', split_axis=0, concat_axis=0, tiled=True)  11.1 us
    unnamed x2, matrix products  10.9 us
  transfers between devices with their start and end apart: 19, of which 15 were waited for; matrix products, arithmetic and copies ran while one was open for 25% of the time, Pallas kernels for 0%

profile of v3, /device:TPU:0, one launch (start us, length us, event | category | flops | bytes accessed | tf_op | source)
XLA Modules:
  0.0 436.4 jit_solution(9819825152684655348)
XLA Ops:
  6.5 1.3 convert_reduce_fusion.1
  7.8 1.3 fusion.30
  9.1 2.1 fusion.32
  11.2 1.1 constant_dynamic-slice_fusion.1
  12.3 2.9 collective-permute-start.9
  16.9 1.1 constant_dynamic-slice_fusion
  18.0 2.4 collective-permute-start.2
  20.4 1.5 collective-permute-start.1
  22.9 1.3 collective-permute-done.9
  24.4 4.5 %collective-permute-done.7 = bf16[104,832]{1,0:T(8,128)(2,1)S(1)} collective-permute-done((bf16[104,832]{1,0:T(8,128)(2,1)S(1)}, bf16[104,832]{1,0:T(8,128)(2,1)S(1)}, u32[]{:S(2)}, u32[]{:S(2)}) %collective-permute-start.7) | collective-permute-done | bytes 173088 | tf_op jit(solution)/shard_map/ppermute | solution.py:83
  29.0 3.1 collective-permute-start.12
  32.9 1.8 collective-permute-done.2
  35.9 3.6 collective-permute-done
  39.6 3.2 collective-permute-start.5
  43.3 26.3 %collective-permute-done.12 = bf16[4,104,832]{2,1,0:T(8,128)(2,1)S(1)} collective-permute-done((bf16[4,104,832]{2,1,0:T(8,128)(2,1)S(1)}, bf16[4,104,832]{2,1,0:T(8,128)(2,1)S(1)}, u32[]{:S(2)}, u32[]{:S(2)}) %collective-permute-start.12) | collective-permute-done | bytes 692256 | tf_op jit(solution)/shard_map/ppermute | solution.py:84
  69.8 7.3 %collective-permute-done.10 = bf16[4,104,832]{2,1,0:T(8,128)(2,1)S(1)} collective-permute-done((bf16[4,104,832]{2,1,0:T(8,128)(2,1)S(1)}, bf16[4,104,832]{2,1,0:T(8,128)(2,1)S(1)}, u32[]{:S(2)}, u32[]{:S(2)}) %collective-permute-start.10) | collective-permute-done | bytes 692256 | tf_op jit(solution)/shard_map/ppermute | solution.py:84
  77.0 1.9 pad_maximum_fusion.1
  78.9 4.4 %gather_fusion.2 = bf16[4,4,104,832]{3,2,1,0:T(8,128)(2,1)} fusion(bf16[4,4,104,832]{3,2,1,0:T(8,128)(2,1)} %pad_maximum_fusion.1, s32[1024]{0:T(1024)S(1)} %pad_clamp_fusion.1), kind=kCustom, calls=%fused_computation.2.clone | custom fusion | bytes 5537808 | tf_op jit(solution)/shard_map/jit(_take)/gather | solution.py:85
  83.3 19.9 %collective-permute-done.5 = bf16[4,104,832]{2,1,0:T(8,128)(2,1)} collective-permute-done((bf16[4,104,832]{2,1,0:T(8,128)(2,1)S(1)}, bf16[4,104,832]{2,1,0:T(8,128)(2,1)}, u32[]{:S(2)}, u32[]{:S(2)}) %collective-permute-start.5) | collective-permute-done | bytes 692256 | tf_op jit(solution)/shard_map/ppermute | solution.py:84
  103.1 3.9 collective-permute-done.4
  107.0 20.6 %collective-permute-done.3 = bf16[4,104,832]{2,1,0:T(8,128)(2,1)} collective-permute-done((bf16[4,104,832]{2,1,0:T(8,128)(2,1)S(1)}, bf16[4,104,832]{2,1,0:T(8,128)(2,1)}, u32[]{:S(2)}, u32[]{:S(2)}) %collective-permute-start.3) | collective-permute-done | bytes 692256 | tf_op jit(solution)/shard_map/ppermute | solution.py:84
  127.6 3.1 pad_maximum_fusion
  130.7 4.3 gather_fusion
  135.0 5.9 %broadcast_select_fusion = (bf16[4,4,104,832]{3,2,1,0:T(8,128)(2,1)}, bf16[4,4,104,832]{3,2,1,0:T(8,128)(2,1)}) fusion(bf16[4,4,104,832]{3,2,1,0:T(8,128)(2,1)} %gather_fusion.2, pred[4]{0:T(512)(128)(4,1)S(1)} %get-tuple-element.307, bf16[4,4,104,832]{3,2,1,0:T(8,128)(2,1)} %gather_fusion), kind=kLoop, calls=%fused_computation.49 | loop fusion | flops 2768896 | bytes 11075588 | tf_op jit(solution)/shard_map/jit(_take)/select_n | solution.py:85
  140.9 4.3 gather_fusion.3
  145.3 4.4 %gather_fusion.1 = bf16[4,4,104,832]{3,2,1,0:T(8,128)(2,1)} fusion(bf16[4,4,104,832]{3,2,1,0:T(8,128)(2,1)} %get-tuple-element.303, s32[1024]{0:T(1024)S(1)} %pad_clamp_fusion), kind=kCustom, calls=%fused_computation.1.clone | custom fusion | bytes 5537808 | tf_op jit(solution)/shard_map/jit(_take)/gather | solution.py:86
  149.7 5.0 %select_bitcast_fusion = (bf16[4,4,104,832]{3,2,0,1:T(8,128)(2,1)}, bf16[4,4,104,832]{3,2,0,1:T(8,128)(2,1)S(1)}) fusion(bf16[4,4,104,832]{3,2,1,0:T(8,128)(2,1)} %gather_fusion.3, pred[4]{0:T(512)(128)(4,1)S(1)} %get-tuple-element.306, bf16[4,4,104,832]{3,2,1,0:T(8,128)(2,1)} %gather_fusion.1), kind=kLoop, calls=%fused_computation.47 | loop fusion | flops 2768896 | bytes 11075588 | tf_op jit(solution)/shard_map/jit(_take)/select_n | solution.py:86
  154.7 1.9 copy.70
  156.6 5.4 %copy.71 = bf16[1664,832]{0,1:T(8,128)(2,1)} copy(bf16[1664,832]{1,0:T(8,128)(2,1)} %bitcast.162) | data formatting | bytes 5537792 | tf_op jit(solution)/shard_map/reshape | solution.py:87
  162.0 5.5 %fusion.56 = f32[2048,312]{0,1:S(1)} fusion(bf16[2048,1664]{1,0:T(8,128)(2,1)} %all-gather.3.cloned.1.call-done, bf16[1664,312]{0,1:T(8,128)(2,1)S(1)} %bitcast.185), kind=kOutput, calls=%fused_computation.141 | convolution fusion | flops 2126512128 | bytes 10409984
  168.2 16.5 %while.24 = (s32[]{:T(128)}, bf16[4,512,1,104]{1,3,2,0:T(8,128)(2,1)S(1)}, s32[4]{0:T(128)S(1)}, s32[3]{0:T(128)S(1)}, s32[2048]{0:T(1024)S(1)}, /*index=5*/bf16...) while((s32[]{:T(128)}, ...), condition=%wide.region_10.11_spmd, body=%wide.region_6.10_spmd.sunk | while | flops 445709312 | bytes 13674633 | solution.py:59
  171.2 1.1 fusion.88
  175.3 1.1 fusion.88
  177.8 1.0 fusion.86
  179.5 1.1 fusion.88
  181.9 1.0 fusion.86
  183.6 1.1 fusion.88
  186.0 5.8 %all-to-all-start = ((bf16[16,128,104]{1,2,0:T(8,128)(2,1)}), bf16[16,128,104]{1,2,0:T(8,128)(2,1)S(1)}, u32[]{:S(2)}, u32[]{:S(2)}) async-start(bf16[16,128,104]{1,2,0:T(8,128)(2,1)} %copy.69), calls=%async_computation | async-start | bytes 851968 | tf_op jit(solution)/shard_map/all_to_all | solution.py:67
  191.8 11.1 %all-to-all-done = bf16[16,128,104]{1,2,0:T(8,128)(2,1)S(1)} async-done(((bf16[16,128,104]{1,2,0:T(8,128)(2,1)}), bf16[16,128,104]{1,2,0:T(8,128)(2,1)S(1)}, u32[]{:S(2)}, u32[]{:S(2)}) %all-to-all-start) | async-done | bytes 426016 | tf_op jit(solution)/shard_map/all_to_all | solution.py:67
  202.9 2.5 fusion.57
  205.4 2.8 broadcast_select_fusion.5
  210.0 14.1 %all_to_all.34 = bf16[32,16,416]{2,0,1:T(8,128)(2,1)S(1)} all-to-all(bf16[32,16,416]{2,0,1:T(8,128)(2,1)S(1)} %copy.76), channel_id=1, replica_groups=mesh['seq'=16,'grp'=8] {'seq'}, dimensions={1} | all-to-all | bytes 851968 | tf_op jit(solution)/shard_map/all_to_all | solution.py:154
  224.1 2.8 fusion.58
  228.1 74.1 %reduce-scatter.2.cloned.1.call-done = f32[32,1664]{1,0:T(8,128)} async-done(((f32[512,1664]{1,0:T(8,128)}), f32[32,1664]{1,0:T(8,128)}) %reduce-scatter.2.cloned.1.call-update) | async-done | bytes 213008 | tf_op jit(solution)/shard_map/reduce_scatter | solution.py:156
  302.2 1.1 convolution_convert_fusion
  304.2 4.4 %all-to-all-start.2 = ((bf16[8,9,1664]{2,1,0:T(8,128)(2,1)}), bf16[8,9,1664]{2,1,0:T(8,128)(2,1)S(1)}, u32[]{:S(2)}, u32[]{:S(2)}) async-start(bf16[8,9,1664]{2,1,0:T(8,128)(2,1)} %pad_maximum_fusion.4), calls=%async_computation.3 | async-start | bytes 851968 | tf_op jit(solution)/shard_map/all_to_all | solution.py:176
  308.7 9.2 %all-to-all-done.2 = bf16[8,9,1664]{2,1,0:T(8,128)(2,1)S(1)} async-done(((bf16[8,9,1664]{2,1,0:T(8,128)(2,1)}), bf16[8,9,1664]{2,1,0:T(8,128)(2,1)S(1)}, u32[]{:S(2)}, u32[]{:S(2)}) %all-to-all-start.2) | async-done | bytes 239648 | tf_op jit(solution)/shard_map/all_to_all | solution.py:176
  319.5 3.7 copy.81
  323.3 5.5 %copy.82 = bf16[1664,832]{0,1:T(8,128)(2,1)} copy(bf16[1664,832]{1,0:T(8,128)(2,1)} %bitcast.164) | data formatting | bytes 5537792 | tf_op jit(solution)/shard_map/reshape | solution.py:87
  328.7 51.9 %all-gather.5.cloned.1.call-done = bf16[2048,1664]{1,0:T(8,128)(2,1)} async-done(((bf16[128,1664]{1,0:T(8,128)(2,1)}), bf16[2048,1664]{1,0:T(8,128)(2,1)}) %all-gather.5.cloned.1.call-update) | async-done | bytes 6815760 | tf_op jit(solution)/shard_map/all_gather | solution.py:195
  380.6 5.4 %fusion.59 = f32[2048,312]{0,1:S(1)} fusion(bf16[2048,1664]{1,0:T(8,128)(2,1)} %all-gather.5.cloned.1.call-done, bf16[1664,312]{0,1:T(8,128)(2,1)S(1)} %bitcast.186), kind=kOutput, calls=%fused_computation.144 | convolution fusion | flops 2126512128 | bytes 10409984
  386.7 20.8 %while.25 = (s32[]{:T(128)}, bf16[4,512,1,104]{1,3,2,0:T(8,128)(2,1)S(1)}, s32[4]{0:T(128)S(1)}, s32[]{:T(128)}, bf16[4,512,1,104]{1,3,2,0:T(8,128)(2,1)S(1)}, /...) while((s32[]{:T(128)}, ...), condition=%wide.region_20.23_spmd.clone.clone, body=%wide.region_17.22_spmd.clone.clone.sunk | while | flops 446748160 | bytes 13666425 | solution.py:59
  388.6 1.5 fusion.90
  390.8 1.1 fusion.92
  393.9 1.5 fusion.90
  396.0 1.1 fusion.92
  399.1 1.5 fusion.90
  401.3 1.1 fusion.92
  404.3 1.5 fusion.90
  406.5 1.1 fusion.92
  408.1 15.3 %all_to_all.35 = bf16[16,128,104]{1,2,0:T(8,128)(2,1)S(1)} all-to-all(bf16[16,128,104]{1,2,0:T(8,128)(2,1)S(1)} %copy.80), channel_id=1, replica_groups=mesh['seq'=16,'grp'=8] {'seq'}, dimensions={0} | all-to-all | bytes 851968 | tf_op jit(solution)/shard_map/all_to_all | solution.py:67
  423.4 2.6 fusion.60
  426.1 2.7 broadcast_select_fusion.3
  428.8 1.1 maximum_add_fusion
  (134 shorter events, 34.7 us)
Async XLA Ops:
  6.5 217.6 %copy-start = (bf16[416,1664]{1,0:T(8,128)(2,1)S(1)}, bf16[416,1664]{1,0:T(8,128)(2,1)}, u32[]{:S(2)}) copy-start(bf16[416,1664]{1,0:T(8,128)(2,1)} %param.27) | copy-start | bytes 4153348
  6.5 16.2 %copy-start.4 = (bf16[104,1664]{1,0:T(8,128)(2,1)S(1)}, bf16[104,1664]{1,0:T(8,128)(2,1)}, u32[]{:S(2)}) copy-start(bf16[104,1664]{1,0:T(8,128)(2,1)} %param.35) | copy-start | bytes 1038340
  6.5 25.6 %copy-start.5 = (bf16[104,1664]{1,0:T(8,128)(2,1)S(1)}, bf16[104,1664]{1,0:T(8,128)(2,1)}, u32[]{:S(2)}) copy-start(bf16[104,1664]{1,0:T(8,128)(2,1)} %param.25) | copy-start | bytes 1038340
  6.5 155.5 %all-gather.3.cloned.1.call-start = ((), (), s32[]{:S(2)}) async-start(), calls=%async_computation.5 | async-start | bytes 7241728 | tf_op jit(solution)/shard_map/all_gather | solution.py:132
  12.3 11.9 %collective-permute-start.9 = (bf16[104,832]{1,0:T(8,128)(2,1)S(1)}, bf16[104,832]{1,0:T(8,128)(2,1)S(1)}, u32[]{:S(2)}, u32[]{:S(2)}) collective-permute-start(bf16[104,832]{1,0:T(8,128)(2,1)S(1)} %constant_dynamic-slice_fusion.1), channel_id=1, source_target_pairs={{0,24},{8,0},{16,8},{24,16},{32,56},{40,32},{48,40},{56,48},{64,88... | collective-permute-start | bytes 519176 | tf_op jit(solution)/shard_map/ppermute | solution.py:83
  15.2 9.1 %collective-permute-start.8 = (bf16[104,832]{1,0:T(8,128)(2,1)S(1)}, bf16[104,832]{1,0:T(8,128)(2,1)S(1)}, u32[]{:S(2)}, u32[]{:S(2)}) collective-permute-start(bf16[104,832]{1,0:T(8,128)(2,1)S(1)} %constant_dynamic-slice_fusion.1), channel_id=1, source_target_pairs={{0,16},{8,24},{16,0},{24,8},{32,48},{40,56},{48,32},{56,40},{64,80... | collective-permute-start | bytes 519176 | tf_op jit(solution)/shard_map/ppermute | solution.py:83
  16.0 12.8 %collective-permute-start.7 = (bf16[104,832]{1,0:T(8,128)(2,1)S(1)}, bf16[104,832]{1,0:T(8,128)(2,1)S(1)}, u32[]{:S(2)}, u32[]{:S(2)}) collective-permute-start(bf16[104,832]{1,0:T(8,128)(2,1)S(1)} %constant_dynamic-slice_fusion.1), channel_id=1, source_target_pairs={{0,8},{8,16},{16,24},{24,0},{32,40},{40,48},{48,56},{56,32},{64,72... | collective-permute-start | bytes 519176 | tf_op jit(solution)/shard_map/ppermute | solution.py:83
  18.0 16.7 %collective-permute-start.2 = (bf16[104,832]{1,0:T(8,128)(2,1)S(1)}, bf16[104,832]{1,0:T(8,128)(2,1)S(1)}, u32[]{:S(2)}, u32[]{:S(2)}) collective-permute-start(bf16[104,832]{1,0:T(8,128)(2,1)S(1)} %constant_dynamic-slice_fusion), channel_id=1, source_target_pairs={{0,24},{8,0},{16,8},{24,16},{32,56},{40,32},{48,40},{56,48},{64,88... | collective-permute-start | bytes 519176 | tf_op jit(solution)/shard_map/ppermute | solution.py:83
  20.4 15.5 %collective-permute-start.1 = (bf16[104,832]{1,0:T(8,128)(2,1)S(1)}, bf16[104,832]{1,0:T(8,128)(2,1)S(1)}, u32[]{:S(2)}, u32[]{:S(2)}) collective-permute-start(bf16[104,832]{1,0:T(8,128)(2,1)S(1)} %constant_dynamic-slice_fusion), channel_id=1, source_target_pairs={{0,16},{8,24},{16,0},{24,8},{32,48},{40,56},{48,32},{56,40},{64,80... | collective-permute-start | bytes 519176 | tf_op jit(solution)/shard_map/ppermute | solution.py:83
  24.2 15.3 %collective-permute-start = (bf16[104,832]{1,0:T(8,128)(2,1)S(1)}, bf16[104,832]{1,0:T(8,128)(2,1)S(1)}, u32[]{:S(2)}, u32[]{:S(2)}) collective-permute-start(bf16[104,832]{1,0:T(8,128)(2,1)S(1)} %constant_dynamic-slice_fusion), channel_id=1, source_target_pairs={{0,8},{8,16},{16,24},{24,0},{32,40},{40,48},{48,56},{56,32},{64,72... | collective-permute-start | bytes 519176 | tf_op jit(solution)/shard_map/ppermute | solution.py:83
  29.0 40.6 %collective-permute-start.12 = (bf16[4,104,832]{2,1,0:T(8,128)(2,1)S(1)}, bf16[4,104,832]{2,1,0:T(8,128)(2,1)S(1)}, u32[]{:S(2)}, u32[]{:S(2)}) collective-permute-start(bf16[4,104,832]{2,1,0:T(8,128)(2,1)S(1)} %get-tuple-element.297), channel_id=1, source_target_pairs={{0,96},{8,104},{16,112},{24,120},{32,0},{40,8},{48,16},{56,24},{64... | collective-permute-start | bytes 2076680 | tf_op jit(solution)/shard_map/ppermute | solution.py:84
  32.3 37.5 %collective-permute-start.11 = (bf16[4,104,832]{2,1,0:T(8,128)(2,1)S(1)}, bf16[4,104,832]{2,1,0:T(8,128)(2,1)S(1)}, u32[]{:S(2)}, u32[]{:S(2)}) collective-permute-start(bf16[4,104,832]{2,1,0:T(8,128)(2,1)S(1)} %get-tuple-element.297), channel_id=1, source_target_pairs={{0,64},{8,72},{16,80},{24,88},{32,96},{40,104},{48,112},{56,120},{... | collective-permute-start | bytes 2076680 | tf_op jit(solution)/shard_map/ppermute | solution.py:84
  34.7 42.3 %collective-permute-start.10 = (bf16[4,104,832]{2,1,0:T(8,128)(2,1)S(1)}, bf16[4,104,832]{2,1,0:T(8,128)(2,1)S(1)}, u32[]{:S(2)}, u32[]{:S(2)}) collective-permute-start(bf16[4,104,832]{2,1,0:T(8,128)(2,1)S(1)} %get-tuple-element.297), channel_id=1, source_target_pairs={{0,32},{8,40},{16,48},{24,56},{32,64},{40,72},{48,80},{56,88},{64,... | collective-permute-start | bytes 2076680 | tf_op jit(solution)/shard_map/ppermute | solution.py:84
  39.6 63.6 %collective-permute-start.5 = (bf16[4,104,832]{2,1,0:T(8,128)(2,1)S(1)}, bf16[4,104,832]{2,1,0:T(8,128)(2,1)}, u32[]{:S(2)}, u32[]{:S(2)}) collective-permute-start(bf16[4,104,832]{2,1,0:T(8,128)(2,1)S(1)} %get-tuple-element.299), channel_id=1, source_target_pairs={{0,96},{8,104},{16,112},{24,120},{32,0},{40,8},{48,16},{56,24},{64... | collective-permute-start | bytes 2076680 | tf_op jit(solution)/shard_map/ppermute | solution.py:84
  42.8 64.2 %collective-permute-start.4 = (bf16[4,104,832]{2,1,0:T(8,128)(2,1)S(1)}, bf16[4,104,832]{2,1,0:T(8,128)(2,1)}, u32[]{:S(2)}, u32[]{:S(2)}) collective-permute-start(bf16[4,104,832]{2,1,0:T(8,128)(2,1)S(1)} %get-tuple-element.299), channel_id=1, source_target_pairs={{0,64},{8,72},{16,80},{24,88},{32,96},{40,104},{48,112},{56,120},{... | collective-permute-start | bytes 2076680 | tf_op jit(solution)/shard_map/ppermute | solution.py:84
  69.7 58.0 %collective-permute-start.3 = (bf16[4,104,832]{2,1,0:T(8,128)(2,1)S(1)}, bf16[4,104,832]{2,1,0:T(8,128)(2,1)}, u32[]{:S(2)}, u32[]{:S(2)}) collective-permute-start(bf16[4,104,832]{2,1,0:T(8,128)(2,1)S(1)} %get-tuple-element.299), channel_id=1, source_target_pairs={{0,32},{8,40},{16,48},{24,56},{32,64},{40,72},{48,80},{56,88},{64,... | collective-permute-start | bytes 2076680 | tf_op jit(solution)/shard_map/ppermute | solution.py:84
  156.6 5.4 %copy-start.9 = (bf16[3,1664,104]{1,2,0:T(8,128)(2,1)S(1)}, bf16[3,1664,104]{1,2,0:T(8,128)(2,1)}, u32[]{:S(2)}) copy-start(bf16[3,1664,104]{1,2,0:T(8,128)(2,1)} %param.24) | copy-start | bytes 3115012
  162.0 43.4 %collective-permute-start.6 = (bf16[1664,832]{0,1:T(8,128)(2,1)}, bf16[1664,832]{0,1:T(8,128)(2,1)}, u32[]{:S(2)}, u32[]{:S(2)}) collective-permute-start(bf16[1664,832]{0,1:T(8,128)(2,1)} %copy.71), channel_id=1, source_target_pairs={{0,1},{1,0},{2,3},{3,2},{4,5},{5,4},{6,7},{7,6},{8,9},{9,8},{10,11... | collective-permute-start | bytes 8306696 | tf_op jit(solution)/shard_map/ppermute | solution.py:96
  186.0 16.9 %all-to-all-start = ((bf16[16,128,104]{1,2,0:T(8,128)(2,1)}), bf16[16,128,104]{1,2,0:T(8,128)(2,1)S(1)}, u32[]{:S(2)}, u32[]{:S(2)}) async-start(bf16[16,128,104]{1,2,0:T(8,128)(2,1)} %copy.69), calls=%async_computation | async-start | bytes 851968 | tf_op jit(solution)/shard_map/all_to_all | solution.py:67
  191.7 110.5 %reduce-scatter.2.cloned.1.call-start = ((), (), s32[]{:S(2)}) async-start(), calls=%async_computation.6 | async-start | bytes 3620864 | tf_op jit(solution)/shard_map/reduce_scatter | solution.py:156
  205.4 2.9 copy-start.2
  205.4 3.4 copy-start.6
  226.9 0.7 copy-start.8
  226.9 81.7 %copy-start.11 = (s32[1,1,128]{2,1,0:T(1,128)S(1)}, s32[1,1,128]{2,1,0:T(1,128)}, u32[]{:S(2)}) copy-start(s32[1,1,128]{2,1,0:T(1,128)} %param.30) | copy-start | bytes 1540
  226.9 91.1 %copy-start.3 = (bf16[128,1664]{1,0:T(8,128)(2,1)S(1)}, bf16[128,1664]{1,0:T(8,128)(2,1)}, u32[]{:S(2)}) copy-start(bf16[128,1664]{1,0:T(8,128)(2,1)} %param.32) | copy-start | bytes 1277956
  226.9 91.6 %copy-start.7 = (f32[1664]{0:T(1024)S(1)}, f32[1664]{0:T(1024)}, u32[]{:S(2)}) copy-start(f32[1664]{0:T(1024)} %param.33) | copy-start | bytes 19972
  304.2 13.7 %all-to-all-start.2 = ((bf16[8,9,1664]{2,1,0:T(8,128)(2,1)}), bf16[8,9,1664]{2,1,0:T(8,128)(2,1)S(1)}, u32[]{:S(2)}, u32[]{:S(2)}) async-start(bf16[8,9,1664]{2,1,0:T(8,128)(2,1)} %pad_maximum_fusion.4), calls=%async_computation.3 | async-start | bytes 851968 | tf_op jit(solution)/shard_map/all_to_all | solution.py:176
  308.6 72.0 %all-gather.5.cloned.1.call-start = ((), (), s32[]{:S(2)}) async-start(), calls=%async_computation.7 | async-start | bytes 7241728 | tf_op jit(solution)/shard_map/all_gather | solution.py:195
  323.3 57.3 %copy-start.10 = (bf16[3,1664,104]{1,2,0:T(8,128)(2,1)S(1)}, bf16[3,1664,104]{1,2,0:T(8,128)(2,1)}, u32[]{:S(2)}) copy-start(bf16[3,1664,104]{1,2,0:T(8,128)(2,1)} %param.34) | copy-start | bytes 3115012
  328.7 97.3 %collective-permute-start.13 = (bf16[1664,832]{0,1:T(8,128)(2,1)}, bf16[1664,832]{0,1:T(8,128)(2,1)}, u32[]{:S(2)}, u32[]{:S(2)}) collective-permute-start(bf16[1664,832]{0,1:T(8,128)(2,1)} %copy.82), channel_id=1, source_target_pairs={{0,1},{1,0},{2,3},{3,2},{4,5},{5,4},{6,7},{7,6},{8,9},{9,8},{10,11... | collective-permute-start | bytes 8306696 | tf_op jit(solution)/shard_map/ppermute | solution.py:96
  423.4 6.5 %copy-start.1 = (bf16[416,1664]{1,0:T(8,128)(2,1)S(1)}, bf16[416,1664]{1,0:T(8,128)(2,1)}, u32[]{:S(2)}) copy-start(bf16[416,1664]{1,0:T(8,128)(2,1)} %param.27) | copy-start | bytes 4153348
Sparse Core Ops, SparseCore 0:
  11.3 119.9 all-gather.2
  227.1 75.0 reduce-scatter.1
  319.6 60.8 all-gather.4

commit v4 on v1

--- a/solution.py
+++ b/solution.py
@@ -87,10 +87,18 @@
     token_count = patches.shape[0]
     model_width = patches.shape[1]
     group_patches = token_count * seq_count
-    vis_out_full = lax.all_gather(vis_out, "seq", axis=0, tiled=True)
-    txt_out_full = lax.all_gather(txt_out, "seq", axis=0, tiled=True)
     vis_normed = layer_norm(patches, vis_gain).astype(jnp.bfloat16)
-    vis_proj = projector(vis_qkv, lax.all_gather(vis_normed, "seq", axis=0, tiled=True))
+    weight_rows = vis_out.shape[0]
+    padded_rows = -(-weight_rows // 16) * 16
+    pad = ((0, padded_rows - weight_rows), (0, 0))
+    bundle = jnp.concatenate([vis_normed, jnp.pad(vis_out, pad), jnp.pad(txt_out, pad)], axis=0)
+    bundle = lax.all_gather(bundle, "seq", axis=0, tiled=False)
+    vis_gathered = bundle[:, :token_count].reshape(group_patches, model_width)
+    vis_out_full = bundle[:, token_count : token_count + weight_rows].reshape(-1, model_width)
+    txt_out_full = bundle[:, token_count + padded_rows : token_count + padded_rows + weight_rows].reshape(
+        -1, model_width
+    )
+    vis_proj = projector(vis_qkv, vis_gathered)
     bounds = jnp.cumsum(image_blocks[0])[:-1]
 
     def segment(indices):
@@ -132,10 +140,12 @@
         "gct,td->gcd", selector, visual, preferred_element_type=jnp.float32
     ).astype(jnp.bfloat16)
     arrived_flags = jnp.sum(selector.astype(jnp.float32), axis=2).astype(jnp.bfloat16)
-    incoming, arrived = (
-        lax.all_to_all(outgoing, "grp", split_axis=0, concat_axis=0, tiled=True),
-        lax.all_to_all(arrived_flags, "grp", split_axis=0, concat_axis=0, tiled=True),
+    flag_row = jnp.pad(arrived_flags, ((0, 0), (0, model_width - capacity)))[:, None, :]
+    payload = lax.all_to_all(
+        jnp.concatenate([outgoing, flag_row], axis=1), "grp", split_axis=0, concat_axis=0, tiled=True
     )
+    incoming = payload[:, :capacity, :]
+    arrived = payload[:, capacity, :capacity]
     prompt_rows = text_emb.shape[0]
     slot_targets = slot_rows[0, 0, : groups * capacity]
     placement_map = (

time: 389 us -> 405 us (1.041)
  blocking collectives: 15.7 us -> 44.3 us
  starting transfers between devices: 19.6 us -> 4.69 us
  waiting for transfers between devices: 258 us -> 268 us
  matrix products: 47.6 us -> 39.1 us
    all_to_all x0 -> x2, blocking collectives: none -> 30.8 us  [heads_to_rows(): lax.all_to_all(blocks, 'seq', split_axis=0, concat_axis=0, tiled=True)]
    all_to_all x4 -> x1, starting transfers between devices: 19.3 us -> 4.43 us  [per_device(): lax.all_to_all(jnp.concatenate([outgoing, flag_row], axis=1), 'grp', spli...]
    reduce_scatter x1, waiting for transfers between devices: 63.9 us -> 74.1 us  [per_device(): lax.psum_scatter(jnp.dot(picked, merge_w, preferred_element_type=jnp.floa...]
    dot_general x8, matrix products: 14.2 us -> 9.85 us  [one_block(): jnp.einsum('qhe,khe->hqk', query_part, key_heads, preferred_element_type=...]
    all_gather x3 -> x1, waiting for transfers between devices: 120 us -> 123 us  [per_device(): bundle = lax.all_gather(bundle, 'seq', axis=0, tiled=False)]
    all_to_all x4 -> x1, waiting for transfers between devices: 12.1 us -> 9.02 us  [per_device(): lax.all_to_all(jnp.concatenate([outgoing, flag_row], axis=1), 'grp', spli...]
  transfers between devices with their start and end apart: 9 -> 4, of which waited for: 7 -> 4; matrix products, arithmetic and copies ran while one was open for 16% -> 0% of each run, Pallas kernels for 0% -> 0%
where the time goes in v4:
time: 405 us; the launch traced here: 404 us
  waiting for transfers between devices  268 us (66%)
  blocking collectives  44.3 us (11%)
  matrix products  39.1 us (10%)
  other arithmetic  23.1 us (6%)
  between operations  13.4 us (3%)
  local copies, waits for them, and re-layouts  11.7 us (3%)
  starting transfers between devices  4.69 us (1%)
    all_gather x1, waiting for transfers between devices, per_device(): bundle = lax.all_gather(bundle, 'seq', axis=0, tiled=False)  123 us
    reduce_scatter x1, waiting for transfers between devices, per_device(): lax.psum_scatter(jnp.dot(picked, merge_w, preferred_element_type=jnp.floa...  74.1 us
    all_gather x1, waiting for transfers between devices, per_device(): lax.all_gather(txt_normed, 'seq', axis=0, tiled=True)  61.1 us
    all_to_all x2, blocking collectives, heads_to_rows(): lax.all_to_all(blocks, 'seq', split_axis=0, concat_axis=0, tiled=True)  30.8 us
    all_to_all x1, blocking collectives, per_device(): lax.all_to_all(merged_in, 'seq', split_axis=1, concat_axis=0, tiled=True)  13.5 us
    dot_general x8, matrix products, one_block(): jnp.einsum('qhe,khe->hqk', query_part, key_heads, preferred_element_type=...  9.85 us
    all_to_all x1, waiting for transfers between devices, per_device(): lax.all_to_all(jnp.concatenate([outgoing, flag_row], axis=1), 'grp', spli...  9.02 us
    dot_general x8, matrix products, one_block(): jnp.einsum('hqk,khe->qhe', probabilities, value_heads, preferred_element_...  8.62 us
  transfers between devices with their start and end apart: 4, of which 4 were waited for; matrix products, arithmetic and copies ran while one was open for 0% of the time, Pallas kernels for 0%

profile of v4, /device:TPU:0, one launch (start us, length us, event | category | flops | bytes accessed | tf_op | source)
XLA Modules:
  0.0 404.2 jit_solution(3875613882730612158)
XLA Ops:
  6.5 1.3 convert_reduce_fusion.1
  7.8 1.3 fusion.51
  9.1 1.3 fusion.53
  10.4 2.2 fusion.48
  13.0 123.4 %all-gather.6.cloned.1.call-done = bf16[5632,1664]{1,0:T(8,128)(2,1)} async-done(((bf16[352,1664]{1,0:T(8,128)(2,1)}), bf16[5632,1664]{1,0:T(8,128)(2,1)}) %all-gather.6.cloned.1.call-update) | async-done | bytes 18743312 | tf_op jit(solution)/shard_map/all_gather | solution.py:95
  136.4 3.7 slice.56
  140.1 2.5 fusion.75
  143.3 16.6 %while.24 = (s32[]{:T(128)}, bf16[4,512,1,104]{1,3,2,0:T(8,128)(2,1)S(1)}, s32[4]{0:T(128)S(1)}, s32[3]{0:T(128)S(1)}, s32[2048]{0:T(1024)S(1)}, /*index=5*/bf16...) while((s32[]{:T(128)}, ...), condition=%wide.region_10.11_spmd, body=%wide.region_6.10_spmd.sunk | while | flops 445709312 | bytes 13674625 | solution.py:57
  143.4 0.6 dynamic_slice.41
  144.0 0.6 add_select_fusion.3
  144.7 1.0 fusion.93
  145.7 0.7 fusion.94
  146.4 1.1 fusion.95
  147.5 0.6 dynamic_slice.41
  148.1 0.6 add_select_fusion.3
  148.9 1.0 fusion.93
  149.8 0.7 fusion.94
  150.6 1.1 fusion.95
  151.7 0.6 dynamic_slice.41
  152.3 0.6 add_select_fusion.3
  153.0 1.0 fusion.93
  154.0 0.7 fusion.94
  154.7 1.1 fusion.95
  155.8 0.6 dynamic_slice.41
  156.4 0.6 add_select_fusion.3
  157.2 1.0 fusion.93
  158.2 0.7 fusion.94
  158.9 1.1 fusion.95
  160.5 15.3 %all_to_all.34 = bf16[16,128,104]{1,2,0:T(8,128)(2,1)S(1)} all-to-all(bf16[16,128,104]{1,2,0:T(8,128)(2,1)S(1)} %copy.31), channel_id=1, replica_groups=mesh['seq'=16,'grp'=8] {'seq'}, dimensions={0} | all-to-all | bytes 851968 | tf_op jit(solution)/shard_map/all_to_all | solution.py:65
  175.8 3.7 fusion.74
  180.0 0.6 all_to_all.24
  180.9 13.5 %all_to_all.35 = bf16[32,16,416]{2,0,1:T(8,128)(2,1)S(1)} all-to-all(bf16[32,16,416]{2,0,1:T(8,128)(2,1)S(1)} %copy.32), channel_id=1, replica_groups=mesh['seq'=16,'grp'=8] {'seq'}, dimensions={1} | all-to-all | bytes 851968 | tf_op jit(solution)/shard_map/all_to_all | solution.py:122
  194.4 2.9 fusion.76
  197.8 74.1 %reduce-scatter.2.cloned.1.call-done = f32[32,1664]{1,0:T(8,128)} async-done(((f32[512,1664]{1,0:T(8,128)}), f32[32,1664]{1,0:T(8,128)}) %reduce-scatter.2.cloned.1.call-update) | async-done | bytes 213008 | tf_op jit(solution)/shard_map/reduce_scatter | solution.py:124
  271.8 1.1 convolution_convert_fusion
  273.0 0.8 pad_maximum_fusion
  273.8 4.4 %all-to-all-start.2 = ((bf16[8,9,1664]{2,1,0:T(8,128)(2,1)}), bf16[8,9,1664]{2,1,0:T(8,128)(2,1)S(1)}, u32[]{:S(2)}, u32[]{:S(2)}) async-start(bf16[8,9,1664]{2,1,0:T(8,128)(2,1)} %pad_maximum_fusion), calls=%async_computation.3 | async-start | bytes 851968 | tf_op jit(solution)/shard_map/all_to_all | solution.py:144
  278.5 9.0 %all-to-all-done.2 = bf16[8,9,1664]{2,1,0:T(8,128)(2,1)S(1)} async-done(((bf16[8,9,1664]{2,1,0:T(8,128)(2,1)}), bf16[8,9,1664]{2,1,0:T(8,128)(2,1)S(1)}, u32[]{:S(2)}, u32[]{:S(2)}) %all-to-all-start.2) | async-done | bytes 239648 | tf_op jit(solution)/shard_map/all_to_all | solution.py:144
  288.2 0.9 multiply_convert_fusion
  289.1 61.1 %all-gather.4.cloned.1.call-done = bf16[2048,1664]{1,0:T(8,128)(2,1)} async-done(((bf16[128,1664]{1,0:T(8,128)(2,1)}), bf16[2048,1664]{1,0:T(8,128)(2,1)}) %all-gather.4.cloned.1.call-update) | async-done | bytes 6815760 | tf_op jit(solution)/shard_map/all_gather | solution.py:163
  350.2 5.5 %fusion.77 = f32[2048,312]{0,1:S(1)} fusion(bf16[2048,1664]{1,0:T(8,128)(2,1)} %all-gather.4.cloned.1.call-done, bf16[1664,312]{0,1:T(8,128)(2,1)S(1)} %bitcast.151), kind=kOutput, calls=%fused_computation.125 | convolution fusion | flops 2126512128 | bytes 10409984
  356.4 20.7 %while.25 = (s32[]{:T(128)}, bf16[4,512,1,104]{1,3,2,0:T(8,128)(2,1)S(1)}, s32[4]{0:T(128)S(1)}, s32[]{:T(128)}, bf16[4,512,1,104]{1,3,2,0:T(8,128)(2,1)S(1)}, /...) while((s32[]{:T(128)}, ...), condition=%wide.region_20.21_spmd.clone.clone, body=%wide.region_17.20_spmd.clone.clone.sunk | while | flops 446748160 | bytes 13666417 | solution.py:57
  357.0 0.6 iota_add_fusion.3
  357.7 0.7 iota_compare_fusion.10
  358.4 1.5 fusion.97
  359.8 0.7 fusion.98
  360.6 1.1 fusion.99
  362.2 0.6 iota_add_fusion.3
  362.9 0.7 iota_compare_fusion.10
  363.5 1.5 fusion.97
  365.0 0.7 fusion.98
  365.7 1.1 fusion.99
  367.4 0.6 iota_add_fusion.3
  368.1 0.7 iota_compare_fusion.10
  368.7 1.5 fusion.97
  370.2 0.7 fusion.98
  370.9 1.1 fusion.99
  372.6 0.6 iota_add_fusion.3
  373.3 0.7 iota_compare_fusion.10
  373.9 1.5 fusion.97
  375.4 0.7 fusion.98
  376.1 1.1 fusion.99
  377.7 15.4 %all_to_all.36 = bf16[16,128,104]{1,2,0:T(8,128)(2,1)S(1)} all-to-all(bf16[16,128,104]{1,2,0:T(8,128)(2,1)S(1)} %copy.36), channel_id=1, replica_groups=mesh['seq'=16,'grp'=8] {'seq'}, dimensions={0} | all-to-all | bytes 851968 | tf_op jit(solution)/shard_map/all_to_all | solution.py:65
  393.2 4.5 %fusion.36 = f32[128,1664]{1,0:T(8,128)} fusion(f32[128,1664]{1,0:T(8,128)S(1)} %get-tuple-element.278, bf16[16,352,1664]{2,1,0:T(8,128)(2,1)} %bitcast.142, bf16[16,128,104]{1,2,0:T(8,128)(2,1)S(1)} %all_to_all.36), kind=kOutput, calls=%fused_computation.50 | convolution fusion | flops 709050368 | bytes 7667712 | tf_op jit(solution)/shard_map/dot_general | solution.py:171
  (78 shorter events, 7.6 us)
Async XLA Ops:
  6.5 187.8 %copy-start = (bf16[416,1664]{1,0:T(8,128)(2,1)S(1)}, bf16[416,1664]{1,0:T(8,128)(2,1)}, u32[]{:S(2)}) copy-start(bf16[416,1664]{1,0:T(8,128)(2,1)} %param.23) | copy-start | bytes 4153348
  6.5 6.1 %copy-start.9 = (s32[1,4]{1,0:T(1,128)S(1)}, s32[1,4]{1,0:T(1,128)}, u32[]{:S(2)}) copy-start(s32[1,4]{1,0:T(1,128)} %param.24) | copy-start | bytes 52
  6.5 129.9 %all-gather.6.cloned.1.call-start = ((), (), s32[]{:S(2)}) async-start(), calls=%async_computation.7 | async-start | bytes 19914752 | tf_op jit(solution)/shard_map/all_gather | solution.py:95
  12.6 259.2 %reduce-scatter.2.cloned.1.call-start = ((), (), s32[]{:S(2)}) async-start(), calls=%async_computation.5 | async-start | bytes 3620864 | tf_op jit(solution)/shard_map/reduce_scatter | solution.py:124
  136.4 3.7 copy-start.7
  143.3 32.5 %copy-start.2 = (bf16[128,1664]{1,0:T(8,128)(2,1)S(1)}, bf16[128,1664]{1,0:T(8,128)(2,1)}, u32[]{:S(2)}) copy-start(bf16[128,1664]{1,0:T(8,128)(2,1)} %param.18) | copy-start | bytes 1277956
  175.8 4.0 copy-start.4
  194.4 2.9 copy-start.6
  197.2 81.2 %copy-start.10 = (s32[1,1,128]{2,1,0:T(1,128)S(1)}, s32[1,1,128]{2,1,0:T(1,128)}, u32[]{:S(2)}) copy-start(s32[1,1,128]{2,1,0:T(1,128)} %param.26) | copy-start | bytes 1540
  197.2 90.5 %copy-start.3 = (bf16[128,1664]{1,0:T(8,128)(2,1)S(1)}, bf16[128,1664]{1,0:T(8,128)(2,1)}, u32[]{:S(2)}) copy-start(bf16[128,1664]{1,0:T(8,128)(2,1)} %param.28) | copy-start | bytes 1277956
  197.2 91.0 %copy-start.5 = (f32[1664]{0:T(1024)S(1)}, f32[1664]{0:T(1024)}, u32[]{:S(2)}) copy-start(f32[1664]{0:T(1024)} %param.29) | copy-start | bytes 19972
  197.2 153.0 %copy-start.8 = (bf16[3,1664,104]{1,2,0:T(8,128)(2,1)S(1)}, bf16[3,1664,104]{1,2,0:T(8,128)(2,1)}, u32[]{:S(2)}) copy-start(bf16[3,1664,104]{1,2,0:T(8,128)(2,1)} %param.30) | copy-start | bytes 3115012
  273.8 13.7 %all-to-all-start.2 = ((bf16[8,9,1664]{2,1,0:T(8,128)(2,1)}), bf16[8,9,1664]{2,1,0:T(8,128)(2,1)S(1)}, u32[]{:S(2)}, u32[]{:S(2)}) async-start(bf16[8,9,1664]{2,1,0:T(8,128)(2,1)} %pad_maximum_fusion), calls=%async_computation.3 | async-start | bytes 851968 | tf_op jit(solution)/shard_map/all_to_all | solution.py:144
  278.2 72.0 %all-gather.4.cloned.1.call-start = ((), (), s32[]{:S(2)}) async-start(), calls=%async_computation.6 | async-start | bytes 7241728 | tf_op jit(solution)/shard_map/all_gather | solution.py:163
  377.6 20.1 %copy-start.1 = (bf16[416,1664]{1,0:T(8,128)(2,1)S(1)}, bf16[416,1664]{1,0:T(8,128)(2,1)}, u32[]{:S(2)}) copy-start(bf16[416,1664]{1,0:T(8,128)(2,1)} %param.23) | copy-start | bytes 4153348
Sparse Core Ops, SparseCore 0:
  12.8 123.5 all-gather.5
  197.4 74.3 reduce-scatter.1
  289.3 60.9 all-gather.3

commit v5 on v1

--- a/solution.py
+++ b/solution.py
@@ -88,7 +88,6 @@
     model_width = patches.shape[1]
     group_patches = token_count * seq_count
     vis_out_full = lax.all_gather(vis_out, "seq", axis=0, tiled=True)
-    txt_out_full = lax.all_gather(txt_out, "seq", axis=0, tiled=True)
     vis_normed = layer_norm(patches, vis_gain).astype(jnp.bfloat16)
     vis_proj = projector(vis_qkv, lax.all_gather(vis_normed, "seq", axis=0, tiled=True))
     bounds = jnp.cumsum(image_blocks[0])[:-1]
@@ -102,6 +101,8 @@
         return segment(row_indices)[:, None] == key_segments[None, :]
 
     vis_heads = attend_local(vis_proj[0], vis_proj[1], vis_proj[2], vis_allowed)
+    vis_heads, txt_out = lax.optimization_barrier((vis_heads, txt_out))
+    txt_out_full = lax.all_gather(txt_out, "seq", axis=0, tiled=True)
     vis_attn = jnp.dot(
         heads_to_rows(vis_heads, seq_count), vis_out_full, preferred_element_type=jnp.float32
     )
@@ -112,13 +113,11 @@
         .reshape(token_count // 4, 4 * model_width)
     )
     feature_slices = lax.all_to_all(merged_in, "seq", split_axis=1, concat_axis=0, tiled=True)
-    picked = feature_slices
-    visual = lax.psum_scatter(
-        jnp.dot(picked, merge_w, preferred_element_type=jnp.float32),
-        "seq",
-        scatter_dimension=0,
-        tiled=True,
-    ).astype(jnp.bfloat16)
+    merge_partial = jnp.dot(feature_slices, merge_w, preferred_element_type=jnp.float32)
+    merge_parts = lax.all_to_all(
+        merge_partial.reshape(seq_count, -1, model_width), "seq", split_axis=0, concat_axis=0, tiled=True
+    )
+    visual = jnp.sum(merge_parts, axis=0).astype(jnp.bfloat16)
     dest_rows = dest_group[:, 0]
     merged_rows = dest_rows.shape[0]
     capacity = max(2, 2 * merged_rows // groups)
@@ -132,10 +131,12 @@
         "gct,td->gcd", selector, visual, preferred_element_type=jnp.float32
     ).astype(jnp.bfloat16)
     arrived_flags = jnp.sum(selector.astype(jnp.float32), axis=2).astype(jnp.bfloat16)
-    incoming, arrived = (
-        lax.all_to_all(outgoing, "grp", split_axis=0, concat_axis=0, tiled=True),
-        lax.all_to_all(arrived_flags, "grp", split_axis=0, concat_axis=0, tiled=True),
+    flag_row = jnp.pad(arrived_flags, ((0, 0), (0, model_width - capacity)))[:, None, :]
+    payload = lax.all_to_all(
+        jnp.concatenate([outgoing, flag_row], axis=1), "grp", split_axis=0, concat_axis=0, tiled=True
     )
+    incoming = payload[:, :capacity, :]
+    arrived = payload[:, capacity, :capacity]
     prompt_rows = text_emb.shape[0]
     slot_targets = slot_rows[0, 0, : groups * capacity]
     placement_map = (
@@ -150,6 +151,7 @@
     )
     hidden = (text_emb.astype(jnp.float32) * (1.0 - replaced) + placed).astype(jnp.bfloat16)
     txt_normed = rms_norm(hidden, txt_gain).astype(jnp.bfloat16)
+    txt_normed, txt_out_full = lax.optimization_barrier((txt_normed, txt_out_full))
     txt_proj = projector(txt_qkv, lax.all_gather(txt_normed, "seq", axis=0, tiled=True))
     length = prompt_len[0]
     key_positions = jnp.arange(prompt_rows * seq_count, dtype=jnp.int32)

time: 389 us -> 365 us (0.938)
  waiting for transfers between devices: 258 us -> 228 us
  blocking collectives: 15.7 us -> 34.3 us
  starting transfers between devices: 19.6 us -> 13.7 us
  matrix products: 47.6 us -> 42.2 us
    reduce_scatter x1 -> x0, waiting for transfers between devices: 63.9 us -> none  [per_device(): lax.psum_scatter(jnp.dot(picked, merge_w, preferred_element_type=jnp.floa...]
    all_to_all x2, waiting for transfers between devices: 12.1 us -> 72.2 us  [the longest x1 63.2 us: per_device(): lax.all_to_all(merge_partial.reshape(seq_count, -1, model_width), 'seq',...]
    all_gather x1, waiting for transfers between devices: 23.8 us -> 0.01 us  [per_device(): txt_out_full = lax.all_gather(txt_out, 'seq', axis=0, tiled=True)]
    all_to_all x0 -> x1, blocking collectives: none -> 15.5 us  [heads_to_rows(): lax.all_to_all(blocks, 'seq', split_axis=0, concat_axis=0, tiled=True)]
    all_to_all x2 -> x1, starting transfers between devices: 10.5 us -> 5.25 us  [heads_to_rows(): lax.all_to_all(blocks, 'seq', split_axis=0, concat_axis=0, tiled=True)]
    dot_general x8, matrix products: 14.2 us -> 9.87 us  [one_block(): jnp.einsum('qhe,khe->hqk', query_part, key_heads, preferred_element_type=...]
  transfers between devices with their start and end apart: 9 -> 7, of which waited for: 7 -> 5; matrix products, arithmetic and copies ran while one was open for 16% -> 10% of each run, Pallas kernels for 0% -> 0%
where the time goes in v5:
time: 365 us; the launch traced here: 364 us
  waiting for transfers between devices  228 us (62%)
  matrix products  42.2 us (12%)
  blocking collectives  34.3 us (9%)
  other arithmetic  23.5 us (6%)
  starting transfers between devices  13.7 us (4%)
  between operations  13.4 us (4%)
  local copies, waits for them, and re-layouts  9.11 us (2%)
    all_gather x1, waiting for transfers between devices, per_device(): lax.all_gather(vis_normed, 'seq', axis=0, tiled=True)  64.5 us
    all_to_all x1, waiting for transfers between devices, per_device(): lax.all_to_all(merge_partial.reshape(seq_count, -1, model_width), 'seq',...  63.2 us
    all_gather x1, waiting for transfers between devices, per_device(): lax.all_gather(txt_normed, 'seq', axis=0, tiled=True)  58.5 us
    all_gather x1, waiting for transfers between devices, per_device(): vis_out_full = lax.all_gather(vis_out, 'seq', axis=0, tiled=True)  31.9 us
    all_to_all x1, blocking collectives, per_device(): lax.all_to_all(merged_in, 'seq', split_axis=1, concat_axis=0, tiled=True)  18.9 us
    all_to_all x1, blocking collectives, heads_to_rows(): lax.all_to_all(blocks, 'seq', split_axis=0, concat_axis=0, tiled=True)  15.5 us
    unnamed x2, matrix products  11.1 us
    dot_general x8, matrix products, one_block(): jnp.einsum('qhe,khe->hqk', query_part, key_heads, preferred_element_type=...  9.87 us
  transfers between devices with their start and end apart: 7, of which 5 were waited for; matrix products, arithmetic and copies ran while one was open for 10% of the time, Pallas kernels for 0%

profile of v5, /device:TPU:0, one launch (start us, length us, event | category | flops | bytes accessed | tf_op | source)
XLA Modules:
  0.0 364.3 jit_solution(9718671733893464787)
XLA Ops:
  6.5 1.3 convert_reduce_fusion.1
  7.8 1.3 fusion.32
  9.1 2.1 fusion.34
  11.2 0.7 all-gather.7.cloned.1.call-update
  12.0 0.8 reduce-window.4
  12.9 64.5 %all-gather.5.cloned.1.call-done = bf16[2048,1664]{1,0:T(8,128)(2,1)} async-done(((bf16[128,1664]{1,0:T(8,128)(2,1)}), bf16[2048,1664]{1,0:T(8,128)(2,1)}) %all-gather.5.cloned.1.call-update) | async-done | bytes 6815760 | tf_op jit(solution)/shard_map/all_gather | solution.py:92
  77.4 5.7 %fusion.55 = f32[2048,312]{0,1:S(1)} fusion(bf16[2048,1664]{1,0:T(8,128)(2,1)} %all-gather.5.cloned.1.call-done, bf16[1664,312]{0,1:T(8,128)(2,1)} %bitcast.150), kind=kOutput, calls=%fused_computation.111 | convolution fusion | flops 2126512128 | bytes 10409984
  83.8 16.5 %while.24 = (s32[]{:T(128)}, bf16[4,512,1,104]{1,3,2,0:T(8,128)(2,1)S(1)}, s32[4]{0:T(128)S(1)}, s32[3]{0:T(128)S(1)}, s32[2048]{0:T(1024)S(1)}, /*index=5*/bf16...) while((s32[]{:T(128)}, ...), condition=%wide.region_10.11_spmd, body=%wide.region_6.10_spmd.sunk | while | flops 445709312 | bytes 13674625 | solution.py:57
  84.4 0.7 add_select_fusion.3
  85.2 1.0 fusion.75
  86.2 0.7 fusion.76
  86.9 1.1 fusion.77
  88.5 0.7 add_select_fusion.3
  89.3 1.0 fusion.75
  90.3 0.7 fusion.76
  91.0 1.1 fusion.77
  92.7 0.7 add_select_fusion.3
  93.4 1.0 fusion.75
  94.4 0.7 fusion.76
  95.1 1.1 fusion.77
  96.8 0.7 add_select_fusion.3
  97.5 1.0 fusion.75
  98.5 0.7 fusion.76
  99.2 1.1 fusion.77
  100.6 0.8 copy_bitcast_fusion
  101.5 5.2 %all-to-all-start = ((bf16[16,128,104]{1,2,0:T(8,128)(2,1)}), bf16[16,128,104]{1,2,0:T(8,128)(2,1)S(1)}, u32[]{:S(2)}, u32[]{:S(2)}) async-start(bf16[16,128,104]{1,2,0:T(8,128)(2,1)} %copy_bitcast_fusion), calls=%async_computation | async-start | bytes 851968 | tf_op jit(solution)/shard_map/all_to_all | solution.py:65
  106.7 31.9 %all-gather.7.cloned.1.call-done = bf16[1664,1664]{1,0:T(8,128)(2,1)} async-done(((bf16[104,1664]{1,0:T(8,128)(2,1)}), bf16[1664,1664]{1,0:T(8,128)(2,1)}) %all-gather.7.cloned.1.call-update) | async-done | bytes 5537808 | tf_op jit(solution)/shard_map/all_gather | solution.py:90
  138.6 3.7 %fusion.54 = (f32[128]{0:T(128)S(1)}, f32[128,1664]{1,0:T(8,128)S(1)}) fusion(bf16[128,1664]{0,1:T(8,128)(2,1)S(1)} %bitcast.143, bf16[1664,1664]{1,0:T(8,128)(2,1)} %all-gather.7.cloned.1.call-done, bf16[128,1664]{1,0:T(8,128)(2,1)S(1)} %copy-done.2), kind=kOutput, calls=%fused_computation.110 | convolution fusion | flops 709476224 | bytes 7242240 | tf_op jit(solution)/shard_map/dot_general | solution.py:106
  142.8 0.6 all_to_all.25
  143.7 18.9 %all_to_all.36 = bf16[32,16,416]{2,0,1:T(8,128)(2,1)S(1)} all-to-all(bf16[32,16,416]{2,0,1:T(8,128)(2,1)S(1)} %copy.39), channel_id=1, replica_groups=mesh['seq'=16,'grp'=8] {'seq'}, dimensions={1} | all-to-all | bytes 851968 | tf_op jit(solution)/shard_map/all_to_all | solution.py:115
  162.6 2.8 fusion.28
  165.4 3.9 %all-to-all-start.2 = ((f32[16,32,1664]{2,1,0:T(8,128)}), f32[16,32,1664]{2,1,0:T(8,128)S(1)}, u32[]{:S(2)}, u32[]{:S(2)}) async-start(f32[16,32,1664]{2,1,0:T(8,128)} %fusion.28), calls=%async_computation.2 | async-start | bytes 6815744 | tf_op jit(solution)/shard_map/all_to_all | solution.py:117
  169.8 0.7 copy.40
  170.4 63.2 %all-to-all-done.2 = f32[16,32,1664]{2,1,0:T(8,128)S(1)} async-done(((f32[16,32,1664]{2,1,0:T(8,128)}), f32[16,32,1664]{2,1,0:T(8,128)S(1)}, u32[]{:S(2)}, u32[]{:S(2)}) %all-to-all-start.2) | async-done | bytes 3407904 | tf_op jit(solution)/shard_map/all_to_all | solution.py:117
  234.0 1.7 pad_maximum_fusion
  235.7 4.3 %all-to-all-start.3 = ((bf16[8,9,1664]{2,1,0:T(8,128)(2,1)}), bf16[8,9,1664]{2,1,0:T(8,128)(2,1)S(1)}, u32[]{:S(2)}, u32[]{:S(2)}) async-start(bf16[8,9,1664]{2,1,0:T(8,128)(2,1)} %pad_maximum_fusion), calls=%async_computation.3 | async-start | bytes 851968 | tf_op jit(solution)/shard_map/all_to_all | solution.py:135
  240.3 9.0 %all-to-all-done.3 = bf16[8,9,1664]{2,1,0:T(8,128)(2,1)S(1)} async-done(((bf16[8,9,1664]{2,1,0:T(8,128)(2,1)}), bf16[8,9,1664]{2,1,0:T(8,128)(2,1)S(1)}, u32[]{:S(2)}, u32[]{:S(2)}) %all-to-all-start.3) | async-done | bytes 239648 | tf_op jit(solution)/shard_map/all_to_all | solution.py:135
  249.5 1.5 multiply_reduce_fusion
  251.0 0.9 multiply_convert_fusion
  251.9 58.5 %all-gather.11.cloned.1.call-done = bf16[2048,1664]{1,0:T(8,128)(2,1)} async-done(((bf16[128,1664]{1,0:T(8,128)(2,1)}), bf16[2048,1664]{1,0:T(8,128)(2,1)}) %all-gather.11.cloned.1.call-update) | async-done | bytes 6815760 | tf_op jit(solution)/shard_map/all_gather | solution.py:155
  310.4 5.5 %fusion.56 = f32[2048,312]{0,1:S(1)} fusion(bf16[2048,1664]{1,0:T(8,128)(2,1)} %all-gather.11.cloned.1.call-done, bf16[1664,312]{0,1:T(8,128)(2,1)S(1)} %bitcast.151), kind=kOutput, calls=%fused_computation.112 | convolution fusion | flops 2126512128 | bytes 10409984
  316.6 20.7 %while.25 = (s32[]{:T(128)}, bf16[4,512,1,104]{1,3,2,0:T(8,128)(2,1)S(1)}, s32[4]{0:T(128)S(1)}, s32[]{:T(128)}, bf16[4,512,1,104]{1,3,2,0:T(8,128)(2,1)S(1)}, /...) while((s32[]{:T(128)}, ...), condition=%wide.region_20.21_spmd.clone.clone, body=%wide.region_17.20_spmd.clone.clone.sunk | while | flops 446748160 | bytes 13666417 | solution.py:57
  317.2 0.6 iota_add_fusion.3
  317.8 0.7 iota_compare_fusion.7
  318.5 1.5 fusion.79
  320.0 0.7 fusion.80
  320.7 1.1 fusion.81
  322.4 0.6 iota_add_fusion.3
  323.0 0.7 iota_compare_fusion.7
  323.7 1.5 fusion.79
  325.2 0.7 fusion.80
  325.9 1.1 fusion.81
  327.5 0.6 iota_add_fusion.3
  328.2 0.7 iota_compare_fusion.7
  328.8 1.5 fusion.79
  330.3 0.7 fusion.80
  331.0 1.1 fusion.81
  332.7 0.6 iota_add_fusion.3
  333.4 0.7 iota_compare_fusion.7
  334.0 1.5 fusion.79
  335.5 0.7 fusion.80
  336.2 1.1 fusion.81
  337.8 15.5 %all_to_all.37 = bf16[16,128,104]{1,2,0:T(8,128)(2,1)S(1)} all-to-all(bf16[16,128,104]{1,2,0:T(8,128)(2,1)S(1)} %copy.43), channel_id=1, replica_groups=mesh['seq'=16,'grp'=8] {'seq'}, dimensions={0} | all-to-all | bytes 851968 | tf_op jit(solution)/shard_map/all_to_all | solution.py:65
  353.3 4.5 %convolution_add_fusion = f32[128,1664]{1,0:T(8,128)} fusion(f32[128,1664]{1,0:T(8,128)S(1)} %get-tuple-element.301, bf16[128,1664]{0,1:T(8,128)(2,1)S(1)} %bitcast.146, bf16[1664,1664]{1,0:T(8,128)(2,1)} %all-gather.9.cloned.1.call-done), kind=kOutput, calls=%fused_computation.41 | convolution fusion | flops 709050368 | bytes 7667712 | tf_op jit(solution)/shard_map/dot_general | solution.py:163
  (77 shorter events, 9.5 us)
Async XLA Ops:
  6.5 156.1 %copy-start = (bf16[416,1664]{1,0:T(8,128)(2,1)S(1)}, bf16[416,1664]{1,0:T(8,128)(2,1)}, u32[]{:S(2)}) copy-start(bf16[416,1664]{1,0:T(8,128)(2,1)} %param.23) | copy-start | bytes 4153348
  6.5 70.8 %all-gather.5.cloned.1.call-start = ((), (), s32[]{:S(2)}) async-start(), calls=%async_computation.5 | async-start | bytes 7241728 | tf_op jit(solution)/shard_map/all_gather | solution.py:92
  11.2 127.5 %all-gather.7.cloned.1.call-start = ((), (), s32[]{:S(2)}) async-start(), calls=%async_computation.6 | async-start | bytes 5883904 | tf_op jit(solution)/shard_map/all_gather | solution.py:90
  11.9 240.0 %all-gather.9.cloned.1.call-start = ((), (), s32[]{:S(2)}) async-start(), calls=%async_computation.7 | async-start | bytes 5883904 | tf_op jit(solution)/shard_map/all_gather | solution.py:105
  83.8 54.8 %copy-start.2 = (bf16[128,1664]{1,0:T(8,128)(2,1)S(1)}, bf16[128,1664]{1,0:T(8,128)(2,1)}, u32[]{:S(2)}) copy-start(bf16[128,1664]{1,0:T(8,128)(2,1)} %param.18) | copy-start | bytes 1277956
  101.5 37.2 %all-to-all-start = ((bf16[16,128,104]{1,2,0:T(8,128)(2,1)}), bf16[16,128,104]{1,2,0:T(8,128)(2,1)S(1)}, u32[]{:S(2)}, u32[]{:S(2)}) async-start(bf16[16,128,104]{1,2,0:T(8,128)(2,1)} %copy_bitcast_fusion), calls=%async_computation | async-start | bytes 851968 | tf_op jit(solution)/shard_map/all_to_all | solution.py:65
  106.7 35.9 %copy-start.3 = (f32[1664]{0:T(1024)S(1)}, f32[1664]{0:T(1024)}, u32[]{:S(2)}) copy-start(f32[1664]{0:T(1024)} %param.22) | copy-start | bytes 19972
  165.4 3.9 %copy-start.5 = (s32[32,1]{0,1:T(1,128)S(1)}, s32[32,1]{0,1:T(1,128)}, u32[]{:S(2)}) copy-start(s32[32,1]{0,1:T(1,128)} %param.25) | copy-start | bytes 388
  165.4 68.2 %all-to-all-start.2 = ((f32[16,32,1664]{2,1,0:T(8,128)}), f32[16,32,1664]{2,1,0:T(8,128)S(1)}, u32[]{:S(2)}, u32[]{:S(2)}) async-start(f32[16,32,1664]{2,1,0:T(8,128)} %fusion.28), calls=%async_computation.2 | async-start | bytes 6815744 | tf_op jit(solution)/shard_map/all_to_all | solution.py:117
  169.3 71.0 %copy-start.7 = (s32[1,1,128]{2,1,0:T(1,128)S(1)}, s32[1,1,128]{2,1,0:T(1,128)}, u32[]{:S(2)}) copy-start(s32[1,1,128]{2,1,0:T(1,128)} %param.26) | copy-start | bytes 1540
  169.3 81.7 %copy-start.4 = (f32[1664]{0:T(1024)S(1)}, f32[1664]{0:T(1024)}, u32[]{:S(2)}) copy-start(f32[1664]{0:T(1024)} %param.29) | copy-start | bytes 19972
  233.8 76.6 %copy-start.6 = (bf16[3,1664,104]{1,2,0:T(8,128)(2,1)S(1)}, bf16[3,1664,104]{1,2,0:T(8,128)(2,1)}, u32[]{:S(2)}) copy-start(bf16[3,1664,104]{1,2,0:T(8,128)(2,1)} %param.30) | copy-start | bytes 3115012
  235.7 13.6 %all-to-all-start.3 = ((bf16[8,9,1664]{2,1,0:T(8,128)(2,1)}), bf16[8,9,1664]{2,1,0:T(8,128)(2,1)S(1)}, u32[]{:S(2)}, u32[]{:S(2)}) async-start(bf16[8,9,1664]{2,1,0:T(8,128)(2,1)} %pad_maximum_fusion), calls=%async_computation.3 | async-start | bytes 851968 | tf_op jit(solution)/shard_map/all_to_all | solution.py:135
  240.0 70.4 %all-gather.11.cloned.1.call-start = ((), (), s32[]{:S(2)}) async-start(), calls=%async_computation.8 | async-start | bytes 7241728 | tf_op jit(solution)/shard_map/all_gather | solution.py:155
  337.7 20.1 %copy-start.1 = (bf16[416,1664]{1,0:T(8,128)(2,1)S(1)}, bf16[416,1664]{1,0:T(8,128)(2,1)}, u32[]{:S(2)}) copy-start(bf16[416,1664]{1,0:T(8,128)(2,1)} %param.23) | copy-start | bytes 4153348
Sparse Core Ops, SparseCore 0:
  11.3 66.0 all-gather.4
  79.5 59.0 all-gather.6
  140.8 90.1 all-gather.8
  252.1 58.3 all-gather.10

commit v6 on v5

--- a/solution.py
+++ b/solution.py
@@ -64,6 +64,35 @@
     blocks = heads.reshape(seq_count, rows, width)
     swapped = lax.all_to_all(blocks, "seq", split_axis=0, concat_axis=0, tiled=True)
     return swapped.transpose(1, 0, 2).reshape(rows, seq_count * width)
+
+
+def attend_causal(queries, key_rows, value_rows, allowed_fn):
+    length = queries.shape[0]
+    head_width = queries.shape[1]
+    head_count = head_width // HEAD_DIM
+    block_rows = min(512, length)
+    block_count = length // block_rows
+    key_heads = key_rows.reshape(length, head_count, HEAD_DIM)
+    value_heads = value_rows.reshape(length, head_count, HEAD_DIM)
+    outputs = []
+    for block in range(block_count):
+        first_row = block * block_rows
+        key_end = first_row + block_rows
+        query_part = queries[first_row:key_end].reshape(block_rows, head_count, HEAD_DIM)
+        scores = jnp.einsum(
+            "qhe,khe->hqk", query_part, key_heads[:key_end], preferred_element_type=jnp.float32
+        ) * HEAD_DIM ** (-0.5)
+        allowed = allowed_fn(first_row + jnp.arange(block_rows, dtype=jnp.int32))[:, :key_end]
+        scores = jnp.where(allowed[None], scores, -1e30)
+        row_max = jnp.max(scores, axis=-1, keepdims=True)
+        expo = jnp.exp(scores - row_max)
+        probabilities = (expo / jnp.sum(expo, axis=-1, keepdims=True)).astype(jnp.bfloat16)
+        outputs.append(
+            jnp.einsum(
+                "hqk,khe->qhe", probabilities, value_heads[:key_end], preferred_element_type=jnp.float32
+            ).astype(jnp.bfloat16)
+        )
+    return jnp.concatenate(outputs, axis=0).reshape(length, head_width)
 
 
 def per_device(
@@ -115,9 +144,13 @@
     feature_slices = lax.all_to_all(merged_in, "seq", split_axis=1, concat_axis=0, tiled=True)
     merge_partial = jnp.dot(feature_slices, merge_w, preferred_element_type=jnp.float32)
     merge_parts = lax.all_to_all(
-        merge_partial.reshape(seq_count, -1, model_width), "seq", split_axis=0, concat_axis=0, tiled=True
-    )
-    visual = jnp.sum(merge_parts, axis=0).astype(jnp.bfloat16)
+        merge_partial.astype(jnp.bfloat16).reshape(seq_count, -1, model_width),
+        "seq",
+        split_axis=0,
+        concat_axis=0,
+        tiled=True,
+    )
+    visual = jnp.sum(merge_parts.astype(jnp.float32), axis=0).astype(jnp.bfloat16)
     dest_rows = dest_group[:, 0]
     merged_rows = dest_rows.shape[0]
     capacity = max(2, 2 * merged_rows // groups)
@@ -159,7 +192,7 @@
     def txt_allowed(row_indices):
         return (key_positions[None, :] <= row_indices[:, None]) & (key_positions[None, :] < length)
 
-    txt_heads = attend_local(txt_proj[0], txt_proj[1], txt_proj[2], txt_allowed)
+    txt_heads = attend_causal(txt_proj[0], txt_proj[1], txt_proj[2], txt_allowed)
     txt_attn = jnp.dot(
         heads_to_rows(txt_heads, seq_count), txt_out_full, preferred_element_type=jnp.float32
     )

time: 365 us -> 322 us (0.88)
  waiting for transfers between devices: 228 us -> 199 us
  matrix products: 42.2 us -> 34.8 us
  other arithmetic: 23.5 us -> 19.2 us
    all_to_all x1, waiting for transfers between devices: 63.2 us -> 34.2 us  [per_device(): lax.all_to_all(merge_partial.astype(jnp.bfloat16).reshape(seq_count, -1,...]
    dot_general x8 -> x4, matrix products: 9.87 us -> 3.92 us  [one_block(): jnp.einsum('qhe,khe->hqk', query_part, key_heads, preferred_element_type=...]
    dot_general x0 -> x8, matrix products: none -> 5.66 us  [the longest x4 3.46 us: attend_causal(): jnp.einsum('qhe,khe->hqk', query_part, key_heads[:key_end], preferred_ele...]
    dot_general x8 -> x4, matrix products: 8.53 us -> 4.36 us  [one_block(): jnp.einsum('hqk,khe->qhe', probabilities, value_heads, preferred_element_...]
  transfers between devices with their start and end apart: 7 -> 7, of which waited for: 5 -> 5; matrix products, arithmetic and copies ran while one was open for 10% -> 12% of each run, Pallas kernels for 0% -> 0%
where the time goes in v6:
time: 322 us
  waiting for transfers between devices  199 us (62%)
  matrix products  34.8 us (11%)
  blocking collectives  34.5 us (11%)
  other arithmetic  19.2 us (6%)
  between operations  14.1 us (4%)
  starting transfers between devices  13.8 us (4%)
  local copies, waits for them, and re-layouts  6.74 us (2%)
    all_gather x1, waiting for transfers between devices, per_device(): lax.all_gather(vis_normed, 'seq', axis=0, tiled=True)  64.4 us
    all_gather x1, waiting for transfers between devices, per_device(): lax.all_gather(txt_normed, 'seq', axis=0, tiled=True)  58.3 us
    all_to_all x1, waiting for transfers between devices, per_device(): lax.all_to_all(merge_partial.astype(jnp.bfloat16).reshape(seq_count, -1,...  34.2 us
    all_gather x1, waiting for transfers between devices, per_device(): vis_out_full = lax.all_gather(vis_out, 'seq', axis=0, tiled=True)  31.9 us
    all_to_all x1, blocking collectives, per_device(): lax.all_to_all(merged_in, 'seq', split_axis=1, concat_axis=0, tiled=True)  19 us
    all_to_all x1, blocking collectives, heads_to_rows(): lax.all_to_all(blocks, 'seq', split_axis=0, concat_axis=0, tiled=True)  15.5 us
    unnamed x2, matrix products  11.3 us
    all_to_all x1, waiting for transfers between devices, per_device(): lax.all_to_all(jnp.concatenate([outgoing, flag_row], axis=1), 'grp', spli...  9.02 us
  transfers between devices with their start and end apart: 7, of which 5 were waited for; matrix products, arithmetic and copies ran while one was open for 12% of the time, Pallas kernels for 0%

profile of v6, /device:TPU:0, one launch (start us, length us, event | category | flops | bytes accessed | tf_op | source)
XLA Modules:
  0.0 321.7 jit_solution(5109617639158701575)
XLA Ops:
  6.5 1.3 convert_reduce_fusion.1
  7.8 1.3 fusion.35
  9.1 2.1 fusion.37
  11.2 0.7 all-gather.7.cloned.1.call-update
  12.0 0.8 reduce-window.4
  12.9 64.4 %all-gather.5.cloned.1.call-done = bf16[2048,1664]{1,0:T(8,128)(2,1)} async-done(((bf16[128,1664]{1,0:T(8,128)(2,1)}), bf16[2048,1664]{1,0:T(8,128)(2,1)}) %all-gather.5.cloned.1.call-update) | async-done | bytes 6815760 | tf_op jit(solution)/shard_map/all_gather | solution.py:121
  77.4 5.7 %fusion.59 = f32[2048,312]{0,1:S(1)} fusion(bf16[2048,1664]{1,0:T(8,128)(2,1)} %all-gather.5.cloned.1.call-done, bf16[1664,312]{0,1:T(8,128)(2,1)} %bitcast.190), kind=kOutput, calls=%fused_computation.144 | convolution fusion | flops 2126512128 | bytes 10409984
  83.3 0.3 reshape_squeeze.12
  83.7 16.5 %while.12 = (s32[]{:T(128)}, bf16[4,512,1,104]{1,3,2,0:T(8,128)(2,1)S(1)}, s32[4]{0:T(128)S(1)}, s32[3]{0:T(128)S(1)}, s32[2048]{0:T(1024)S(1)}, /*index=5*/bf16...) while((s32[]{:T(128)}, ...), condition=%wide.region_10.11_spmd, body=%wide.region_6.10_spmd.sunk | while | flops 445709312 | bytes 13674625 | solution.py:57
  83.7 0.6 dynamic_slice.23
  84.3 0.7 add_select_fusion.3
  85.1 1.0 fusion.77
  86.0 0.7 fusion.78
  86.8 1.1 fusion.79
  87.9 0.6 dynamic_slice.23
  88.4 0.7 add_select_fusion.3
  89.2 1.0 fusion.77
  90.2 0.7 fusion.78
  90.9 1.1 fusion.79
  92.0 0.6 dynamic_slice.23
  92.6 0.7 add_select_fusion.3
  93.3 1.0 fusion.77
  94.3 0.7 fusion.78
  95.0 1.1 fusion.79
  96.1 0.6 dynamic_slice.23
  96.7 0.7 add_select_fusion.3
  97.4 1.0 fusion.77
  98.4 0.7 fusion.78
  99.1 1.1 fusion.79
  100.6 0.8 copy_bitcast_fusion
  101.4 5.2 %all-to-all-start = ((bf16[16,128,104]{1,2,0:T(8,128)(2,1)}), bf16[16,128,104]{1,2,0:T(8,128)(2,1)S(1)}, u32[]{:S(2)}, u32[]{:S(2)}) async-start(bf16[16,128,104]{1,2,0:T(8,128)(2,1)} %copy_bitcast_fusion), calls=%async_computation | async-start | bytes 851968 | tf_op jit(solution)/shard_map/all_to_all | solution.py:65
  106.7 31.9 %all-gather.7.cloned.1.call-done = bf16[1664,1664]{1,0:T(8,128)(2,1)} async-done(((bf16[104,1664]{1,0:T(8,128)(2,1)}), bf16[1664,1664]{1,0:T(8,128)(2,1)}) %all-gather.7.cloned.1.call-update) | async-done | bytes 5537808 | tf_op jit(solution)/shard_map/all_gather | solution.py:119
  138.6 3.7 %fusion.54 = (f32[128]{0:T(128)S(1)}, f32[128,1664]{1,0:T(8,128)S(1)}) fusion(bf16[128,1664]{0,1:T(8,128)(2,1)S(1)} %bitcast.179, bf16[1664,1664]{1,0:T(8,128)(2,1)} %all-gather.7.cloned.1.call-done, bf16[128,1664]{1,0:T(8,128)(2,1)S(1)} %copy-done.1), kind=kOutput, calls=%fused_computation.139 | convolution fusion | flops 709476224 | bytes 7242240 | tf_op jit(solution)/shard_map/dot_general | solution.py:135
  142.8 0.6 all_to_all.27
  143.7 19.0 %all_to_all.39 = bf16[32,16,416]{2,0,1:T(8,128)(2,1)S(1)} all-to-all(bf16[32,16,416]{2,0,1:T(8,128)(2,1)S(1)} %copy.33), channel_id=1, replica_groups=mesh['seq'=16,'grp'=8] {'seq'}, dimensions={1} | all-to-all | bytes 851968 | tf_op jit(solution)/shard_map/all_to_all | solution.py:144
  162.7 2.3 convolution_convert_fusion
  165.0 3.8 %all-to-all-start.2 = ((bf16[16,32,1664]{2,1,0:T(8,128)(2,1)}), bf16[16,32,1664]{2,1,0:T(8,128)(2,1)S(1)}, u32[]{:S(2)}, u32[]{:S(2)}) async-start(bf16[16,32,1664]{2,1,0:T(8,128)(2,1)} %bitcast.180), calls=%async_computation.2 | async-start | bytes 3407872 | tf_op jit(solution)/shard_map/all_to_all | solution.py:146
  169.0 0.9 select_reduce_fusion
  169.9 0.7 iota_compare_fusion.5
  170.6 0.7 copy.34
  171.3 34.2 %all-to-all-done.2 = bf16[16,32,1664]{2,1,0:T(8,128)(2,1)S(1)} async-done(((bf16[16,32,1664]{2,1,0:T(8,128)(2,1)}), bf16[16,32,1664]{2,1,0:T(8,128)(2,1)S(1)}, u32[]{:S(2)}, u32[]{:S(2)}) %all-to-all-start.2) | async-done | bytes 1703968 | tf_op jit(solution)/shard_map/all_to_all | solution.py:146
  205.4 0.9 reduce_sum.159
  206.4 1.1 convolution_convert_fusion.1
  207.4 1.6 pad_maximum_fusion
  209.1 4.4 %all-to-all-start.3 = ((bf16[8,9,1664]{2,1,0:T(8,128)(2,1)}), bf16[8,9,1664]{2,1,0:T(8,128)(2,1)S(1)}, u32[]{:S(2)}, u32[]{:S(2)}) async-start(bf16[8,9,1664]{2,1,0:T(8,128)(2,1)} %pad_maximum_fusion), calls=%async_computation.3 | async-start | bytes 851968 | tf_op jit(solution)/shard_map/all_to_all | solution.py:168
  213.8 9.0 %all-to-all-done.3 = bf16[8,9,1664]{2,1,0:T(8,128)(2,1)S(1)} async-done(((bf16[8,9,1664]{2,1,0:T(8,128)(2,1)}), bf16[8,9,1664]{2,1,0:T(8,128)(2,1)S(1)}, u32[]{:S(2)}, u32[]{:S(2)}) %all-to-all-start.3) | async-done | bytes 239648 | tf_op jit(solution)/shard_map/all_to_all | solution.py:168
  223.0 0.5 multiply_reduce_fusion
  223.5 0.9 multiply_convert_fusion
  225.1 58.3 %all-gather.11.cloned.1.call-done = bf16[2048,1664]{1,0:T(8,128)(2,1)} async-done(((bf16[128,1664]{1,0:T(8,128)(2,1)}), bf16[2048,1664]{1,0:T(8,128)(2,1)}) %all-gather.11.cloned.1.call-update) | async-done | bytes 6815760 | tf_op jit(solution)/shard_map/all_gather | solution.py:188
  283.4 5.7 %fusion.60 = f32[2048,312]{0,1:S(1)} fusion(bf16[2048,1664]{1,0:T(8,128)(2,1)} %all-gather.11.cloned.1.call-done, bf16[1664,312]{0,1:T(8,128)(2,1)} %bitcast.191), kind=kOutput, calls=%fused_computation.145 | convolution fusion | flops 2126512128 | bytes 10409984
  289.3 0.5 slice-done.2
  289.8 0.4 fusion.58
  290.4 0.3 fusion.30
  290.8 0.7 fusion.57
  291.6 0.4 fusion.22
  291.9 0.5 fusion.29
  292.6 1.0 fusion.56
  293.6 0.5 fusion.17
  294.1 0.6 fusion.28
  294.8 1.3 fusion.55
  296.1 0.6 fusion.14
  296.8 0.8 fusion.27
  297.8 15.5 %all_to_all.40 = bf16[16,128,104]{1,2,0:T(8,128)(2,1)S(1)} all-to-all(bf16[16,128,104]{1,2,0:T(8,128)(2,1)S(1)} %copy.38), channel_id=1, replica_groups=mesh['seq'=16,'grp'=8] {'seq'}, dimensions={0} | all-to-all | bytes 851968 | tf_op jit(solution)/shard_map/all_to_all | solution.py:65
  313.3 1.9 convolution_add_fusion
  (75 shorter events, 3.7 us)
Async XLA Ops:
  6.5 156.1 %copy-start = (bf16[416,1664]{1,0:T(8,128)(2,1)S(1)}, bf16[416,1664]{1,0:T(8,128)(2,1)}, u32[]{:S(2)}) copy-start(bf16[416,1664]{1,0:T(8,128)(2,1)} %param.21) | copy-start | bytes 4153348
  6.5 70.8 %all-gather.5.cloned.1.call-start = ((), (), s32[]{:S(2)}) async-start(), calls=%async_computation.5 | async-start | bytes 7241728 | tf_op jit(solution)/shard_map/all_gather | solution.py:121
  11.2 127.4 %all-gather.7.cloned.1.call-start = ((), (), s32[]{:S(2)}) async-start(), calls=%async_computation.6 | async-start | bytes 5883904 | tf_op jit(solution)/shard_map/all_gather | solution.py:119
  11.9 212.5 %all-gather.9.cloned.1.call-start = ((), (), s32[]{:S(2)}) async-start(), calls=%async_computation.7 | async-start | bytes 5883904 | tf_op jit(solution)/shard_map/all_gather | solution.py:134
  100.2 38.3 %copy-start.1 = (bf16[128,1664]{1,0:T(8,128)(2,1)S(1)}, bf16[128,1664]{1,0:T(8,128)(2,1)}, u32[]{:S(2)}) copy-start(bf16[128,1664]{1,0:T(8,128)(2,1)} %param.16) | copy-start | bytes 1277956
  101.4 37.2 %all-to-all-start = ((bf16[16,128,104]{1,2,0:T(8,128)(2,1)}), bf16[16,128,104]{1,2,0:T(8,128)(2,1)S(1)}, u32[]{:S(2)}, u32[]{:S(2)}) async-start(bf16[16,128,104]{1,2,0:T(8,128)(2,1)} %copy_bitcast_fusion), calls=%async_computation | async-start | bytes 851968 | tf_op jit(solution)/shard_map/all_to_all | solution.py:65
  138.6 4.0 %copy-start.3 = (f32[1664]{0:T(1024)S(1)}, f32[1664]{0:T(1024)}, u32[]{:S(2)}) copy-start(f32[1664]{0:T(1024)} %param.20) | copy-start | bytes 19972
  165.0 3.9 %copy-start.7 = (s32[32,1]{0,1:T(1,128)S(1)}, s32[32,1]{0,1:T(1,128)}, u32[]{:S(2)}) copy-start(s32[32,1]{0,1:T(1,128)} %param.23) | copy-start | bytes 388
  165.0 58.0 %copy-start.2 = (bf16[128,1664]{1,0:T(8,128)(2,1)S(1)}, bf16[128,1664]{1,0:T(8,128)(2,1)}, u32[]{:S(2)}) copy-start(bf16[128,1664]{1,0:T(8,128)(2,1)} %param.26) | copy-start | bytes 1277956
  165.0 40.4 %all-to-all-start.2 = ((bf16[16,32,1664]{2,1,0:T(8,128)(2,1)}), bf16[16,32,1664]{2,1,0:T(8,128)(2,1)S(1)}, u32[]{:S(2)}, u32[]{:S(2)}) async-start(bf16[16,32,1664]{2,1,0:T(8,128)(2,1)} %bitcast.180), calls=%async_computation.2 | async-start | bytes 3407872 | tf_op jit(solution)/shard_map/all_to_all | solution.py:146
  168.9 54.6 %copy-start.4 = (f32[1664]{0:T(1024)S(1)}, f32[1664]{0:T(1024)}, u32[]{:S(2)}) copy-start(f32[1664]{0:T(1024)} %param.27) | copy-start | bytes 19972
  169.0 44.7 %copy-start.8 = (s32[1,1,128]{2,1,0:T(1,128)S(1)}, s32[1,1,128]{2,1,0:T(1,128)}, u32[]{:S(2)}) copy-start(s32[1,1,128]{2,1,0:T(1,128)} %param.24) | copy-start | bytes 1540
  209.1 13.7 %all-to-all-start.3 = ((bf16[8,9,1664]{2,1,0:T(8,128)(2,1)}), bf16[8,9,1664]{2,1,0:T(8,128)(2,1)S(1)}, u32[]{:S(2)}, u32[]{:S(2)}) async-start(bf16[8,9,1664]{2,1,0:T(8,128)(2,1)} %pad_maximum_fusion), calls=%async_computation.3 | async-start | bytes 851968 | tf_op jit(solution)/shard_map/all_to_all | solution.py:168
  213.5 69.9 %all-gather.11.cloned.1.call-start = ((), (), s32[]{:S(2)}) async-start(), calls=%async_computation.8 | async-start | bytes 7241728 | tf_op jit(solution)/shard_map/all_gather | solution.py:188
  225.1 64.0 %copy-start.5 = (pred[2048]{0:T(1024)(128)(4,1)}, pred[2048]{0:T(1024)(128)(4,1)S(1)}, u32[]{:S(2)}) copy-start(pred[2048]{0:T(1024)(128)(4,1)S(1)} %iota_compare_fusion.4) | copy-start | bytes 6148
  289.1 0.7 slice-start.2
  290.2 0.7 slice-start.3
  291.9 0.7 copy-start.6
  296.1 17.1 %slice-start = ((s8[5537792]{0:T(1024)(128)(4,1)}), s8[1343488]{0:T(1024)(128)(4,1)S(1)}, s32[]{:S(2)}) async-start(s8[5537792]{0:T(1024)(128)(4,1)} %bitcast.175), calls=%async_computation.9 | async-start | bytes 2686976
  296.8 16.5 %slice-start.1 = ((s8[5537792]{0:T(1024)(128)(4,1)}), s8[4194304]{0:T(1024)(128)(4,1)S(1)}, s32[]{:S(2)}) async-start(s8[5537792]{0:T(1024)(128)(4,1)} %bitcast.175), calls=%async_computation.10 | async-start | bytes 8388608
Sparse Core Ops, SparseCore 0:
  11.3 66.0 all-gather.4
  79.5 59.0 all-gather.6
  140.7 70.9 all-gather.8
  224.5 58.8 all-gather.10

commit v7 on v6

--- a/solution.py
+++ b/solution.py
@@ -95,6 +95,25 @@
     return jnp.concatenate(outputs, axis=0).reshape(length, head_width)
 
 
+def core_half(w_local):
+    half = w_local.shape[1] // 2
+    core = lax.axis_index("grp") % 2
+    return lax.dynamic_slice_in_dim(w_local, core * half, half, axis=1), core
+
+
+def swap_cores(mine_full):
+    groups = lax.axis_size("grp")
+    return lax.ppermute(mine_full, "grp", [(g, g ^ 1) for g in range(groups)])
+
+
+def project_halves(rows, mine_full, other_full, core):
+    out_mine = jnp.dot(rows, mine_full, preferred_element_type=jnp.float32)
+    out_other = jnp.dot(rows, other_full, preferred_element_type=jnp.float32)
+    first = jnp.where(core == 0, out_mine, out_other)
+    second = jnp.where(core == 0, out_other, out_mine)
+    return jnp.concatenate([first, second], axis=1)
+
+
 def per_device(
     patches,
     vis_gain,
@@ -116,9 +135,21 @@
     token_count = patches.shape[0]
     model_width = patches.shape[1]
     group_patches = token_count * seq_count
-    vis_out_full = lax.all_gather(vis_out, "seq", axis=0, tiled=True)
     vis_normed = layer_norm(patches, vis_gain).astype(jnp.bfloat16)
-    vis_proj = projector(vis_qkv, lax.all_gather(vis_normed, "seq", axis=0, tiled=True))
+    vis_mine, core = core_half(vis_out)
+    weight_rows, half_width = vis_mine.shape
+    packed_rows = weight_rows * half_width // model_width
+    padded_rows = -(-packed_rows // 16) * 16
+    packed = jnp.pad(vis_mine.reshape(packed_rows, model_width), ((0, padded_rows - packed_rows), (0, 0)))
+    bundle = lax.all_gather(
+        jnp.concatenate([vis_normed, packed], axis=0), "seq", axis=0, tiled=False
+    )
+    vis_gathered = bundle[:, :token_count].reshape(group_patches, model_width)
+    vis_mine_full = bundle[:, token_count : token_count + packed_rows].reshape(
+        seq_count * weight_rows, half_width
+    )
+    vis_other_full = swap_cores(vis_mine_full)
+    vis_proj = projector(vis_qkv, vis_gathered)
     bounds = jnp.cumsum(image_blocks[0])[:-1]
 
     def segment(indices):
@@ -131,10 +162,8 @@
 
     vis_heads = attend_local(vis_proj[0], vis_proj[1], vis_proj[2], vis_allowed)
     vis_heads, txt_out = lax.optimization_barrier((vis_heads, txt_out))
-    txt_out_full = lax.all_gather(txt_out, "seq", axis=0, tiled=True)
-    vis_attn = jnp.dot(
-        heads_to_rows(vis_heads, seq_count), vis_out_full, preferred_element_type=jnp.float32
-    )
+    txt_mine_full = lax.all_gather(core_half(txt_out)[0], "seq", axis=0, tiled=True)
+    vis_attn = project_halves(heads_to_rows(vis_heads, seq_count), vis_mine_full, vis_other_full, core)
     residual_sum = patches.astype(jnp.float32) + vis_attn
     merged_in = (
         layer_norm(residual_sum, merge_gain)
@@ -184,7 +213,8 @@
     )
     hidden = (text_emb.astype(jnp.float32) * (1.0 - replaced) + placed).astype(jnp.bfloat16)
     txt_normed = rms_norm(hidden, txt_gain).astype(jnp.bfloat16)
-    txt_normed, txt_out_full = lax.optimization_barrier((txt_normed, txt_out_full))
+    txt_normed, txt_mine_full = lax.optimization_barrier((txt_normed, txt_mine_full))
+    txt_other_full = swap_cores(txt_mine_full)
     txt_proj = projector(txt_qkv, lax.all_gather(txt_normed, "seq", axis=0, tiled=True))
     length = prompt_len[0]
     key_positions = jnp.arange(prompt_rows * seq_count, dtype=jnp.int32)
@@ -193,9 +223,7 @@
         return (key_positions[None, :] <= row_indices[:, None]) & (key_positions[None, :] < length)
 
     txt_heads = attend_causal(txt_proj[0], txt_proj[1], txt_proj[2], txt_allowed)
-    txt_attn = jnp.dot(
-        heads_to_rows(txt_heads, seq_count), txt_out_full, preferred_element_type=jnp.float32
-    )
+    txt_attn = project_halves(heads_to_rows(txt_heads, seq_count), txt_mine_full, txt_other_full, core)
     return hidden.astype(jnp.float32) + txt_attn
 
 

time: 322 us -> 338 us (1.050)
  local copies, waits for them, and re-layouts: 6.74 us -> 38 us
  waiting for transfers between devices: 199 us -> 192 us
  blocking collectives: 34.5 us -> 28.8 us
  other arithmetic: 19.2 us -> 14.1 us
    all_gather x3 -> x2, waiting for transfers between devices: 96.3 us -> 81.3 us  [the longest x1 81.3 us: per_device(): lax.all_gather(jnp.concatenate([vis_normed, packed], axis=0), 'seq', axis...]
    reshape x0 -> x4, local copies, waits for them, and re-layouts: none -> 11.6 us  [the longest x2 11.2 us: per_device(): bundle[:, token_count:token_count + packed_rows]]
    all_to_all x1, waiting for transfers between devices: 0.01 us -> 10.1 us  [heads_to_rows(): lax.all_to_all(blocks, 'seq', split_axis=0, concat_axis=0, tiled=True)]
    slice x0 -> x2, local copies, waits for them, and re-layouts: none -> 7.36 us  [the longest x1 3.78 us: per_device(): bundle[:, token_count:token_count + packed_rows]]
    optimization_barrier x0 -> x1, local copies, waits for them, and re-layouts: none -> 5.51 us  [per_device(): lax.optimization_barrier((txt_normed, txt_mine_full))]
    all_to_all x1, blocking collectives: 19 us -> 14.4 us  [per_device(): lax.all_to_all(merged_in, 'seq', split_axis=1, concat_axis=0, tiled=True)]
    dot_general x2 -> x4, matrix products: 5.66 us -> 9.72 us  [the longest x2 5.43 us: project_halves(): out_other = jnp.dot(rows, other_full, preferred_element_type=jnp.float32)]
  transfers between devices with their start and end apart: 7 -> 8, of which waited for: 5 -> 5; matrix products, arithmetic and copies ran while one was open for 12% -> 17% of each run, Pallas kernels for 0% -> 0%
where the time goes in v7:
time: 338 us; the launch traced here: 337 us
  waiting for transfers between devices  192 us (57%)
  local copies, waits for them, and re-layouts  38 us (11%)
  matrix products  35.6 us (11%)
  blocking collectives  28.8 us (9%)
  between operations  14.2 us (4%)
  other arithmetic  14.1 us (4%)
  starting transfers between devices  13.8 us (4%)
    all_gather x1, waiting for transfers between devices, per_device(): lax.all_gather(jnp.concatenate([vis_normed, packed], axis=0), 'seq', axis...  81.3 us
    all_gather x1, waiting for transfers between devices, per_device(): lax.all_gather(txt_normed, 'seq', axis=0, tiled=True)  58.5 us
    all_to_all x1, waiting for transfers between devices, per_device(): lax.all_to_all(merge_partial.astype(jnp.bfloat16).reshape(seq_count, -1,...  32.9 us
    all_to_all x1, blocking collectives, heads_to_rows(): lax.all_to_all(blocks, 'seq', split_axis=0, concat_axis=0, tiled=True)  14.4 us
    all_to_all x1, blocking collectives, per_device(): lax.all_to_all(merged_in, 'seq', split_axis=1, concat_axis=0, tiled=True)  14.4 us
    reshape x2, local copies, waits for them, and re-layouts, per_device(): bundle[:, token_count:token_count + packed_rows]  11.2 us
    all_to_all x1, waiting for transfers between devices, heads_to_rows(): lax.all_to_all(blocks, 'seq', split_axis=0, concat_axis=0, tiled=True)  10.1 us
    all_to_all x1, waiting for transfers between devices, per_device(): lax.all_to_all(jnp.concatenate([outgoing, flag_row], axis=1), 'grp', spli...  9.2 us
  transfers between devices with their start and end apart: 8, of which 5 were waited for; matrix products, arithmetic and copies ran while one was open for 17% of the time, Pallas kernels for 0%

profile of v7, /device:TPU:0, one launch (start us, length us, event | category | flops | bytes accessed | tf_op | source)
XLA Modules:
  0.0 336.7 jit_solution(14727037070686022942)
XLA Ops:
  6.5 1.2 constant_dynamic-slice_fusion
  8.2 1.3 copy.83
  10.4 1.1 copy.85
  11.9 81.3 %all-gather.9.cloned.1.call-done = bf16[3072,1664]{1,0:T(8,128)(2,1)} async-done(((bf16[192,1664]{1,0:T(8,128)(2,1)}), bf16[3072,1664]{1,0:T(8,128)(2,1)}) %all-gather.9.cloned.1.call-update) | async-done | bytes 10223632 | tf_op jit(solution)/shard_map/all_gather | solution.py:144
  93.2 3.6 %slice.121 = bf16[16,128,1664]{2,1,0:T(8,128)(2,1)S(1)} slice(bf16[16,192,1664]{2,1,0:T(8,128)(2,1)} %bitcast.181), slice={[0:16], [0:128], [0:1664]} | slice | bytes 13631488 | tf_op jit(solution)/shard_map/slice | solution.py:147
  96.8 3.8 %slice.125 = bf16[16,52,1664]{2,1,0:T(8,128)(2,1)} slice(bf16[16,192,1664]{2,1,0:T(8,128)(2,1)} %bitcast.182), slice={[0:16], [128:180], [0:1664]} | slice | bytes 5537792 | tf_op jit(solution)/shard_map/slice | solution.py:148
  100.6 2.6 fusion.61
  103.8 5.8 %reshape.381 = bf16[1664,832]{1,0:T(8,128)(2,1)} reshape(bf16[16,52,1664]{2,1,0:T(8,128)(2,1)} %slice.125) | data formatting | bytes 5537792 | tf_op jit(solution)/shard_map/reshape | solution.py:148
  109.6 5.3 %copy.89 = bf16[1664,832]{0,1:T(8,128)(2,1)} copy(bf16[1664,832]{1,0:T(8,128)(2,1)} %reshape.381) | data formatting | bytes 5537792 | tf_op jit(solution)/shard_map/reshape | solution.py:148
  115.0 16.5 %while.12 = (s32[]{:T(128)}, bf16[4,512,1,104]{1,3,2,0:T(8,128)(2,1)S(1)}, s32[4]{0:T(128)S(1)}, s32[3]{0:T(128)S(1)}, s32[2048]{0:T(1024)S(1)}, /*index=5*/bf16...) while((s32[]{:T(128)}, ...), condition=%wide.region_10.11_spmd, body=%wide.region_6.10_spmd.sunk | while | flops 445709312 | bytes 13674625 | solution.py:57
  115.0 0.6 dynamic_slice.33
  115.6 0.7 add_select_fusion.3
  116.3 1.0 fusion.85
  117.3 0.7 fusion.86
  118.0 1.1 fusion.87
  119.1 0.6 dynamic_slice.33
  119.7 0.7 add_select_fusion.3
  120.4 1.0 fusion.85
  121.4 0.7 fusion.86
  122.1 1.1 fusion.87
  123.2 0.6 dynamic_slice.33
  123.8 0.7 add_select_fusion.3
  124.6 1.0 fusion.85
  125.5 0.7 fusion.86
  126.3 1.1 fusion.87
  127.4 0.6 dynamic_slice.33
  128.0 0.7 add_select_fusion.3
  128.7 1.0 fusion.85
  129.7 0.7 fusion.86
  130.4 1.1 fusion.87
  131.8 0.8 copy_bitcast_fusion
  132.6 5.3 %all-to-all-start = ((bf16[16,128,104]{1,2,0:T(8,128)(2,1)}), bf16[16,128,104]{1,2,0:T(8,128)(2,1)S(1)}, u32[]{:S(2)}, u32[]{:S(2)}) async-start(bf16[16,128,104]{1,2,0:T(8,128)(2,1)} %copy_bitcast_fusion), calls=%async_computation | async-start | bytes 851968 | tf_op jit(solution)/shard_map/all_to_all | solution.py:65
  138.2 0.8 constant_dynamic-slice_fusion.1
  139.0 10.1 %all-to-all-done = bf16[16,128,104]{1,2,0:T(8,128)(2,1)S(1)} async-done(((bf16[16,128,104]{1,2,0:T(8,128)(2,1)}), bf16[16,128,104]{1,2,0:T(8,128)(2,1)S(1)}, u32[]{:S(2)}, u32[]{:S(2)}) %all-to-all-start) | async-done | bytes 426016 | tf_op jit(solution)/shard_map/all_to_all | solution.py:65
  149.1 3.1 fusion.62
  152.2 2.8 broadcast_select_fusion.3
  156.0 0.6 all_to_all.27
  156.9 14.4 %all_to_all.39 = bf16[32,16,416]{2,0,1:T(8,128)(2,1)S(1)} all-to-all(bf16[32,16,416]{2,0,1:T(8,128)(2,1)S(1)} %copy.91), channel_id=1, replica_groups=mesh['seq'=16,'grp'=8] {'seq'}, dimensions={1} | all-to-all | bytes 851968 | tf_op jit(solution)/shard_map/all_to_all | solution.py:173
  171.3 2.3 convolution_convert_fusion
  173.6 3.8 %all-to-all-start.2 = ((bf16[16,32,1664]{2,1,0:T(8,128)(2,1)}), bf16[16,32,1664]{2,1,0:T(8,128)(2,1)S(1)}, u32[]{:S(2)}, u32[]{:S(2)}) async-start(bf16[16,32,1664]{2,1,0:T(8,128)(2,1)} %bitcast.190), calls=%async_computation.2 | async-start | bytes 3407872 | tf_op jit(solution)/shard_map/all_to_all | solution.py:175
  177.9 0.7 copy.92
  178.6 1.3 copy.82
  179.8 32.9 %all-to-all-done.2 = bf16[16,32,1664]{2,1,0:T(8,128)(2,1)S(1)} async-done(((bf16[16,32,1664]{2,1,0:T(8,128)(2,1)}), bf16[16,32,1664]{2,1,0:T(8,128)(2,1)S(1)}, u32[]{:S(2)}, u32[]{:S(2)}) %all-to-all-start.2) | async-done | bytes 1703968 | tf_op jit(solution)/shard_map/all_to_all | solution.py:175
  212.8 0.9 reduce_sum.159
  213.7 1.1 convolution_convert_fusion.1
  214.8 1.6 pad_maximum_fusion
  216.4 4.4 %all-to-all-start.3 = ((bf16[8,9,1664]{2,1,0:T(8,128)(2,1)}), bf16[8,9,1664]{2,1,0:T(8,128)(2,1)S(1)}, u32[]{:S(2)}, u32[]{:S(2)}) async-start(bf16[8,9,1664]{2,1,0:T(8,128)(2,1)} %pad_maximum_fusion), calls=%async_computation.3 | async-start | bytes 851968 | tf_op jit(solution)/shard_map/all_to_all | solution.py:197
  220.9 9.2 %all-to-all-done.3 = bf16[8,9,1664]{2,1,0:T(8,128)(2,1)S(1)} async-done(((bf16[8,9,1664]{2,1,0:T(8,128)(2,1)}), bf16[8,9,1664]{2,1,0:T(8,128)(2,1)S(1)}, u32[]{:S(2)}, u32[]{:S(2)}) %all-to-all-start.3) | async-done | bytes 239648 | tf_op jit(solution)/shard_map/all_to_all | solution.py:197
  230.3 0.5 multiply_reduce_fusion
  230.8 1.0 multiply_convert_fusion
  232.6 5.5 %copy.99 = bf16[1664,832]{0,1:T(8,128)(2,1)} copy(bf16[1664,832]{1,0:T(8,128)(2,1)} %all-gather.5.cloned.1.call-done) | data formatting | bytes 5537792 | tf_op jit(solution)/shard_map/optimization_barrier | solution.py:216
  238.1 58.5 %all-gather.7.cloned.1.call-done = bf16[2048,1664]{0,1:T(8,128)(2,1)} async-done(((bf16[128,1664]{0,1:T(8,128)(2,1)}), bf16[2048,1664]{0,1:T(8,128)(2,1)}) %all-gather.7.cloned.1.call-update) | async-done | bytes 6815760 | tf_op jit(solution)/shard_map/all_gather | solution.py:218
  296.6 5.5 %fusion.63 = f32[2048,312]{0,1:S(1)} fusion(bf16[2048,1664]{0,1:T(8,128)(2,1)} %all-gather.7.cloned.1.call-done, bf16[1664,312]{0,1:T(8,128)(2,1)S(1)} %bitcast.200), kind=kOutput, calls=%fused_computation.155 | convolution fusion | flops 2126512128 | bytes 10409984
  303.7 1.3 fusion.57
  305.1 0.7 fusion.59
  305.8 1.0 fusion.58
  306.8 0.5 fusion.17
  307.7 0.6 fusion.14
  308.8 0.6 fusion.29
  309.4 0.8 fusion.28
  310.5 14.4 %all_to_all.40 = bf16[16,128,104]{1,2,0:T(8,128)(2,1)S(1)} all-to-all(bf16[16,128,104]{1,2,0:T(8,128)(2,1)S(1)} %copy.98), channel_id=1, replica_groups=mesh['seq'=16,'grp'=8] {'seq'}, dimensions={0} | all-to-all | bytes 851968 | tf_op jit(solution)/shard_map/all_to_all | solution.py:65
  324.9 1.2 fusion.64
  326.1 2.7 broadcast_select_fusion.1
  328.9 1.2 copy.100
  (100 shorter events, 8.1 us)
Async XLA Ops:
  6.5 164.7 %copy-start = (bf16[416,1664]{1,0:T(8,128)(2,1)S(1)}, bf16[416,1664]{1,0:T(8,128)(2,1)}, u32[]{:S(2)}) copy-start(bf16[416,1664]{1,0:T(8,128)(2,1)} %param.21) | copy-start | bytes 4153348
  6.5 3.4 %copy-start.4 = (f32[1664]{0:T(1024)S(1)}, f32[1664]{0:T(1024)}, u32[]{:S(2)}) copy-start(f32[1664]{0:T(1024)} %param.17) | copy-start | bytes 19972
  6.5 86.7 %all-gather.9.cloned.1.call-start = ((), (), s32[]{:S(2)}) async-start(), calls=%async_computation.7 | async-start | bytes 10862592 | tf_op jit(solution)/shard_map/all_gather | solution.py:144
  9.5 2.1 copy-start.12
  96.8 3.8 %copy-start.10 = (bf16[3,1664,104]{1,2,0:T(8,128)(2,1)S(1)}, bf16[3,1664,104]{1,2,0:T(8,128)(2,1)}, u32[]{:S(2)}) copy-start(bf16[3,1664,104]{1,2,0:T(8,128)(2,1)} %param.18) | copy-start | bytes 3115012
  109.6 5.3 %copy-start.2 = (bf16[4,512,1,104]{1,3,2,0:T(8,128)(2,1)S(1)}, bf16[4,512,1,104]{1,3,2,0:T(8,128)(2,1)}, u32[]{:S(2)}) copy-start(bf16[4,512,1,104]{1,3,2,0:T(8,128)(2,1)} %custom-call) | copy-start | bytes 1277956
  115.0 37.2 %collective-permute-start = (bf16[1664,832]{0,1:T(8,128)(2,1)}, bf16[1664,832]{0,1:T(8,128)(2,1)}, u32[]{:S(2)}, u32[]{:S(2)}) collective-permute-start(bf16[1664,832]{0,1:T(8,128)(2,1)} %copy.89), channel_id=1, source_target_pairs={{0,1},{1,0},{2,3},{3,2},{4,5},{5,4},{6,7},{7,6},{8,9},{9,8},{10,11... | collective-permute-start | bytes 8306696 | tf_op jit(solution)/shard_map/ppermute | solution.py:106
  131.5 6.7 %copy-start.3 = (bf16[104,1664]{1,0:T(8,128)(2,1)S(1)}, bf16[104,1664]{1,0:T(8,128)(2,1)}, u32[]{:S(2)}) copy-start(bf16[104,1664]{1,0:T(8,128)(2,1)} %param.29) | copy-start | bytes 1038340
  132.6 16.4 %all-to-all-start = ((bf16[16,128,104]{1,2,0:T(8,128)(2,1)}), bf16[16,128,104]{1,2,0:T(8,128)(2,1)S(1)}, u32[]{:S(2)}, u32[]{:S(2)}) async-start(bf16[16,128,104]{1,2,0:T(8,128)(2,1)} %copy_bitcast_fusion), calls=%async_computation | async-start | bytes 851968 | tf_op jit(solution)/shard_map/all_to_all | solution.py:65
  137.9 93.9 %all-gather.5.cloned.1.call-start = ((), (), s32[]{:S(2)}) async-start(), calls=%async_computation.5 | async-start | bytes 3168256 | tf_op jit(solution)/shard_map/all_gather | solution.py:165
  152.1 3.3 copy-start.5
  173.6 3.9 %copy-start.9 = (s32[32,1]{0,1:T(1,128)S(1)}, s32[32,1]{0,1:T(1,128)}, u32[]{:S(2)}) copy-start(s32[32,1]{0,1:T(1,128)} %param.23) | copy-start | bytes 388
  173.6 39.2 %all-to-all-start.2 = ((bf16[16,32,1664]{2,1,0:T(8,128)(2,1)}), bf16[16,32,1664]{2,1,0:T(8,128)(2,1)S(1)}, u32[]{:S(2)}, u32[]{:S(2)}) async-start(bf16[16,32,1664]{2,1,0:T(8,128)(2,1)} %bitcast.190), calls=%async_computation.2 | async-start | bytes 3407872 | tf_op jit(solution)/shard_map/all_to_all | solution.py:175
  177.4 43.4 %copy-start.13 = (s32[1,1,128]{2,1,0:T(1,128)S(1)}, s32[1,1,128]{2,1,0:T(1,128)}, u32[]{:S(2)}) copy-start(s32[1,1,128]{2,1,0:T(1,128)} %param.24) | copy-start | bytes 1540
  179.8 51.0 %copy-start.6 = (f32[1664]{0:T(1024)S(1)}, f32[1664]{0:T(1024)}, u32[]{:S(2)}) copy-start(f32[1664]{0:T(1024)} %param.27) | copy-start | bytes 19972
  216.4 13.7 %all-to-all-start.3 = ((bf16[8,9,1664]{2,1,0:T(8,128)(2,1)}), bf16[8,9,1664]{2,1,0:T(8,128)(2,1)S(1)}, u32[]{:S(2)}, u32[]{:S(2)}) async-start(bf16[8,9,1664]{2,1,0:T(8,128)(2,1)} %pad_maximum_fusion), calls=%async_computation.3 | async-start | bytes 851968 | tf_op jit(solution)/shard_map/all_to_all | solution.py:197
  220.8 75.8 %all-gather.7.cloned.1.call-start = ((), (), s32[]{:S(2)}) async-start(), calls=%async_computation.6 | async-start | bytes 7241728 | tf_op jit(solution)/shard_map/all_gather | solution.py:218
  232.5 5.6 %copy-start.7 = (pred[2048]{0:T(1024)(128)(4,1)}, pred[2048]{0:T(1024)(128)(4,1)S(1)}, u32[]{:S(2)}) copy-start(pred[2048]{0:T(1024)(128)(4,1)S(1)} %iota_compare_fusion.5) | copy-start | bytes 6148
  232.6 64.0 %copy-start.11 = (bf16[3,1664,104]{1,2,0:T(8,128)(2,1)S(1)}, bf16[3,1664,104]{1,2,0:T(8,128)(2,1)}, u32[]{:S(2)}) copy-start(bf16[3,1664,104]{1,2,0:T(8,128)(2,1)} %param.28) | copy-start | bytes 3115012
  238.1 88.0 %collective-permute-start.1 = (bf16[1664,832]{0,1:T(8,128)(2,1)}, bf16[1664,832]{0,1:T(8,128)(2,1)}, u32[]{:S(2)}, u32[]{:S(2)}) collective-permute-start(bf16[1664,832]{0,1:T(8,128)(2,1)} %copy.99), channel_id=1, source_target_pairs={{0,1},{1,0},{2,3},{3,2},{4,5},{5,4},{6,7},{7,6},{8,9},{9,8},{10,11... | collective-permute-start | bytes 8306696 | tf_op jit(solution)/shard_map/ppermute | solution.py:106
  302.1 0.6 slice-start
  303.1 0.6 copy-start.8
  303.7 1.3 slice-start.1
  310.2 14.7 %copy-start.1 = (bf16[1664,832]{1,0:T(8,128)(2,1)S(1)}, bf16[1664,832]{1,0:T(8,128)(2,1)}, u32[]{:S(2)}) copy-start(bf16[1664,832]{1,0:T(8,128)(2,1)} %all-gather.5.cloned.1.call-done) | copy-start | bytes 8306692
Sparse Core Ops, SparseCore 0:
  11.7 81.4 all-gather.8
  140.9 71.0 all-gather.4
  232.0 64.5 all-gather.6

commit v8 on v6

--- a/solution.py
+++ b/solution.py
@@ -95,6 +95,31 @@
     return jnp.concatenate(outputs, axis=0).reshape(length, head_width)
 
 
+def gather_row_half(w_local):
+    half = w_local.shape[0] // 2
+    groups = lax.axis_size("grp")
+    core = lax.axis_index("grp") % 2
+    mine = lax.dynamic_slice_in_dim(w_local, core * half, half, axis=0)
+    mine_full = lax.all_gather(mine, "seq", axis=0, tiled=False)
+    return mine_full, core
+
+
+def swap_cores(mine_full):
+    groups = lax.axis_size("grp")
+    return lax.ppermute(mine_full, "grp", [(g, g ^ 1) for g in range(groups)])
+
+
+def project_row_halves(rows, mine_full, other_full, core):
+    count, half, width = mine_full.shape
+    split = rows.reshape(rows.shape[0], count, 2, half)
+    first, second = split[:, :, 0, :], split[:, :, 1, :]
+    rows_mine = jnp.where(core == 0, first, second)
+    rows_other = jnp.where(core == 0, second, first)
+    return jnp.einsum(
+        "rnh,nhd->rd", rows_mine, mine_full, preferred_element_type=jnp.float32
+    ) + jnp.einsum("rnh,nhd->rd", rows_other, other_full, preferred_element_type=jnp.float32)
+
+
 def per_device(
     patches,
     vis_gain,
@@ -116,9 +141,11 @@
     token_count = patches.shape[0]
     model_width = patches.shape[1]
     group_patches = token_count * seq_count
-    vis_out_full = lax.all_gather(vis_out, "seq", axis=0, tiled=True)
     vis_normed = layer_norm(patches, vis_gain).astype(jnp.bfloat16)
-    vis_proj = projector(vis_qkv, lax.all_gather(vis_normed, "seq", axis=0, tiled=True))
+    vis_gathered = lax.all_gather(vis_normed, "seq", axis=0, tiled=True)
+    vis_gathered, vis_out = lax.optimization_barrier((vis_gathered, vis_out))
+    vis_mine_full, core = gather_row_half(vis_out)
+    vis_proj = projector(vis_qkv, vis_gathered)
     bounds = jnp.cumsum(image_blocks[0])[:-1]
 
     def segment(indices):
@@ -131,9 +158,11 @@
 
     vis_heads = attend_local(vis_proj[0], vis_proj[1], vis_proj[2], vis_allowed)
     vis_heads, txt_out = lax.optimization_barrier((vis_heads, txt_out))
-    txt_out_full = lax.all_gather(txt_out, "seq", axis=0, tiled=True)
-    vis_attn = jnp.dot(
-        heads_to_rows(vis_heads, seq_count), vis_out_full, preferred_element_type=jnp.float32
+    txt_mine_full = gather_row_half(txt_out)[0]
+    vis_heads, vis_mine_full = lax.optimization_barrier((vis_heads, vis_mine_full))
+    vis_other_full = swap_cores(vis_mine_full)
+    vis_attn = project_row_halves(
+        heads_to_rows(vis_heads, seq_count), vis_mine_full, vis_other_full, core
     )
     residual_sum = patches.astype(jnp.float32) + vis_attn
     merged_in = (
@@ -184,7 +213,8 @@
     )
     hidden = (text_emb.astype(jnp.float32) * (1.0 - replaced) + placed).astype(jnp.bfloat16)
     txt_normed = rms_norm(hidden, txt_gain).astype(jnp.bfloat16)
-    txt_normed, txt_out_full = lax.optimization_barrier((txt_normed, txt_out_full))
+    txt_normed, txt_mine_full = lax.optimization_barrier((txt_normed, txt_mine_full))
+    txt_other_full = swap_cores(txt_mine_full)
     txt_proj = projector(txt_qkv, lax.all_gather(txt_normed, "seq", axis=0, tiled=True))
     length = prompt_len[0]
     key_positions = jnp.arange(prompt_rows * seq_count, dtype=jnp.int32)
@@ -193,8 +223,8 @@
         return (key_positions[None, :] <= row_indices[:, None]) & (key_positions[None, :] < length)
 
     txt_heads = attend_causal(txt_proj[0], txt_proj[1], txt_proj[2], txt_allowed)
-    txt_attn = jnp.dot(
-        heads_to_rows(txt_heads, seq_count), txt_out_full, preferred_element_type=jnp.float32
+    txt_attn = project_row_halves(
+        heads_to_rows(txt_heads, seq_count), txt_mine_full, txt_other_full, core
     )
     return hidden.astype(jnp.float32) + txt_attn
 

time: 322 us -> 335 us (1.040)
  local copies, waits for them, and re-layouts: 6.74 us -> 15.8 us
  matrix products: 34.8 us -> 39.9 us
  blocking collectives: 34.5 us -> 30.1 us
  waiting for transfers between devices: 199 us -> 203 us
    all_to_all x1, waiting for transfers between devices: 0.01 us -> 10.3 us  [heads_to_rows(): lax.all_to_all(blocks, 'seq', split_axis=0, concat_axis=0, tiled=True)]
    optimization_barrier x0 -> x2, local copies, waits for them, and re-layouts: none -> 7.51 us  [the longest x1 3.77 us: per_device(): lax.optimization_barrier((txt_normed, txt_mine_full))]
    dot_general x2 -> x4, matrix products: 5.66 us -> 10.9 us  [the longest x2 6.02 us: project_row_halves(): jnp.einsum('rnh,nhd->rd', rows_other, other_full, preferred_element_type=...]
    all_to_all x1, blocking collectives: 19 us -> 14.8 us  [per_device(): lax.all_to_all(merged_in, 'seq', split_axis=1, concat_axis=0, tiled=True)]
    all_gather x1, waiting for transfers between devices: 58.3 us -> 54.4 us  [per_device(): lax.all_gather(txt_normed, 'seq', axis=0, tiled=True)]
  transfers between devices with their start and end apart: 7 -> 9, of which waited for: 5 -> 6; matrix products, arithmetic and copies ran while one was open for 12% -> 16% of each run, Pallas kernels for 0% -> 0%
where the time goes in v8:
time: 335 us; the launch traced here: 334 us
  waiting for transfers between devices  203 us (61%)
  matrix products  39.9 us (12%)
  blocking collectives  30.1 us (9%)
  other arithmetic  18.8 us (6%)
  local copies, waits for them, and re-layouts  15.8 us (5%)
  between operations  14.2 us (4%)
  starting transfers between devices  13.1 us (4%)
    all_gather x1, waiting for transfers between devices, per_device(): vis_gathered = lax.all_gather(vis_normed, 'seq', axis=0, tiled=True)  65.2 us
    all_gather x1, waiting for transfers between devices, per_device(): lax.all_gather(txt_normed, 'seq', axis=0, tiled=True)  54.4 us
    all_to_all x1, waiting for transfers between devices, per_device(): lax.all_to_all(merge_partial.astype(jnp.bfloat16).reshape(seq_count, -1,...  32.8 us
    all_gather x2, waiting for transfers between devices, gather_row_half(): mine_full = lax.all_gather(mine, 'seq', axis=0, tiled=False)  30.7 us
    all_to_all x1, blocking collectives, heads_to_rows(): lax.all_to_all(blocks, 'seq', split_axis=0, concat_axis=0, tiled=True)  15.3 us
    all_to_all x1, blocking collectives, per_device(): lax.all_to_all(merged_in, 'seq', split_axis=1, concat_axis=0, tiled=True)  14.8 us
    unnamed x2, matrix products  11.1 us
    all_to_all x1, waiting for transfers between devices, heads_to_rows(): lax.all_to_all(blocks, 'seq', split_axis=0, concat_axis=0, tiled=True)  10.3 us
  transfers between devices with their start and end apart: 9, of which 6 were waited for; matrix products, arithmetic and copies ran while one was open for 16% of the time, Pallas kernels for 0%

profile of v8, /device:TPU:0, one launch (start us, length us, event | category | flops | bytes accessed | tf_op | source)
XLA Modules:
  0.0 334.4 jit_solution(6242521302651415674)
XLA Ops:
  6.5 1.3 convert_reduce_fusion.1
  7.8 1.3 fusion.39
  9.1 2.1 fusion.41
  11.2 0.8 reduce-window.4
  12.2 65.2 %all-gather.9.cloned.1.call-done = bf16[2048,1664]{1,0:T(8,128)(2,1)} async-done(((bf16[128,1664]{1,0:T(8,128)(2,1)}), bf16[2048,1664]{1,0:T(8,128)(2,1)}) %all-gather.9.cloned.1.call-update) | async-done | bytes 6815760 | tf_op jit(solution)/shard_map/all_gather | solution.py:145
  77.4 5.7 %fusion.83 = f32[2048,312]{0,1:S(1)} fusion(bf16[2048,1664]{1,0:T(8,128)(2,1)} %all-gather.9.cloned.1.call-done, bf16[1664,312]{0,1:T(8,128)(2,1)} %bitcast.224), kind=kOutput, calls=%fused_computation.172 | convolution fusion | flops 2126512128 | bytes 10409984
  83.7 1.7 dynamic-slice_bitcast_fusion.1
  85.4 16.0 %while.12 = (s32[]{:T(128)}, bf16[4,512,1,104]{1,3,2,0:T(8,128)(2,1)S(1)}, s32[4]{0:T(128)S(1)}, s32[3]{0:T(128)S(1)}, s32[2048]{0:T(1024)S(1)}, /*index=5*/bf16...) while((s32[]{:T(128)}, ...), condition=%wide.region_10.11_spmd, body=%wide.region_6.10_spmd.sunk | while | flops 445709312 | bytes 13674633 | solution.py:57
  85.4 0.6 dynamic_slice.33
  86.0 0.6 add_select_fusion.3
  86.6 1.0 fusion.101
  87.6 0.7 fusion.102
  88.3 1.1 fusion.103
  89.4 0.6 dynamic_slice.33
  90.0 0.6 add_select_fusion.3
  90.6 1.0 fusion.101
  91.6 0.7 fusion.102
  92.3 1.1 fusion.103
  93.4 0.6 dynamic_slice.33
  94.0 0.6 add_select_fusion.3
  94.6 1.0 fusion.101
  95.6 0.7 fusion.102
  96.3 1.1 fusion.103
  97.4 0.6 dynamic_slice.33
  98.0 0.6 add_select_fusion.3
  98.6 1.0 fusion.101
  99.6 0.7 fusion.102
  100.3 1.1 fusion.103
  101.7 30.7 %all-gather.13.cloned.1.call-done = bf16[16,52,1664]{2,1,0:T(8,128)(2,1)} async-done(((bf16[1,52,1664]{2,1,0:T(8,128)(2,1)}), bf16[16,52,1664]{2,1,0:T(8,128)(2,1)}) %all-gather.13.cloned.1.call-update) | async-done | bytes 2768912 | tf_op jit(solution)/shard_map/all_gather | solution.py:103
  132.4 3.7 %copy.51 = bf16[16,52,1664]{2,0,1:T(8,128)(2,1)} copy(bf16[16,52,1664]{2,1,0:T(8,128)(2,1)} %all-gather.13.cloned.1.call-done) | data formatting | bytes 5537792 | tf_op jit(solution)/shard_map/optimization_barrier | solution.py:162
  136.2 0.8 copy_bitcast_fusion
  137.0 4.5 %all-to-all-start = ((bf16[16,128,104]{1,2,0:T(8,128)(2,1)}), bf16[16,128,104]{1,2,0:T(8,128)(2,1)S(1)}, u32[]{:S(2)}, u32[]{:S(2)}) async-start(bf16[16,128,104]{1,2,0:T(8,128)(2,1)} %copy_bitcast_fusion), calls=%async_computation | async-start | bytes 851968 | tf_op jit(solution)/shard_map/all_to_all | solution.py:65
  141.5 0.7 dynamic-slice_bitcast_fusion
  142.3 10.3 %all-to-all-done = bf16[16,128,104]{1,2,0:T(8,128)(2,1)S(1)} async-done(((bf16[16,128,104]{1,2,0:T(8,128)(2,1)}), bf16[16,128,104]{1,2,0:T(8,128)(2,1)S(1)}, u32[]{:S(2)}, u32[]{:S(2)}) %all-to-all-start) | async-done | bytes 426016 | tf_op jit(solution)/shard_map/all_to_all | solution.py:65
  152.7 2.5 convolution_bitcast_fusion.3
  155.2 2.6 fusion.78
  158.3 0.6 all_to_all.27
  159.2 14.8 %all_to_all.39 = bf16[32,16,416]{2,0,1:T(8,128)(2,1)S(1)} all-to-all(bf16[32,16,416]{2,0,1:T(8,128)(2,1)S(1)} %copy.53), channel_id=1, replica_groups=mesh['seq'=16,'grp'=8] {'seq'}, dimensions={1} | all-to-all | bytes 851968 | tf_op jit(solution)/shard_map/all_to_all | solution.py:173
  174.0 2.3 convolution_convert_fusion
  176.3 3.9 %all-to-all-start.2 = ((bf16[16,32,1664]{2,1,0:T(8,128)(2,1)}), bf16[16,32,1664]{2,1,0:T(8,128)(2,1)S(1)}, u32[]{:S(2)}, u32[]{:S(2)}) async-start(bf16[16,32,1664]{2,1,0:T(8,128)(2,1)} %bitcast.211), calls=%async_computation.2 | async-start | bytes 3407872 | tf_op jit(solution)/shard_map/all_to_all | solution.py:175
  180.3 0.8 select_reduce_fusion
  181.2 0.7 iota_compare_fusion.5
  182.0 0.7 copy.54
  182.6 32.8 %all-to-all-done.2 = bf16[16,32,1664]{2,1,0:T(8,128)(2,1)S(1)} async-done(((bf16[16,32,1664]{2,1,0:T(8,128)(2,1)}), bf16[16,32,1664]{2,1,0:T(8,128)(2,1)S(1)}, u32[]{:S(2)}, u32[]{:S(2)}) %all-to-all-start.2) | async-done | bytes 1703968 | tf_op jit(solution)/shard_map/all_to_all | solution.py:175
  215.4 0.9 reduce_sum.159
  216.3 1.1 convolution_convert_fusion.1
  217.4 1.6 pad_maximum_fusion
  219.0 4.5 %all-to-all-start.3 = ((bf16[8,9,1664]{2,1,0:T(8,128)(2,1)}), bf16[8,9,1664]{2,1,0:T(8,128)(2,1)S(1)}, u32[]{:S(2)}, u32[]{:S(2)}) async-start(bf16[8,9,1664]{2,1,0:T(8,128)(2,1)} %pad_maximum_fusion), calls=%async_computation.3 | async-start | bytes 851968 | tf_op jit(solution)/shard_map/all_to_all | solution.py:197
  223.7 9.0 %all-to-all-done.3 = bf16[8,9,1664]{2,1,0:T(8,128)(2,1)S(1)} async-done(((bf16[8,9,1664]{2,1,0:T(8,128)(2,1)}), bf16[8,9,1664]{2,1,0:T(8,128)(2,1)S(1)}, u32[]{:S(2)}, u32[]{:S(2)}) %all-to-all-start.3) | async-done | bytes 239648 | tf_op jit(solution)/shard_map/all_to_all | solution.py:197
  233.0 0.5 multiply_reduce_fusion
  233.5 0.9 multiply_convert_fusion
  235.1 3.8 %copy.60 = bf16[16,52,1664]{2,0,1:T(8,128)(2,1)} copy(bf16[16,52,1664]{2,1,0:T(8,128)(2,1)} %all-gather.15.cloned.1.call-done) | data formatting | bytes 5537792 | tf_op jit(solution)/shard_map/optimization_barrier | solution.py:216
  238.9 54.4 %all-gather.11.cloned.1.call-done = bf16[2048,1664]{1,0:T(8,128)(2,1)} async-done(((bf16[128,1664]{1,0:T(8,128)(2,1)}), bf16[2048,1664]{1,0:T(8,128)(2,1)}) %all-gather.11.cloned.1.call-update) | async-done | bytes 6815760 | tf_op jit(solution)/shard_map/all_gather | solution.py:218
  293.3 5.5 %fusion.84 = f32[2048,312]{0,1:S(1)} fusion(bf16[2048,1664]{1,0:T(8,128)(2,1)} %all-gather.11.cloned.1.call-done, bf16[1664,312]{0,1:T(8,128)(2,1)S(1)} %bitcast.225), kind=kOutput, calls=%fused_computation.173 | convolution fusion | flops 2126512128 | bytes 10409984
  299.0 1.4 fusion.79
  301.2 1.0 fusion.80
  302.3 0.5 fusion.17
  302.7 0.7 fusion.81
  303.8 0.6 fusion.14
  304.9 0.6 fusion.32
  305.6 0.8 fusion.31
  306.6 15.3 %all_to_all.40 = bf16[16,128,104]{1,2,0:T(8,128)(2,1)S(1)} all-to-all(bf16[16,128,104]{1,2,0:T(8,128)(2,1)S(1)} %copy.58), channel_id=1, replica_groups=mesh['seq'=16,'grp'=8] {'seq'}, dimensions={0} | all-to-all | bytes 851968 | tf_op jit(solution)/shard_map/all_to_all | solution.py:65
  322.0 2.5 convolution_bitcast_fusion.1
  324.5 3.4 %fusion.21 = f32[128,1664]{1,0:T(8,128)} fusion(f32[128,1664]{1,0:T(8,128)S(1)} %get-tuple-element.180, f32[128,1664]{1,0:T(8,128)S(1)} %convolution_bitcast_fusion.1, bf16[16,52,1664]{2,0,1:T(8,128)(2,1)} %collective-permute-done.1, pred[]{:T(512)S(6)} %eq.111, bf16[128,16,2,52]{0,1,3,2:T(8,128)(2,1)S(1)} %bitcast.218), kind=kOutput, calls=%fused_computation.45 | convolution fusion | flops 354951168 | bytes 5750785 | tf_op jit(solution)/shard_map/rnh,nhd->rd/dot_general | solution.py:120
  (80 shorter events, 5.3 us)
Async XLA Ops:
  6.5 167.5 %copy-start = (bf16[416,1664]{1,0:T(8,128)(2,1)S(1)}, bf16[416,1664]{1,0:T(8,128)(2,1)}, u32[]{:S(2)}) copy-start(bf16[416,1664]{1,0:T(8,128)(2,1)} %param.21) | copy-start | bytes 4153348
  6.5 70.8 %all-gather.9.cloned.1.call-start = ((), (), s32[]{:S(2)}) async-start(), calls=%async_computation.5 | async-start | bytes 7241728 | tf_op jit(solution)/shard_map/all_gather | solution.py:145
  11.2 121.2 %all-gather.13.cloned.1.call-start = ((), (), s32[]{:S(2)}) async-start(), calls=%async_computation.7 | async-start | bytes 3168256 | tf_op jit(solution)/shard_map/all_gather | solution.py:103
  101.7 39.8 %copy-start.3 = (bf16[104,1664]{1,0:T(8,128)(2,1)S(1)}, bf16[104,1664]{1,0:T(8,128)(2,1)}, u32[]{:S(2)}) copy-start(bf16[104,1664]{1,0:T(8,128)(2,1)} %param.29) | copy-start | bytes 1038340
  136.2 19.0 %collective-permute-start = (bf16[16,52,1664]{2,0,1:T(8,128)(2,1)}, bf16[16,52,1664]{2,0,1:T(8,128)(2,1)}, u32[]{:S(2)}, u32[]{:S(2)}) collective-permute-start(bf16[16,52,1664]{2,0,1:T(8,128)(2,1)} %copy.51), channel_id=1, source_target_pairs={{0,1},{1,0},{2,3},{3,2},{4,5},{5,4},{6,7},{7,6},{8,9},{9,8},{10,11... | collective-permute-start | bytes 8306696 | tf_op jit(solution)/shard_map/ppermute | solution.py:109
  137.0 15.6 %all-to-all-start = ((bf16[16,128,104]{1,2,0:T(8,128)(2,1)}), bf16[16,128,104]{1,2,0:T(8,128)(2,1)S(1)}, u32[]{:S(2)}, u32[]{:S(2)}) async-start(bf16[16,128,104]{1,2,0:T(8,128)(2,1)} %copy_bitcast_fusion), calls=%async_computation | async-start | bytes 851968 | tf_op jit(solution)/shard_map/all_to_all | solution.py:65
  141.5 13.7 %copy-start.1 = (bf16[128,1664]{1,0:T(8,128)(2,1)S(1)}, bf16[128,1664]{1,0:T(8,128)(2,1)}, u32[]{:S(2)}) copy-start(bf16[128,1664]{1,0:T(8,128)(2,1)} %param.16) | copy-start | bytes 1277956
  141.5 92.9 %all-gather.15.cloned.1.call-start = ((), (), s32[]{:S(2)}) async-start(), calls=%async_computation.8 | async-start | bytes 3168256 | tf_op jit(solution)/shard_map/all_gather | solution.py:103
  155.1 2.9 copy-start.4
  176.3 3.9 %copy-start.6 = (s32[32,1]{0,1:T(1,128)S(1)}, s32[32,1]{0,1:T(1,128)}, u32[]{:S(2)}) copy-start(s32[32,1]{0,1:T(1,128)} %param.23) | copy-start | bytes 388
  176.3 39.1 %all-to-all-start.2 = ((bf16[16,32,1664]{2,1,0:T(8,128)(2,1)}), bf16[16,32,1664]{2,1,0:T(8,128)(2,1)S(1)}, u32[]{:S(2)}, u32[]{:S(2)}) async-start(bf16[16,32,1664]{2,1,0:T(8,128)(2,1)} %bitcast.211), calls=%async_computation.2 | async-start | bytes 3407872 | tf_op jit(solution)/shard_map/all_to_all | solution.py:175
  180.2 52.8 %copy-start.2 = (bf16[128,1664]{1,0:T(8,128)(2,1)S(1)}, bf16[128,1664]{1,0:T(8,128)(2,1)}, u32[]{:S(2)}) copy-start(bf16[128,1664]{1,0:T(8,128)(2,1)} %param.26) | copy-start | bytes 1277956
  180.2 53.3 %copy-start.5 = (f32[1664]{0:T(1024)S(1)}, f32[1664]{0:T(1024)}, u32[]{:S(2)}) copy-start(f32[1664]{0:T(1024)} %param.27) | copy-start | bytes 19972
  180.3 43.4 %copy-start.8 = (s32[1,1,128]{2,1,0:T(1,128)S(1)}, s32[1,1,128]{2,1,0:T(1,128)}, u32[]{:S(2)}) copy-start(s32[1,1,128]{2,1,0:T(1,128)} %param.24) | copy-start | bytes 1540
  219.0 13.7 %all-to-all-start.3 = ((bf16[8,9,1664]{2,1,0:T(8,128)(2,1)}), bf16[8,9,1664]{2,1,0:T(8,128)(2,1)S(1)}, u32[]{:S(2)}, u32[]{:S(2)}) async-start(bf16[8,9,1664]{2,1,0:T(8,128)(2,1)} %pad_maximum_fusion), calls=%async_computation.3 | async-start | bytes 851968 | tf_op jit(solution)/shard_map/all_to_all | solution.py:197
  223.5 69.8 %all-gather.11.cloned.1.call-start = ((), (), s32[]{:S(2)}) async-start(), calls=%async_computation.6 | async-start | bytes 7241728 | tf_op jit(solution)/shard_map/all_gather | solution.py:218
  235.1 58.2 %copy-start.7 = (bf16[3,1664,104]{1,2,0:T(8,128)(2,1)S(1)}, bf16[3,1664,104]{1,2,0:T(8,128)(2,1)}, u32[]{:S(2)}) copy-start(bf16[3,1664,104]{1,2,0:T(8,128)(2,1)} %param.28) | copy-start | bytes 3115012
  238.9 85.5 %collective-permute-start.1 = (bf16[16,52,1664]{2,0,1:T(8,128)(2,1)}, bf16[16,52,1664]{2,0,1:T(8,128)(2,1)}, u32[]{:S(2)}, u32[]{:S(2)}) collective-permute-start(bf16[16,52,1664]{2,0,1:T(8,128)(2,1)} %copy.60), channel_id=1, source_target_pairs={{0,1},{1,0},{2,3},{3,2},{4,5},{5,4},{6,7},{7,6},{8,9},{9,8},{10,11... | collective-permute-start | bytes 8306696 | tf_op jit(solution)/shard_map/ppermute | solution.py:109
Sparse Core Ops, SparseCore 0:
  11.3 66.0 all-gather.8
  85.5 46.8 all-gather.12
  144.4 70.0 all-gather.14
  234.5 58.7 all-gather.10

commit v9 on v6

--- a/solution.py
+++ b/solution.py
@@ -95,6 +95,26 @@
     return jnp.concatenate(outputs, axis=0).reshape(length, head_width)
 
 
+def split_gather(rows_local, seq_count):
+    first = rows_local.shape[0] * 5 // 8 // 16 * 16
+    gathered = lax.all_gather(rows_local[:first], "seq", axis=0, tiled=False)
+    rest = rows_local[first:]
+    copies = jnp.broadcast_to(rest[None], (seq_count,) + rest.shape)
+    exchanged = lax.all_to_all(copies, "seq", split_axis=0, concat_axis=0, tiled=True)
+    return gathered, exchanged
+
+
+def split_project(weights, pieces):
+    outs = [
+        jnp.einsum("srd,kde->ksre", piece, weights, preferred_element_type=jnp.float32).astype(
+            jnp.bfloat16
+        )
+        for piece in pieces
+    ]
+    joined = jnp.concatenate(outs, axis=2)
+    return joined.reshape(joined.shape[0], -1, joined.shape[-1])
+
+
 def per_device(
     patches,
     vis_gain,
@@ -118,7 +138,7 @@
     group_patches = token_count * seq_count
     vis_out_full = lax.all_gather(vis_out, "seq", axis=0, tiled=True)
     vis_normed = layer_norm(patches, vis_gain).astype(jnp.bfloat16)
-    vis_proj = projector(vis_qkv, lax.all_gather(vis_normed, "seq", axis=0, tiled=True))
+    vis_proj = split_project(vis_qkv, split_gather(vis_normed, seq_count))
     bounds = jnp.cumsum(image_blocks[0])[:-1]
 
     def segment(indices):
@@ -185,7 +205,7 @@
     hidden = (text_emb.astype(jnp.float32) * (1.0 - replaced) + placed).astype(jnp.bfloat16)
     txt_normed = rms_norm(hidden, txt_gain).astype(jnp.bfloat16)
     txt_normed, txt_out_full = lax.optimization_barrier((txt_normed, txt_out_full))
-    txt_proj = projector(txt_qkv, lax.all_gather(txt_normed, "seq", axis=0, tiled=True))
+    txt_proj = split_project(txt_qkv, split_gather(txt_normed, seq_count))
     length = prompt_len[0]
     key_positions = jnp.arange(prompt_rows * seq_count, dtype=jnp.int32)
 

time: 322 us -> 343 us (1.065)
  blocking collectives: 34.5 us -> 56.1 us
  waiting for transfers between devices: 199 us -> 181 us
  matrix products: 34.8 us -> 43.7 us
  starting transfers between devices: 13.8 us -> 20.5 us
  local copies, waits for them, and re-layouts: 6.74 us -> 10.9 us
  other arithmetic: 19.2 us -> 15.4 us
    all_gather x2, waiting for transfers between devices: 123 us -> 37.1 us  [split_gather(): gathered = lax.all_gather(rows_local[:first], 'seq', axis=0, tiled=False)]
    all_to_all x1 -> x2, waiting for transfers between devices: 0.01 us -> 84.9 us  [split_gather(): lax.all_to_all(copies, 'seq', split_axis=0, concat_axis=0, tiled=True)]
    all_to_all x1 -> x2, blocking collectives: 15.5 us -> 36.3 us  [heads_to_rows(): lax.all_to_all(blocks, 'seq', split_axis=0, concat_axis=0, tiled=True)]
    all_gather x1, waiting for transfers between devices: 31.9 us -> 14.1 us  [per_device(): vis_out_full = lax.all_gather(vis_out, 'seq', axis=0, tiled=True)]
    dot_general x0 -> x4, matrix products: none -> 16 us  [split_project(): jnp.einsum('srd,kde->ksre', piece, weights, preferred_element_type=jnp.fl...]
    unnamed x2 -> x0, matrix products: 11.3 us -> none
    all_to_all x1 -> x2, starting transfers between devices: 5.25 us -> 11.9 us  [split_gather(): lax.all_to_all(copies, 'seq', split_axis=0, concat_axis=0, tiled=True)]
  transfers between devices with their start and end apart: 7 -> 8, of which waited for: 5 -> 7; matrix products, arithmetic and copies ran while one was open for 12% -> 14% of each run, Pallas kernels for 0% -> 0%
where the time goes in v9:
time: 343 us; the launch traced here: 342 us
  waiting for transfers between devices  181 us (53%)
  blocking collectives  56.1 us (16%)
  matrix products  43.7 us (13%)
  starting transfers between devices  20.5 us (6%)
  other arithmetic  15.4 us (4%)
  between operations  14.2 us (4%)
  local copies, waits for them, and re-layouts  10.9 us (3%)
    all_to_all x2, waiting for transfers between devices, split_gather(): lax.all_to_all(copies, 'seq', split_axis=0, concat_axis=0, tiled=True)  84.9 us
    all_gather x2, waiting for transfers between devices, split_gather(): gathered = lax.all_gather(rows_local[:first], 'seq', axis=0, tiled=False)  37.1 us
    all_to_all x2, blocking collectives, heads_to_rows(): lax.all_to_all(blocks, 'seq', split_axis=0, concat_axis=0, tiled=True)  36.3 us
    all_to_all x1, waiting for transfers between devices, per_device(): lax.all_to_all(merge_partial.astype(jnp.bfloat16).reshape(seq_count, -1,...  34.8 us
    all_to_all x1, blocking collectives, per_device(): lax.all_to_all(merged_in, 'seq', split_axis=1, concat_axis=0, tiled=True)  19.7 us
    dot_general x4, matrix products, split_project(): jnp.einsum('srd,kde->ksre', piece, weights, preferred_element_type=jnp.fl...  16 us
    all_gather x1, waiting for transfers between devices, per_device(): vis_out_full = lax.all_gather(vis_out, 'seq', axis=0, tiled=True)  14.1 us
    all_to_all x2, starting transfers between devices, split_gather(): lax.all_to_all(copies, 'seq', split_axis=0, concat_axis=0, tiled=True)  11.9 us
  transfers between devices with their start and end apart: 8, of which 7 were waited for; matrix products, arithmetic and copies ran while one was open for 14% of the time, Pallas kernels for 0%

profile of v9, /device:TPU:0, one launch (start us, length us, event | category | flops | bytes accessed | tf_op | source)
XLA Modules:
  0.0 341.6 jit_solution(3104415055626663953)
XLA Ops:
  6.5 1.3 convert_reduce_fusion.1
  7.8 1.3 fusion.57
  9.1 1.3 fusion.59
  10.4 0.7 slice.135
  11.2 0.7 all-gather.7.cloned.1.call-update
  11.9 1.7 broadcast_in_dim.39
  13.6 7.3 %all-to-all-start = ((bf16[16,48,1664]{2,1,0:T(8,128)(2,1)}), bf16[16,48,1664]{2,1,0:T(8,128)(2,1)}, u32[]{:S(2)}, u32[]{:S(2)}) async-start(bf16[16,48,1664]{2,1,0:T(8,128)(2,1)} %broadcast_in_dim.39), calls=%async_computation | async-start | bytes 5111808 | tf_op jit(solution)/shard_map/all_to_all | solution.py:103
  21.2 0.7 convert_reduce_fusion.3
  21.9 41.9 %all-to-all-done = bf16[16,48,1664]{2,1,0:T(8,128)(2,1)} async-done(((bf16[16,48,1664]{2,1,0:T(8,128)(2,1)}), bf16[16,48,1664]{2,1,0:T(8,128)(2,1)}, u32[]{:S(2)}, u32[]{:S(2)}) %all-to-all-start) | async-done | bytes 2555936 | tf_op jit(solution)/shard_map/all_to_all | solution.py:103
  63.8 3.3 fusion.40
  67.1 20.5 %all-gather.11.cloned.1.call-done = bf16[1280,1664]{1,0:T(8,128)(2,1)} async-done(((bf16[80,1664]{1,0:T(8,128)(2,1)}), bf16[1280,1664]{1,0:T(8,128)(2,1)}) %all-gather.11.cloned.1.call-update) | async-done | bytes 4259856 | tf_op jit(solution)/shard_map/all_gather | solution.py:100
  87.6 4.7 %fusion.29 = bf16[3,16,80,104]{3,2,0,1:T(8,128)(2,1)S(1)} fusion(bf16[16,80,1664,1]{2,1,3,0:T(8,128)(2,1)} %bitcast.204, bf16[3,1664,104]{1,2,0:T(8,128)(2,1)S(1)} %copy-done.9), kind=kOutput, calls=%fused_computation.85 | convolution fusion | flops 1329469440 | bytes 6096896 | tf_op jit(solution)/shard_map/srd,kde->ksre/dot_general | solution.py:109
  92.3 0.4 pad_maximum_fusion.1
  93.4 21.8 %while.12 = (s32[]{:T(128)}, bf16[4,512,1,104]{1,3,2,0:T(8,128)(2,1)}, s32[4]{0:T(128)S(1)}, s32[3]{0:T(128)S(1)}, s32[2048]{0:T(1024)}, /*index=5*/bf16[4,512,1...) while((s32[]{:T(128)}, ...), condition=%wide.region_10.11_spmd, body=%wide.region_6.10_spmd.sunk | while | flops 445709312 | bytes 13675133 | solution.py:57
  93.5 0.6 dynamic_slice.23
  94.1 0.6 add_select_fusion.3
  94.8 1.7 fusion.120
  96.5 0.7 fusion.121
  97.2 1.7 fusion.122
  98.9 0.6 dynamic_slice.23
  99.5 0.6 add_select_fusion.3
  100.2 1.7 fusion.120
  101.9 0.7 fusion.121
  102.6 1.7 fusion.122
  104.3 0.6 dynamic_slice.23
  104.9 0.6 add_select_fusion.3
  105.7 1.7 fusion.120
  107.4 0.7 fusion.121
  108.1 1.7 fusion.122
  109.8 0.6 dynamic_slice.23
  110.4 0.6 add_select_fusion.3
  111.1 1.7 fusion.120
  112.8 0.7 fusion.121
  113.5 1.7 fusion.122
  115.2 1.3 copy.35
  116.7 20.9 %all_to_all.49 = bf16[16,128,104]{1,2,0:T(8,128)(2,1)S(1)} all-to-all(bf16[16,128,104]{1,2,0:T(8,128)(2,1)S(1)} %copy_bitcast_fusion), channel_id=1, replica_groups=mesh['seq'=16,'grp'=8] {'seq'}, dimensions={0} | all-to-all | bytes 851968 | tf_op jit(solution)/shard_map/all_to_all | solution.py:65
  137.6 14.1 %all-gather.7.cloned.1.call-done = bf16[1664,1664]{1,0:T(8,128)(2,1)} async-done(((bf16[104,1664]{1,0:T(8,128)(2,1)}), bf16[1664,1664]{1,0:T(8,128)(2,1)}) %all-gather.7.cloned.1.call-update) | async-done | bytes 5537808 | tf_op jit(solution)/shard_map/all_gather | solution.py:139
  151.6 3.7 %fusion.89 = (f32[128]{0:T(128)S(1)}, f32[128,1664]{1,0:T(8,128)S(1)}) fusion(bf16[128,1664]{0,1:T(8,128)(2,1)S(1)} %bitcast.181, bf16[1664,1664]{1,0:T(8,128)(2,1)} %all-gather.7.cloned.1.call-done, bf16[128,1664]{1,0:T(8,128)(2,1)S(1)} %copy-done.2), kind=kOutput, calls=%fused_computation.180 | convolution fusion | flops 709476224 | bytes 7242240 | tf_op jit(solution)/shard_map/dot_general | solution.py:155
  155.8 0.6 all_to_all.34
  156.7 19.7 %all_to_all.50 = bf16[32,16,416]{2,0,1:T(8,128)(2,1)S(1)} all-to-all(bf16[32,16,416]{2,0,1:T(8,128)(2,1)S(1)} %copy.37), channel_id=1, replica_groups=mesh['seq'=16,'grp'=8] {'seq'}, dimensions={1} | all-to-all | bytes 851968 | tf_op jit(solution)/shard_map/all_to_all | solution.py:164
  176.4 2.3 convolution_convert_fusion
  178.8 4.0 %all-to-all-start.3 = ((bf16[16,32,1664]{2,1,0:T(8,128)(2,1)}), bf16[16,32,1664]{2,1,0:T(8,128)(2,1)S(1)}, u32[]{:S(2)}, u32[]{:S(2)}) async-start(bf16[16,32,1664]{2,1,0:T(8,128)(2,1)} %bitcast.182), calls=%async_computation.3 | async-start | bytes 3407872 | tf_op jit(solution)/shard_map/all_to_all | solution.py:166
  183.3 34.8 %all-to-all-done.3 = bf16[16,32,1664]{2,1,0:T(8,128)(2,1)S(1)} async-done(((bf16[16,32,1664]{2,1,0:T(8,128)(2,1)}), bf16[16,32,1664]{2,1,0:T(8,128)(2,1)S(1)}, u32[]{:S(2)}, u32[]{:S(2)}) %all-to-all-start.3) | async-done | bytes 1703968 | tf_op jit(solution)/shard_map/all_to_all | solution.py:166
  218.5 0.8 pad_maximum_fusion.2
  219.3 4.5 %all-to-all-start.4 = ((bf16[8,9,1664]{2,1,0:T(8,128)(2,1)}), bf16[8,9,1664]{2,1,0:T(8,128)(2,1)S(1)}, u32[]{:S(2)}, u32[]{:S(2)}) async-start(bf16[8,9,1664]{2,1,0:T(8,128)(2,1)} %pad_maximum_fusion.2), calls=%async_computation.4 | async-start | bytes 851968 | tf_op jit(solution)/shard_map/all_to_all | solution.py:188
  223.9 9.2 %all-to-all-done.4 = bf16[8,9,1664]{2,1,0:T(8,128)(2,1)S(1)} async-done(((bf16[8,9,1664]{2,1,0:T(8,128)(2,1)}), bf16[8,9,1664]{2,1,0:T(8,128)(2,1)S(1)}, u32[]{:S(2)}, u32[]{:S(2)}) %all-to-all-start.4) | async-done | bytes 239648 | tf_op jit(solution)/shard_map/all_to_all | solution.py:188
  233.3 0.5 multiply_reduce_fusion
  234.0 0.7 slice.118
  234.8 1.7 broadcast_in_dim.41
  236.4 4.6 %all-to-all-start.5 = ((bf16[16,48,1664]{2,1,0:T(8,128)(2,1)}), bf16[16,48,1664]{2,1,0:T(8,128)(2,1)}, u32[]{:S(2)}, u32[]{:S(2)}) async-start(bf16[16,48,1664]{2,1,0:T(8,128)(2,1)} %broadcast_in_dim.41), calls=%async_computation.5 | async-start | bytes 5111808 | tf_op jit(solution)/shard_map/all_to_all | solution.py:103
  241.7 42.9 %all-to-all-done.5 = bf16[16,48,1664]{2,1,0:T(8,128)(2,1)} async-done(((bf16[16,48,1664]{2,1,0:T(8,128)(2,1)}), bf16[16,48,1664]{2,1,0:T(8,128)(2,1)}, u32[]{:S(2)}, u32[]{:S(2)}) %all-to-all-start.5) | async-done | bytes 2555936 | tf_op jit(solution)/shard_map/all_to_all | solution.py:103
  284.7 3.3 fusion.37
  288.0 16.6 %all-gather.13.cloned.1.call-done = bf16[1280,1664]{1,0:T(8,128)(2,1)} async-done(((bf16[80,1664]{1,0:T(8,128)(2,1)}), bf16[1280,1664]{1,0:T(8,128)(2,1)}) %all-gather.13.cloned.1.call-update) | async-done | bytes 4259856 | tf_op jit(solution)/shard_map/all_gather | solution.py:100
  304.6 4.7 %fusion.30 = bf16[3,16,80,104]{3,2,0,1:T(8,128)(2,1)S(1)} fusion(bf16[16,80,1664,1]{2,1,3,0:T(8,128)(2,1)} %bitcast.205, bf16[3,1664,104]{1,2,0:T(8,128)(2,1)S(1)} %copy-done.10), kind=kOutput, calls=%fused_computation.86 | convolution fusion | flops 1329469440 | bytes 6096896 | tf_op jit(solution)/shard_map/srd,kde->ksre/dot_general | solution.py:109
  310.9 0.7 fusion.92
  311.9 0.5 fusion.48
  312.6 0.9 fusion.91
  313.5 0.5 fusion.17
  314.0 0.7 fusion.47
  314.7 1.2 fusion.90
  315.9 0.6 fusion.14
  316.5 0.8 fusion.45
  317.6 15.5 %all_to_all.51 = bf16[16,128,104]{1,2,0:T(8,128)(2,1)S(1)} all-to-all(bf16[16,128,104]{1,2,0:T(8,128)(2,1)S(1)} %copy.42), channel_id=1, replica_groups=mesh['seq'=16,'grp'=8] {'seq'}, dimensions={0} | all-to-all | bytes 851968 | tf_op jit(solution)/shard_map/all_to_all | solution.py:65
  333.1 1.9 convolution_add_fusion
  (97 shorter events, 6.0 us)
Async XLA Ops:
  6.5 169.9 %copy-start = (bf16[416,1664]{1,0:T(8,128)(2,1)S(1)}, bf16[416,1664]{1,0:T(8,128)(2,1)}, u32[]{:S(2)}) copy-start(bf16[416,1664]{1,0:T(8,128)(2,1)} %param.21) | copy-start | bytes 4153348
  6.5 81.1 %all-gather.11.cloned.1.call-start = ((), (), s32[]{:S(2)}) async-start(), calls=%async_computation.9 | async-start | bytes 4526080 | tf_op jit(solution)/shard_map/all_gather | solution.py:100
  11.2 140.5 %all-gather.7.cloned.1.call-start = ((), (), s32[]{:S(2)}) async-start(), calls=%async_computation.7 | async-start | bytes 5883904 | tf_op jit(solution)/shard_map/all_gather | solution.py:139
  13.6 7.4 %copy-start.11 = (s32[1,4]{1,0:T(1,128)S(1)}, s32[1,4]{1,0:T(1,128)}, u32[]{:S(2)}) copy-start(s32[1,4]{1,0:T(1,128)} %param.22) | copy-start | bytes 52
  13.6 50.2 %copy-start.9 = (bf16[3,1664,104]{1,2,0:T(8,128)(2,1)S(1)}, bf16[3,1664,104]{1,2,0:T(8,128)(2,1)}, u32[]{:S(2)}) copy-start(bf16[3,1664,104]{1,2,0:T(8,128)(2,1)} %param.18) | copy-start | bytes 3115012
  13.6 50.2 %all-to-all-start = ((bf16[16,48,1664]{2,1,0:T(8,128)(2,1)}), bf16[16,48,1664]{2,1,0:T(8,128)(2,1)}, u32[]{:S(2)}, u32[]{:S(2)}) async-start(bf16[16,48,1664]{2,1,0:T(8,128)(2,1)} %broadcast_in_dim.39), calls=%async_computation | async-start | bytes 5111808 | tf_op jit(solution)/shard_map/all_to_all | solution.py:103
  20.9 213.0 %all-gather.9.cloned.1.call-start = ((), (), s32[]{:S(2)}) async-start(), calls=%async_computation.8 | async-start | bytes 5883904 | tf_op jit(solution)/shard_map/all_gather | solution.py:154
  115.2 36.4 %copy-start.2 = (bf16[128,1664]{1,0:T(8,128)(2,1)S(1)}, bf16[128,1664]{1,0:T(8,128)(2,1)}, u32[]{:S(2)}) copy-start(bf16[128,1664]{1,0:T(8,128)(2,1)} %param.16) | copy-start | bytes 1277956
  151.6 4.0 %copy-start.4 = (f32[1664]{0:T(1024)S(1)}, f32[1664]{0:T(1024)}, u32[]{:S(2)}) copy-start(f32[1664]{0:T(1024)} %param.20) | copy-start | bytes 19972
  178.8 4.1 %copy-start.8 = (s32[32,1]{0,1:T(1,128)S(1)}, s32[32,1]{0,1:T(1,128)}, u32[]{:S(2)}) copy-start(s32[32,1]{0,1:T(1,128)} %param.23) | copy-start | bytes 388
  178.8 45.1 %copy-start.12 = (s32[1,1,128]{2,1,0:T(1,128)S(1)}, s32[1,1,128]{2,1,0:T(1,128)}, u32[]{:S(2)}) copy-start(s32[1,1,128]{2,1,0:T(1,128)} %param.24) | copy-start | bytes 1540
  178.8 54.5 %copy-start.3 = (bf16[128,1664]{1,0:T(8,128)(2,1)S(1)}, bf16[128,1664]{1,0:T(8,128)(2,1)}, u32[]{:S(2)}) copy-start(bf16[128,1664]{1,0:T(8,128)(2,1)} %param.26) | copy-start | bytes 1277956
  178.8 39.3 %all-to-all-start.3 = ((bf16[16,32,1664]{2,1,0:T(8,128)(2,1)}), bf16[16,32,1664]{2,1,0:T(8,128)(2,1)S(1)}, u32[]{:S(2)}, u32[]{:S(2)}) async-start(bf16[16,32,1664]{2,1,0:T(8,128)(2,1)} %bitcast.182), calls=%async_computation.3 | async-start | bytes 3407872 | tf_op jit(solution)/shard_map/all_to_all | solution.py:166
  182.8 51.0 %copy-start.5 = (f32[1664]{0:T(1024)S(1)}, f32[1664]{0:T(1024)}, u32[]{:S(2)}) copy-start(f32[1664]{0:T(1024)} %param.27) | copy-start | bytes 19972
  219.3 13.7 %all-to-all-start.4 = ((bf16[8,9,1664]{2,1,0:T(8,128)(2,1)}), bf16[8,9,1664]{2,1,0:T(8,128)(2,1)S(1)}, u32[]{:S(2)}, u32[]{:S(2)}) async-start(bf16[8,9,1664]{2,1,0:T(8,128)(2,1)} %pad_maximum_fusion.2), calls=%async_computation.4 | async-start | bytes 851968 | tf_op jit(solution)/shard_map/all_to_all | solution.py:188
  223.8 80.7 %all-gather.13.cloned.1.call-start = ((), (), s32[]{:S(2)}) async-start(), calls=%async_computation.10 | async-start | bytes 4526080 | tf_op jit(solution)/shard_map/all_gather | solution.py:100
  236.4 48.3 %copy-start.10 = (bf16[3,1664,104]{1,2,0:T(8,128)(2,1)S(1)}, bf16[3,1664,104]{1,2,0:T(8,128)(2,1)}, u32[]{:S(2)}) copy-start(bf16[3,1664,104]{1,2,0:T(8,128)(2,1)} %param.28) | copy-start | bytes 3115012
  236.4 48.3 %all-to-all-start.5 = ((bf16[16,48,1664]{2,1,0:T(8,128)(2,1)}), bf16[16,48,1664]{2,1,0:T(8,128)(2,1)}, u32[]{:S(2)}, u32[]{:S(2)}) async-start(bf16[16,48,1664]{2,1,0:T(8,128)(2,1)} %broadcast_in_dim.41), calls=%async_computation.5 | async-start | bytes 5111808 | tf_op jit(solution)/shard_map/all_to_all | solution.py:103
  241.7 46.3 %copy-start.6 = (pred[2048]{0:T(1024)(128)(4,1)}, pred[2048]{0:T(1024)(128)(4,1)S(1)}, u32[]{:S(2)}) copy-start(pred[2048]{0:T(1024)(128)(4,1)S(1)} %iota_compare_fusion.4) | copy-start | bytes 6148
  309.4 0.6 slice-start.2
  310.0 0.9 slice-start.3
  311.9 0.7 copy-start.7
  316.5 16.6 %slice-start = ((s8[5537792]{0:T(1024)(128)(4,1)}), s8[4194304]{0:T(1024)(128)(4,1)S(1)}, s32[]{:S(2)}) async-start(s8[5537792]{0:T(1024)(128)(4,1)} %bitcast.176), calls=%async_computation.11 | async-start | bytes 8388608
  316.5 16.6 %slice-start.1 = ((s8[5537792]{0:T(1024)(128)(4,1)}), s8[1343488]{0:T(1024)(128)(4,1)S(1)}, s32[]{:S(2)}) async-start(s8[5537792]{0:T(1024)(128)(4,1)} %bitcast.176), calls=%async_computation.12 | async-start | bytes 2686976
  333.1 2.0 copy-start.1
Sparse Core Ops, SparseCore 0:
  11.3 76.2 all-gather.10
  89.8 61.8 all-gather.6
  153.8 70.8 all-gather.8
  234.8 69.6 all-gather.12

commit v10 on v6

--- a/solution.py
+++ b/solution.py
@@ -24,9 +24,10 @@
 
 
 def projector(weights, shard_piece):
-    return jnp.einsum(
-        "rd,kde->kre", shard_piece, weights, preferred_element_type=jnp.float32
-    ).astype(jnp.bfloat16)
+    count, width, head_width = weights.shape
+    packed = weights.transpose(1, 0, 2).reshape(width, count * head_width)
+    joined = jnp.dot(shard_piece, packed, preferred_element_type=jnp.float32).astype(jnp.bfloat16)
+    return joined.reshape(shard_piece.shape[0], count, head_width).transpose(1, 0, 2)
 
 
 def attend_local(queries, key_rows, value_rows, allowed_fn):

time: 322 us -> 322 us (level)
    dot_general x0 -> x2, matrix products: none -> 11.3 us  [projector(): jnp.dot(shard_piece, packed, preferred_element_type=jnp.float32)]
    unnamed x2 -> x0, matrix products: 11.3 us -> none
where the time goes in v10:
time: 322 us; the launch traced here: 321 us
  waiting for transfers between devices  199 us (62%)
  matrix products  34.8 us (11%)
  blocking collectives  34.5 us (11%)
  other arithmetic  18.8 us (6%)
  between operations  14.1 us (4%)
  starting transfers between devices  13.8 us (4%)
  local copies, waits for them, and re-layouts  6.3 us (2%)
    all_gather x1, waiting for transfers between devices, per_device(): lax.all_gather(vis_normed, 'seq', axis=0, tiled=True)  64.4 us
    all_gather x1, waiting for transfers between devices, per_device(): lax.all_gather(txt_normed, 'seq', axis=0, tiled=True)  58.3 us
    all_to_all x1, waiting for transfers between devices, per_device(): lax.all_to_all(merge_partial.astype(jnp.bfloat16).reshape(seq_count, -1,...  34.2 us
    all_gather x1, waiting for transfers between devices, per_device(): vis_out_full = lax.all_gather(vis_out, 'seq', axis=0, tiled=True)  31.9 us
    all_to_all x1, blocking collectives, per_device(): lax.all_to_all(merged_in, 'seq', split_axis=1, concat_axis=0, tiled=True)  19 us
    all_to_all x1, blocking collectives, heads_to_rows(): lax.all_to_all(blocks, 'seq', split_axis=0, concat_axis=0, tiled=True)  15.5 us
    dot_general x2, matrix products, projector(): jnp.dot(shard_piece, packed, preferred_element_type=jnp.float32)  11.3 us
    all_to_all x1, waiting for transfers between devices, per_device(): lax.all_to_all(jnp.concatenate([outgoing, flag_row], axis=1), 'grp', spli...  9.02 us
  transfers between devices with their start and end apart: 7, of which 5 were waited for; matrix products, arithmetic and copies ran while one was open for 12% of the time, Pallas kernels for 0%

profile of v10, /device:TPU:0, one launch (start us, length us, event | category | flops | bytes accessed | tf_op | source)
XLA Modules:
  0.0 321.0 jit_solution(7446433832728544742)
XLA Ops:
  6.5 1.3 convert_reduce_fusion.1
  7.8 1.3 fusion.35
  9.1 2.1 fusion.37
  11.2 0.7 all-gather.7.cloned.1.call-update
  12.0 0.8 reduce-window.4
  12.9 64.4 %all-gather.5.cloned.1.call-done = bf16[2048,1664]{1,0:T(8,128)(2,1)} async-done(((bf16[128,1664]{1,0:T(8,128)(2,1)}), bf16[2048,1664]{1,0:T(8,128)(2,1)}) %all-gather.5.cloned.1.call-update) | async-done | bytes 6815760 | tf_op jit(solution)/shard_map/all_gather | solution.py:122
  77.4 5.7 %convolution_convert_fusion.2 = bf16[2048,312]{0,1:T(8,128)(2,1)S(1)} fusion(bf16[2048,1664]{1,0:T(8,128)(2,1)} %all-gather.5.cloned.1.call-done, bf16[1664,312]{0,1:T(8,128)(2,1)} %bitcast.189), kind=kOutput, calls=%fused_computation.38 | convolution fusion | flops 2127151104 | bytes 9132032 | tf_op jit(solution)/shard_map/dot_general | solution.py:29
  83.2 0.3 reshape_squeeze.12
  83.6 16.5 %while.12 = (s32[]{:T(128)}, bf16[4,512,1,104]{1,3,2,0:T(8,128)(2,1)S(1)}, s32[4]{0:T(128)S(1)}, s32[3]{0:T(128)S(1)}, s32[2048]{0:T(1024)S(1)}, /*index=5*/bf16...) while((s32[]{:T(128)}, ...), condition=%wide.region_10.11_spmd, body=%wide.region_6.10_spmd.sunk | while | flops 445709312 | bytes 13674625 | solution.py:58
  83.6 0.6 dynamic_slice.23
  84.2 0.7 add_select_fusion.3
  84.9 1.0 fusion.75
  85.9 0.7 fusion.76
  86.6 1.1 fusion.77
  87.7 0.6 dynamic_slice.23
  88.3 0.7 add_select_fusion.3
  89.1 1.0 fusion.75
  90.0 0.7 fusion.76
  90.8 1.1 fusion.77
  91.9 0.6 dynamic_slice.23
  92.4 0.7 add_select_fusion.3
  93.2 1.0 fusion.75
  94.2 0.7 fusion.76
  94.9 1.1 fusion.77
  96.0 0.6 dynamic_slice.23
  96.6 0.7 add_select_fusion.3
  97.3 1.0 fusion.75
  98.3 0.7 fusion.76
  99.0 1.1 fusion.77
  100.5 0.8 copy_bitcast_fusion
  101.3 5.3 %all-to-all-start = ((bf16[16,128,104]{1,2,0:T(8,128)(2,1)}), bf16[16,128,104]{1,2,0:T(8,128)(2,1)S(1)}, u32[]{:S(2)}, u32[]{:S(2)}) async-start(bf16[16,128,104]{1,2,0:T(8,128)(2,1)} %copy_bitcast_fusion), calls=%async_computation | async-start | bytes 851968 | tf_op jit(solution)/shard_map/all_to_all | solution.py:66
  106.6 31.9 %all-gather.7.cloned.1.call-done = bf16[1664,1664]{1,0:T(8,128)(2,1)} async-done(((bf16[104,1664]{1,0:T(8,128)(2,1)}), bf16[1664,1664]{1,0:T(8,128)(2,1)}) %all-gather.7.cloned.1.call-update) | async-done | bytes 5537808 | tf_op jit(solution)/shard_map/all_gather | solution.py:120
  138.5 3.7 %fusion.54 = (f32[128]{0:T(128)S(1)}, f32[128,1664]{1,0:T(8,128)S(1)}) fusion(bf16[128,1664]{0,1:T(8,128)(2,1)S(1)} %bitcast.177, bf16[1664,1664]{1,0:T(8,128)(2,1)} %all-gather.7.cloned.1.call-done, bf16[128,1664]{1,0:T(8,128)(2,1)S(1)} %copy-done.1), kind=kOutput, calls=%fused_computation.139 | convolution fusion | flops 709476224 | bytes 7242240 | tf_op jit(solution)/shard_map/dot_general | solution.py:136
  142.7 0.6 all_to_all.27
  143.3 0.3 copy.31
  143.6 19.0 %all_to_all.39 = bf16[32,16,416]{2,0,1:T(8,128)(2,1)S(1)} all-to-all(bf16[32,16,416]{2,0,1:T(8,128)(2,1)S(1)} %copy.31), channel_id=1, replica_groups=mesh['seq'=16,'grp'=8] {'seq'}, dimensions={1} | all-to-all | bytes 851968 | tf_op jit(solution)/shard_map/all_to_all | solution.py:145
  162.6 2.3 convolution_convert_fusion
  164.9 3.8 %all-to-all-start.2 = ((bf16[16,32,1664]{2,1,0:T(8,128)(2,1)}), bf16[16,32,1664]{2,1,0:T(8,128)(2,1)S(1)}, u32[]{:S(2)}, u32[]{:S(2)}) async-start(bf16[16,32,1664]{2,1,0:T(8,128)(2,1)} %bitcast.178), calls=%async_computation.2 | async-start | bytes 3407872 | tf_op jit(solution)/shard_map/all_to_all | solution.py:147
  168.9 0.9 select_reduce_fusion
  169.8 0.7 iota_compare_fusion.5
  170.5 0.7 copy.32
  171.2 34.2 %all-to-all-done.2 = bf16[16,32,1664]{2,1,0:T(8,128)(2,1)S(1)} async-done(((bf16[16,32,1664]{2,1,0:T(8,128)(2,1)}), bf16[16,32,1664]{2,1,0:T(8,128)(2,1)S(1)}, u32[]{:S(2)}, u32[]{:S(2)}) %all-to-all-start.2) | async-done | bytes 1703968 | tf_op jit(solution)/shard_map/all_to_all | solution.py:147
  205.4 0.9 reduce_sum.159
  206.3 1.1 convolution_convert_fusion.3
  207.4 1.6 pad_maximum_fusion
  209.0 4.5 %all-to-all-start.3 = ((bf16[8,9,1664]{2,1,0:T(8,128)(2,1)}), bf16[8,9,1664]{2,1,0:T(8,128)(2,1)S(1)}, u32[]{:S(2)}, u32[]{:S(2)}) async-start(bf16[8,9,1664]{2,1,0:T(8,128)(2,1)} %pad_maximum_fusion), calls=%async_computation.3 | async-start | bytes 851968 | tf_op jit(solution)/shard_map/all_to_all | solution.py:169
  213.7 9.0 %all-to-all-done.3 = bf16[8,9,1664]{2,1,0:T(8,128)(2,1)S(1)} async-done(((bf16[8,9,1664]{2,1,0:T(8,128)(2,1)}), bf16[8,9,1664]{2,1,0:T(8,128)(2,1)S(1)}, u32[]{:S(2)}, u32[]{:S(2)}) %all-to-all-start.3) | async-done | bytes 239648 | tf_op jit(solution)/shard_map/all_to_all | solution.py:169
  222.9 0.5 multiply_reduce_fusion
  223.4 0.9 multiply_convert_fusion
  225.1 58.3 %all-gather.11.cloned.1.call-done = bf16[2048,1664]{1,0:T(8,128)(2,1)} async-done(((bf16[128,1664]{1,0:T(8,128)(2,1)}), bf16[2048,1664]{1,0:T(8,128)(2,1)}) %all-gather.11.cloned.1.call-update) | async-done | bytes 6815760 | tf_op jit(solution)/shard_map/all_gather | solution.py:189
  283.3 5.7 %convolution_convert_fusion.1 = bf16[2048,312]{0,1:T(8,128)(2,1)S(1)} fusion(bf16[2048,1664]{1,0:T(8,128)(2,1)} %all-gather.11.cloned.1.call-done, bf16[1664,312]{0,1:T(8,128)(2,1)} %bitcast.190), kind=kOutput, calls=%fused_computation.37 | convolution fusion | flops 2127151104 | bytes 9132032 | tf_op jit(solution)/shard_map/dot_general | solution.py:29
  289.0 0.4 fusion.58
  289.6 0.3 fusion.30
  290.1 0.7 fusion.57
  290.8 0.4 fusion.22
  291.2 0.5 fusion.29
  291.9 1.0 fusion.56
  292.9 0.5 fusion.17
  293.4 0.6 fusion.28
  294.0 1.3 fusion.55
  295.4 0.6 fusion.14
  296.0 0.8 fusion.27
  297.0 15.5 %all_to_all.40 = bf16[16,128,104]{1,2,0:T(8,128)(2,1)S(1)} all-to-all(bf16[16,128,104]{1,2,0:T(8,128)(2,1)S(1)} %copy.36), channel_id=1, replica_groups=mesh['seq'=16,'grp'=8] {'seq'}, dimensions={0} | all-to-all | bytes 851968 | tf_op jit(solution)/shard_map/all_to_all | solution.py:66
  312.5 1.9 convolution_add_fusion
  (72 shorter events, 3.1 us)
Async XLA Ops:
  6.5 156.0 %copy-start = (bf16[416,1664]{1,0:T(8,128)(2,1)S(1)}, bf16[416,1664]{1,0:T(8,128)(2,1)}, u32[]{:S(2)}) copy-start(bf16[416,1664]{1,0:T(8,128)(2,1)} %param.21) | copy-start | bytes 4153348
  6.5 70.8 %all-gather.5.cloned.1.call-start = ((), (), s32[]{:S(2)}) async-start(), calls=%async_computation.5 | async-start | bytes 7241728 | tf_op jit(solution)/shard_map/all_gather | solution.py:122
  11.2 127.3 %all-gather.7.cloned.1.call-start = ((), (), s32[]{:S(2)}) async-start(), calls=%async_computation.6 | async-start | bytes 5883904 | tf_op jit(solution)/shard_map/all_gather | solution.py:120
  11.9 212.4 %all-gather.9.cloned.1.call-start = ((), (), s32[]{:S(2)}) async-start(), calls=%async_computation.7 | async-start | bytes 5883904 | tf_op jit(solution)/shard_map/all_gather | solution.py:135
  100.1 38.4 %copy-start.1 = (bf16[128,1664]{1,0:T(8,128)(2,1)S(1)}, bf16[128,1664]{1,0:T(8,128)(2,1)}, u32[]{:S(2)}) copy-start(bf16[128,1664]{1,0:T(8,128)(2,1)} %param.16) | copy-start | bytes 1277956
  101.3 37.2 %all-to-all-start = ((bf16[16,128,104]{1,2,0:T(8,128)(2,1)}), bf16[16,128,104]{1,2,0:T(8,128)(2,1)S(1)}, u32[]{:S(2)}, u32[]{:S(2)}) async-start(bf16[16,128,104]{1,2,0:T(8,128)(2,1)} %copy_bitcast_fusion), calls=%async_computation | async-start | bytes 851968 | tf_op jit(solution)/shard_map/all_to_all | solution.py:66
  138.5 4.0 %copy-start.3 = (f32[1664]{0:T(1024)S(1)}, f32[1664]{0:T(1024)}, u32[]{:S(2)}) copy-start(f32[1664]{0:T(1024)} %param.20) | copy-start | bytes 19972
  164.9 3.9 %copy-start.7 = (s32[32,1]{0,1:T(1,128)S(1)}, s32[32,1]{0,1:T(1,128)}, u32[]{:S(2)}) copy-start(s32[32,1]{0,1:T(1,128)} %param.23) | copy-start | bytes 388
  164.9 58.0 %copy-start.2 = (bf16[128,1664]{1,0:T(8,128)(2,1)S(1)}, bf16[128,1664]{1,0:T(8,128)(2,1)}, u32[]{:S(2)}) copy-start(bf16[128,1664]{1,0:T(8,128)(2,1)} %param.26) | copy-start | bytes 1277956
  164.9 40.5 %all-to-all-start.2 = ((bf16[16,32,1664]{2,1,0:T(8,128)(2,1)}), bf16[16,32,1664]{2,1,0:T(8,128)(2,1)S(1)}, u32[]{:S(2)}, u32[]{:S(2)}) async-start(bf16[16,32,1664]{2,1,0:T(8,128)(2,1)} %bitcast.178), calls=%async_computation.2 | async-start | bytes 3407872 | tf_op jit(solution)/shard_map/all_to_all | solution.py:147
  168.7 54.7 %copy-start.4 = (f32[1664]{0:T(1024)S(1)}, f32[1664]{0:T(1024)}, u32[]{:S(2)}) copy-start(f32[1664]{0:T(1024)} %param.27) | copy-start | bytes 19972
  168.9 44.8 %copy-start.8 = (s32[1,1,128]{2,1,0:T(1,128)S(1)}, s32[1,1,128]{2,1,0:T(1,128)}, u32[]{:S(2)}) copy-start(s32[1,1,128]{2,1,0:T(1,128)} %param.24) | copy-start | bytes 1540
  209.0 13.7 %all-to-all-start.3 = ((bf16[8,9,1664]{2,1,0:T(8,128)(2,1)}), bf16[8,9,1664]{2,1,0:T(8,128)(2,1)S(1)}, u32[]{:S(2)}, u32[]{:S(2)}) async-start(bf16[8,9,1664]{2,1,0:T(8,128)(2,1)} %pad_maximum_fusion), calls=%async_computation.3 | async-start | bytes 851968 | tf_op jit(solution)/shard_map/all_to_all | solution.py:169
  213.5 69.9 %all-gather.11.cloned.1.call-start = ((), (), s32[]{:S(2)}) async-start(), calls=%async_computation.8 | async-start | bytes 7241728 | tf_op jit(solution)/shard_map/all_gather | solution.py:189
  225.0 64.0 %copy-start.5 = (pred[2048]{0:T(1024)(128)(4,1)}, pred[2048]{0:T(1024)(128)(4,1)S(1)}, u32[]{:S(2)}) copy-start(pred[2048]{0:T(1024)(128)(4,1)S(1)} %iota_compare_fusion.4) | copy-start | bytes 6148
  289.4 0.7 slice-start.2
  291.2 0.7 copy-start.6
  295.4 17.2 %slice-start = ((s8[5537792]{0:T(1024)(128)(4,1)}), s8[1343488]{0:T(1024)(128)(4,1)S(1)}, s32[]{:S(2)}) async-start(s8[5537792]{0:T(1024)(128)(4,1)} %bitcast.175), calls=%async_computation.9 | async-start | bytes 2686976
  296.0 16.5 %slice-start.1 = ((s8[5537792]{0:T(1024)(128)(4,1)}), s8[4194304]{0:T(1024)(128)(4,1)S(1)}, s32[]{:S(2)}) async-start(s8[5537792]{0:T(1024)(128)(4,1)} %bitcast.175), calls=%async_computation.10 | async-start | bytes 8388608
Sparse Core Ops, SparseCore 0:
  11.3 66.0 all-gather.4
  79.5 58.9 all-gather.6
  140.6 70.9 all-gather.8
  224.5 58.8 all-gather.10

commit v11 on v10

--- a/solution.py
+++ b/solution.py
@@ -1,5 +1,7 @@
 import jax
 import jax.numpy as jnp
+from jax.experimental import pallas as pl
+from jax.experimental.pallas import tpu as pltpu
 from jax import lax
 from jax.sharding import PartitionSpec as P
 
@@ -12,6 +14,27 @@
     centred = values_f - row_mean
     variance = jnp.mean(centred * centred, axis=-1, keepdims=True)
     return centred * lax.rsqrt(variance + 1e-06) * scale_gain
+
+
+def layer_norm_kernel(x_ref, g_ref, o_ref):
+    values_f = x_ref[...].astype(jnp.float32)
+    row_mean = jnp.mean(values_f, axis=-1, keepdims=True)
+    centred = values_f - row_mean
+    variance = jnp.mean(centred * centred, axis=-1, keepdims=True)
+    o_ref[...] = (centred * lax.rsqrt(variance + 1e-06) * g_ref[...]).astype(o_ref.dtype)
+
+
+def layer_norm_fused(row_block, scale_gain):
+    rows, width = row_block.shape
+    return pl.pallas_call(
+        layer_norm_kernel,
+        out_shape=jax.ShapeDtypeStruct((rows, width), jnp.bfloat16),
+        in_specs=[pl.BlockSpec(memory_space=pltpu.VMEM)] * 2,
+        out_specs=pl.BlockSpec(memory_space=pltpu.VMEM),
+        cost_estimate=pl.CostEstimate(
+            flops=8 * rows * width, transcendentals=rows, bytes_accessed=4 * rows * width + 4 * width
+        ),
+    )(row_block, scale_gain.reshape(1, width))
 
 
 def rms_norm(row_block, scale_gain):
@@ -118,7 +141,7 @@
     model_width = patches.shape[1]
     group_patches = token_count * seq_count
     vis_out_full = lax.all_gather(vis_out, "seq", axis=0, tiled=True)
-    vis_normed = layer_norm(patches, vis_gain).astype(jnp.bfloat16)
+    vis_normed = layer_norm_fused(patches, vis_gain)
     vis_proj = projector(vis_qkv, lax.all_gather(vis_normed, "seq", axis=0, tiled=True))
     bounds = jnp.cumsum(image_blocks[0])[:-1]
 

time: 322 us -> 321 us (level)
  other arithmetic: 18.8 us -> 14.2 us
where the time goes in v11:
time: 321 us; the launch traced here: 320 us
  waiting for transfers between devices  199 us (62%)
  matrix products  34.8 us (11%)
  blocking collectives  34.5 us (11%)
  other arithmetic  14.2 us (4%)
  between operations  14.1 us (4%)
  starting transfers between devices  13.9 us (4%)
  local copies, waits for them, and re-layouts  7.71 us (2%)
    all_gather x1, waiting for transfers between devices, per_device(): lax.all_gather(vis_normed, 'seq', axis=0, tiled=True)  64.4 us
    all_gather x1, waiting for transfers between devices, per_device(): lax.all_gather(txt_normed, 'seq', axis=0, tiled=True)  58.3 us
    all_to_all x1, waiting for transfers between devices, per_device(): lax.all_to_all(merge_partial.astype(jnp.bfloat16).reshape(seq_count, -1,...  34.2 us
    all_gather x1, waiting for transfers between devices, per_device(): vis_out_full = lax.all_gather(vis_out, 'seq', axis=0, tiled=True)  31.9 us
    all_to_all x1, blocking collectives, per_device(): lax.all_to_all(merged_in, 'seq', split_axis=1, concat_axis=0, tiled=True)  19 us
    all_to_all x1, blocking collectives, heads_to_rows(): lax.all_to_all(blocks, 'seq', split_axis=0, concat_axis=0, tiled=True)  15.5 us
    dot_general x2, matrix products, projector(): jnp.dot(shard_piece, packed, preferred_element_type=jnp.float32)  11.3 us
    all_to_all x1, waiting for transfers between devices, per_device(): lax.all_to_all(jnp.concatenate([outgoing, flag_row], axis=1), 'grp', spli...  9.02 us
  transfers between devices with their start and end apart: 7, of which 5 were waited for; matrix products, arithmetic and copies ran while one was open for 12% of the time, Pallas kernels for 0%

profile of v11, /device:TPU:0, one launch (start us, length us, event | category | flops | bytes accessed | tf_op | source)
XLA Modules:
  0.0 319.9 jit_solution(17381957508605950571)
XLA Ops:
  6.5 1.4 reshape.369.g_ref
  7.9 2.1 shard_map.136
  10.1 0.7 all-gather.7.cloned.1.call-update
  10.9 0.8 reduce-window.4
  11.8 64.4 %all-gather.5.cloned.1.call-done = bf16[2048,1664]{1,0:T(8,128)(2,1)} async-done(((bf16[128,1664]{1,0:T(8,128)(2,1)}), bf16[2048,1664]{1,0:T(8,128)(2,1)}) %all-gather.5.cloned.1.call-update) | async-done | bytes 6815760 | tf_op jit(solution)/shard_map/all_gather | solution.py:145
  76.3 5.7 %convolution_convert_fusion.2 = bf16[2048,312]{0,1:T(8,128)(2,1)S(1)} fusion(bf16[2048,1664]{1,0:T(8,128)(2,1)} %all-gather.5.cloned.1.call-done, bf16[1664,312]{0,1:T(8,128)(2,1)} %bitcast.189), kind=kOutput, calls=%fused_computation.38 | convolution fusion | flops 2127151104 | bytes 9132032 | tf_op jit(solution)/shard_map/dot_general | solution.py:52
  82.1 0.3 reshape_squeeze.12
  82.5 16.5 %while.12 = (s32[]{:T(128)}, bf16[4,512,1,104]{1,3,2,0:T(8,128)(2,1)S(1)}, s32[4]{0:T(128)S(1)}, s32[3]{0:T(128)S(1)}, s32[2048]{0:T(1024)S(1)}, /*index=5*/bf16...) while((s32[]{:T(128)}, ...), condition=%wide.region_8.9_spmd, body=%wide.region_4.8_spmd.sunk | while | flops 445709312 | bytes 13674625 | solution.py:81
  82.5 0.6 dynamic_slice.23
  83.1 0.7 add_select_fusion.3
  83.8 1.0 fusion.70
  84.8 0.7 fusion.71
  85.5 1.1 fusion.72
  86.6 0.6 dynamic_slice.23
  87.2 0.7 add_select_fusion.3
  87.9 1.0 fusion.70
  88.9 0.7 fusion.71
  89.6 1.1 fusion.72
  90.7 0.6 dynamic_slice.23
  91.3 0.7 add_select_fusion.3
  92.1 1.0 fusion.70
  93.1 0.7 fusion.71
  93.8 1.1 fusion.72
  94.9 0.6 dynamic_slice.23
  95.4 0.7 add_select_fusion.3
  96.2 1.0 fusion.70
  97.2 0.7 fusion.71
  97.9 1.1 fusion.72
  99.3 0.8 copy_bitcast_fusion
  100.2 5.3 %all-to-all-start = ((bf16[16,128,104]{1,2,0:T(8,128)(2,1)}), bf16[16,128,104]{1,2,0:T(8,128)(2,1)S(1)}, u32[]{:S(2)}, u32[]{:S(2)}) async-start(bf16[16,128,104]{1,2,0:T(8,128)(2,1)} %copy_bitcast_fusion), calls=%async_computation | async-start | bytes 851968 | tf_op jit(solution)/shard_map/all_to_all | solution.py:89
  105.4 31.9 %all-gather.7.cloned.1.call-done = bf16[1664,1664]{1,0:T(8,128)(2,1)} async-done(((bf16[104,1664]{1,0:T(8,128)(2,1)}), bf16[1664,1664]{1,0:T(8,128)(2,1)}) %all-gather.7.cloned.1.call-update) | async-done | bytes 5537808 | tf_op jit(solution)/shard_map/all_gather | solution.py:143
  137.4 3.7 %fusion.49 = (f32[128]{0:T(128)S(1)}, f32[128,1664]{1,0:T(8,128)S(1)}) fusion(bf16[128,1664]{0,1:T(8,128)(2,1)S(1)} %bitcast.177, bf16[1664,1664]{1,0:T(8,128)(2,1)} %all-gather.7.cloned.1.call-done, bf16[128,1664]{1,0:T(8,128)(2,1)S(1)} %copy-done.1), kind=kOutput, calls=%fused_computation.130 | convolution fusion | flops 709476224 | bytes 7242240 | tf_op jit(solution)/shard_map/dot_general | solution.py:159
  141.1 0.2 multiply_reduce_fusion.1
  141.5 0.6 all_to_all.27
  142.2 0.3 copy.31
  142.5 19.0 %all_to_all.39 = bf16[32,16,416]{2,0,1:T(8,128)(2,1)S(1)} all-to-all(bf16[32,16,416]{2,0,1:T(8,128)(2,1)S(1)} %copy.31), channel_id=1, replica_groups=mesh['seq'=16,'grp'=8] {'seq'}, dimensions={1} | all-to-all | bytes 851968 | tf_op jit(solution)/shard_map/all_to_all | solution.py:168
  161.5 2.3 convolution_convert_fusion
  163.8 3.8 %all-to-all-start.2 = ((bf16[16,32,1664]{2,1,0:T(8,128)(2,1)}), bf16[16,32,1664]{2,1,0:T(8,128)(2,1)S(1)}, u32[]{:S(2)}, u32[]{:S(2)}) async-start(bf16[16,32,1664]{2,1,0:T(8,128)(2,1)} %bitcast.178), calls=%async_computation.2 | async-start | bytes 3407872 | tf_op jit(solution)/shard_map/all_to_all | solution.py:170
  167.8 0.9 select_reduce_fusion
  168.6 0.7 iota_compare_fusion.5
  169.4 0.7 copy.32
  170.1 34.2 %all-to-all-done.2 = bf16[16,32,1664]{2,1,0:T(8,128)(2,1)S(1)} async-done(((bf16[16,32,1664]{2,1,0:T(8,128)(2,1)}), bf16[16,32,1664]{2,1,0:T(8,128)(2,1)S(1)}, u32[]{:S(2)}, u32[]{:S(2)}) %all-to-all-start.2) | async-done | bytes 1703968 | tf_op jit(solution)/shard_map/all_to_all | solution.py:170
  204.2 0.9 reduce_sum.139
  205.2 1.1 convolution_convert_fusion.3
  206.3 1.6 pad_maximum_fusion
  207.9 4.5 %all-to-all-start.3 = ((bf16[8,9,1664]{2,1,0:T(8,128)(2,1)}), bf16[8,9,1664]{2,1,0:T(8,128)(2,1)S(1)}, u32[]{:S(2)}, u32[]{:S(2)}) async-start(bf16[8,9,1664]{2,1,0:T(8,128)(2,1)} %pad_maximum_fusion), calls=%async_computation.3 | async-start | bytes 851968 | tf_op jit(solution)/shard_map/all_to_all | solution.py:192
  212.6 9.0 %all-to-all-done.3 = bf16[8,9,1664]{2,1,0:T(8,128)(2,1)S(1)} async-done(((bf16[8,9,1664]{2,1,0:T(8,128)(2,1)}), bf16[8,9,1664]{2,1,0:T(8,128)(2,1)S(1)}, u32[]{:S(2)}, u32[]{:S(2)}) %all-to-all-start.3) | async-done | bytes 239648 | tf_op jit(solution)/shard_map/all_to_all | solution.py:192
  221.8 0.5 multiply_reduce_fusion
  222.3 0.9 multiply_convert_fusion
  224.0 58.3 %all-gather.11.cloned.1.call-done = bf16[2048,1664]{1,0:T(8,128)(2,1)} async-done(((bf16[128,1664]{1,0:T(8,128)(2,1)}), bf16[2048,1664]{1,0:T(8,128)(2,1)}) %all-gather.11.cloned.1.call-update) | async-done | bytes 6815760 | tf_op jit(solution)/shard_map/all_gather | solution.py:212
  282.2 5.7 %convolution_convert_fusion.1 = bf16[2048,312]{0,1:T(8,128)(2,1)S(1)} fusion(bf16[2048,1664]{1,0:T(8,128)(2,1)} %all-gather.11.cloned.1.call-done, bf16[1664,312]{0,1:T(8,128)(2,1)} %bitcast.190), kind=kOutput, calls=%fused_computation.37 | convolution fusion | flops 2127151104 | bytes 9132032 | tf_op jit(solution)/shard_map/dot_general | solution.py:52
  287.9 0.4 fusion.53
  288.5 0.3 fusion.30
  289.0 0.7 fusion.52
  289.7 0.4 fusion.22
  290.1 0.5 fusion.29
  290.7 1.0 fusion.51
  291.8 0.5 fusion.17
  292.3 0.6 fusion.28
  292.9 1.3 fusion.50
  294.3 0.6 fusion.14
  294.9 0.8 fusion.27
  295.9 15.5 %all_to_all.40 = bf16[16,128,104]{1,2,0:T(8,128)(2,1)S(1)} all-to-all(bf16[16,128,104]{1,2,0:T(8,128)(2,1)S(1)} %copy.36), channel_id=1, replica_groups=mesh['seq'=16,'grp'=8] {'seq'}, dimensions={0} | all-to-all | bytes 851968 | tf_op jit(solution)/shard_map/all_to_all | solution.py:89
  311.4 1.9 convolution_add_fusion
  (69 shorter events, 2.8 us)
Async XLA Ops:
  6.5 154.9 %copy-start = (bf16[416,1664]{1,0:T(8,128)(2,1)S(1)}, bf16[416,1664]{1,0:T(8,128)(2,1)}, u32[]{:S(2)}) copy-start(bf16[416,1664]{1,0:T(8,128)(2,1)} %param.21) | copy-start | bytes 4153348
  6.5 69.7 %all-gather.5.cloned.1.call-start = ((), (), s32[]{:S(2)}) async-start(), calls=%async_computation.5 | async-start | bytes 7241728 | tf_op jit(solution)/shard_map/all_gather | solution.py:145
  10.1 127.3 %all-gather.7.cloned.1.call-start = ((), (), s32[]{:S(2)}) async-start(), calls=%async_computation.6 | async-start | bytes 5883904 | tf_op jit(solution)/shard_map/all_gather | solution.py:143
  10.8 212.4 %all-gather.9.cloned.1.call-start = ((), (), s32[]{:S(2)}) async-start(), calls=%async_computation.7 | async-start | bytes 5883904 | tf_op jit(solution)/shard_map/all_gather | solution.py:158
  99.0 38.4 %copy-start.1 = (bf16[128,1664]{1,0:T(8,128)(2,1)S(1)}, bf16[128,1664]{1,0:T(8,128)(2,1)}, u32[]{:S(2)}) copy-start(bf16[128,1664]{1,0:T(8,128)(2,1)} %x_ref.1) | copy-start | bytes 1277956
  100.2 37.2 %all-to-all-start = ((bf16[16,128,104]{1,2,0:T(8,128)(2,1)}), bf16[16,128,104]{1,2,0:T(8,128)(2,1)S(1)}, u32[]{:S(2)}, u32[]{:S(2)}) async-start(bf16[16,128,104]{1,2,0:T(8,128)(2,1)} %copy_bitcast_fusion), calls=%async_computation | async-start | bytes 851968 | tf_op jit(solution)/shard_map/all_to_all | solution.py:89
  137.4 4.0 %copy-start.3 = (f32[1664]{0:T(1024)S(1)}, f32[1664]{0:T(1024)}, u32[]{:S(2)}) copy-start(f32[1664]{0:T(1024)} %param.20) | copy-start | bytes 19972
  163.8 3.9 %copy-start.7 = (s32[32,1]{0,1:T(1,128)S(1)}, s32[32,1]{0,1:T(1,128)}, u32[]{:S(2)}) copy-start(s32[32,1]{0,1:T(1,128)} %param.23) | copy-start | bytes 388
  163.8 58.0 %copy-start.2 = (bf16[128,1664]{1,0:T(8,128)(2,1)S(1)}, bf16[128,1664]{1,0:T(8,128)(2,1)}, u32[]{:S(2)}) copy-start(bf16[128,1664]{1,0:T(8,128)(2,1)} %param.26) | copy-start | bytes 1277956
  163.8 40.5 %all-to-all-start.2 = ((bf16[16,32,1664]{2,1,0:T(8,128)(2,1)}), bf16[16,32,1664]{2,1,0:T(8,128)(2,1)S(1)}, u32[]{:S(2)}, u32[]{:S(2)}) async-start(bf16[16,32,1664]{2,1,0:T(8,128)(2,1)} %bitcast.178), calls=%async_computation.2 | async-start | bytes 3407872 | tf_op jit(solution)/shard_map/all_to_all | solution.py:170
  167.6 54.7 %copy-start.4 = (f32[1664]{0:T(1024)S(1)}, f32[1664]{0:T(1024)}, u32[]{:S(2)}) copy-start(f32[1664]{0:T(1024)} %param.27) | copy-start | bytes 19972
  167.8 44.8 %copy-start.8 = (s32[1,1,128]{2,1,0:T(1,128)S(1)}, s32[1,1,128]{2,1,0:T(1,128)}, u32[]{:S(2)}) copy-start(s32[1,1,128]{2,1,0:T(1,128)} %param.24) | copy-start | bytes 1540
  207.9 13.7 %all-to-all-start.3 = ((bf16[8,9,1664]{2,1,0:T(8,128)(2,1)}), bf16[8,9,1664]{2,1,0:T(8,128)(2,1)S(1)}, u32[]{:S(2)}, u32[]{:S(2)}) async-start(bf16[8,9,1664]{2,1,0:T(8,128)(2,1)} %pad_maximum_fusion), calls=%async_computation.3 | async-start | bytes 851968 | tf_op jit(solution)/shard_map/all_to_all | solution.py:192
  212.3 69.9 %all-gather.11.cloned.1.call-start = ((), (), s32[]{:S(2)}) async-start(), calls=%async_computation.8 | async-start | bytes 7241728 | tf_op jit(solution)/shard_map/all_gather | solution.py:212
  223.9 64.0 %copy-start.5 = (pred[2048]{0:T(1024)(128)(4,1)}, pred[2048]{0:T(1024)(128)(4,1)S(1)}, u32[]{:S(2)}) copy-start(pred[2048]{0:T(1024)(128)(4,1)S(1)} %iota_compare_fusion.4) | copy-start | bytes 6148
  288.3 0.7 slice-start.2
  290.1 0.7 copy-start.6
  294.2 17.2 %slice-start = ((s8[5537792]{0:T(1024)(128)(4,1)}), s8[1343488]{0:T(1024)(128)(4,1)S(1)}, s32[]{:S(2)}) async-start(s8[5537792]{0:T(1024)(128)(4,1)} %bitcast.175), calls=%async_computation.9 | async-start | bytes 2686976
  294.9 16.5 %slice-start.1 = ((s8[5537792]{0:T(1024)(128)(4,1)}), s8[4194304]{0:T(1024)(128)(4,1)S(1)}, s32[]{:S(2)}) async-start(s8[5537792]{0:T(1024)(128)(4,1)} %bitcast.175), calls=%async_computation.10 | async-start | bytes 8388608
Sparse Core Ops, SparseCore 0:
  10.2 66.0 all-gather.4
  78.4 58.9 all-gather.6
  139.5 70.9 all-gather.8
  223.4 58.8 all-gather.10

commit v12 on v11

--- a/solution.py
+++ b/solution.py
@@ -21,7 +21,7 @@
     row_mean = jnp.mean(values_f, axis=-1, keepdims=True)
     centred = values_f - row_mean
     variance = jnp.mean(centred * centred, axis=-1, keepdims=True)
-    o_ref[...] = (centred * lax.rsqrt(variance + 1e-06) * g_ref[...]).astype(o_ref.dtype)
+    o_ref[...] = (centred * lax.rsqrt(variance + 1e-06) * g_ref[...][None, :]).astype(o_ref.dtype)
 
 
 def layer_norm_fused(row_block, scale_gain):
@@ -34,7 +34,7 @@
         cost_estimate=pl.CostEstimate(
             flops=8 * rows * width, transcendentals=rows, bytes_accessed=4 * rows * width + 4 * width
         ),
-    )(row_block, scale_gain.reshape(1, width))
+    )(row_block, scale_gain)
 
 
 def rms_norm(row_block, scale_gain):

time: 321 us -> 320 us (level)
  no operation moved by 1% of the time
where the time goes in v12:
time: 320 us; the launch traced here: 319 us
  waiting for transfers between devices  199 us (62%)
  matrix products  34.8 us (11%)
  blocking collectives  34.5 us (11%)
  other arithmetic  14.2 us (4%)
  between operations  14.1 us (4%)
  starting transfers between devices  13.8 us (4%)
  local copies, waits for them, and re-layouts  6.3 us (2%)
    all_gather x1, waiting for transfers between devices, per_device(): lax.all_gather(vis_normed, 'seq', axis=0, tiled=True)  65 us
    all_gather x1, waiting for transfers between devices, per_device(): lax.all_gather(txt_normed, 'seq', axis=0, tiled=True)  58.3 us
    all_to_all x1, waiting for transfers between devices, per_device(): lax.all_to_all(merge_partial.astype(jnp.bfloat16).reshape(seq_count, -1,...  34.2 us
    all_gather x1, waiting for transfers between devices, per_device(): vis_out_full = lax.all_gather(vis_out, 'seq', axis=0, tiled=True)  31.9 us
    all_to_all x1, blocking collectives, per_device(): lax.all_to_all(merged_in, 'seq', split_axis=1, concat_axis=0, tiled=True)  19 us
    all_to_all x1, blocking collectives, heads_to_rows(): lax.all_to_all(blocks, 'seq', split_axis=0, concat_axis=0, tiled=True)  15.5 us
    dot_general x2, matrix products, projector(): jnp.dot(shard_piece, packed, preferred_element_type=jnp.float32)  11.3 us
    all_to_all x1, waiting for transfers between devices, per_device(): lax.all_to_all(jnp.concatenate([outgoing, flag_row], axis=1), 'grp', spli...  9.02 us
  transfers between devices with their start and end apart: 7, of which 5 were waited for; matrix products, arithmetic and copies ran while one was open for 12% of the time, Pallas kernels for 0%

profile of v12, /device:TPU:0, one launch (start us, length us, event | category | flops | bytes accessed | tf_op | source)
XLA Modules:
  0.0 319.1 jit_solution(3896641413896565817)
XLA Ops:
  6.5 2.2 shard_map.136
  8.8 0.7 all-gather.7.cloned.1.call-update
  9.6 0.8 reduce-window.4
  10.5 65.0 %all-gather.5.cloned.1.call-done = bf16[2048,1664]{1,0:T(8,128)(2,1)} async-done(((bf16[128,1664]{1,0:T(8,128)(2,1)}), bf16[2048,1664]{1,0:T(8,128)(2,1)}) %all-gather.5.cloned.1.call-update) | async-done | bytes 6815760 | tf_op jit(solution)/shard_map/all_gather | solution.py:145
  75.5 5.7 %convolution_convert_fusion.2 = bf16[2048,312]{0,1:T(8,128)(2,1)S(1)} fusion(bf16[2048,1664]{1,0:T(8,128)(2,1)} %all-gather.5.cloned.1.call-done, bf16[1664,312]{0,1:T(8,128)(2,1)} %bitcast.189), kind=kOutput, calls=%fused_computation.38 | convolution fusion | flops 2127151104 | bytes 9132032 | tf_op jit(solution)/shard_map/dot_general | solution.py:52
  81.4 0.3 reshape_squeeze.12
  81.8 16.5 %while.12 = (s32[]{:T(128)}, bf16[4,512,1,104]{1,3,2,0:T(8,128)(2,1)S(1)}, s32[4]{0:T(128)S(1)}, s32[3]{0:T(128)S(1)}, s32[2048]{0:T(1024)S(1)}, /*index=5*/bf16...) while((s32[]{:T(128)}, ...), condition=%wide.region_8.9_spmd, body=%wide.region_4.8_spmd.sunk | while | flops 445709312 | bytes 13674625 | solution.py:81
  81.8 0.6 dynamic_slice.23
  82.4 0.7 add_select_fusion.3
  83.1 1.0 fusion.70
  84.1 0.7 fusion.71
  84.8 1.1 fusion.72
  85.9 0.6 dynamic_slice.23
  86.5 0.7 add_select_fusion.3
  87.2 1.0 fusion.70
  88.2 0.7 fusion.71
  88.9 1.1 fusion.72
  90.0 0.6 dynamic_slice.23
  90.6 0.7 add_select_fusion.3
  91.4 1.0 fusion.70
  92.3 0.7 fusion.71
  93.0 1.1 fusion.72
  94.2 0.6 dynamic_slice.23
  94.7 0.7 add_select_fusion.3
  95.5 1.0 fusion.70
  96.5 0.7 fusion.71
  97.2 1.1 fusion.72
  98.3 0.2 copy.29
  98.6 0.8 copy_bitcast_fusion
  99.5 5.3 %all-to-all-start = ((bf16[16,128,104]{1,2,0:T(8,128)(2,1)}), bf16[16,128,104]{1,2,0:T(8,128)(2,1)S(1)}, u32[]{:S(2)}, u32[]{:S(2)}) async-start(bf16[16,128,104]{1,2,0:T(8,128)(2,1)} %copy_bitcast_fusion), calls=%async_computation | async-start | bytes 851968 | tf_op jit(solution)/shard_map/all_to_all | solution.py:89
  104.7 31.9 %all-gather.7.cloned.1.call-done = bf16[1664,1664]{1,0:T(8,128)(2,1)} async-done(((bf16[104,1664]{1,0:T(8,128)(2,1)}), bf16[1664,1664]{1,0:T(8,128)(2,1)}) %all-gather.7.cloned.1.call-update) | async-done | bytes 5537808 | tf_op jit(solution)/shard_map/all_gather | solution.py:143
  136.6 3.7 %fusion.49 = (f32[128]{0:T(128)S(1)}, f32[128,1664]{1,0:T(8,128)S(1)}) fusion(bf16[128,1664]{0,1:T(8,128)(2,1)S(1)} %bitcast.177, bf16[1664,1664]{1,0:T(8,128)(2,1)} %all-gather.7.cloned.1.call-done, bf16[128,1664]{1,0:T(8,128)(2,1)S(1)} %copy-done.1), kind=kOutput, calls=%fused_computation.130 | convolution fusion | flops 709476224 | bytes 7242240 | tf_op jit(solution)/shard_map/dot_general | solution.py:159
  140.4 0.2 multiply_reduce_fusion.1
  140.8 0.6 all_to_all.27
  141.4 0.3 copy.31
  141.7 19.0 %all_to_all.39 = bf16[32,16,416]{2,0,1:T(8,128)(2,1)S(1)} all-to-all(bf16[32,16,416]{2,0,1:T(8,128)(2,1)S(1)} %copy.31), channel_id=1, replica_groups=mesh['seq'=16,'grp'=8] {'seq'}, dimensions={1} | all-to-all | bytes 851968 | tf_op jit(solution)/shard_map/all_to_all | solution.py:168
  160.8 2.3 convolution_convert_fusion
  163.1 3.8 %all-to-all-start.2 = ((bf16[16,32,1664]{2,1,0:T(8,128)(2,1)}), bf16[16,32,1664]{2,1,0:T(8,128)(2,1)S(1)}, u32[]{:S(2)}, u32[]{:S(2)}) async-start(bf16[16,32,1664]{2,1,0:T(8,128)(2,1)} %bitcast.178), calls=%async_computation.2 | async-start | bytes 3407872 | tf_op jit(solution)/shard_map/all_to_all | solution.py:170
  167.1 0.9 select_reduce_fusion
  167.9 0.7 iota_compare_fusion.5
  168.7 0.7 copy.32
  169.4 34.2 %all-to-all-done.2 = bf16[16,32,1664]{2,1,0:T(8,128)(2,1)S(1)} async-done(((bf16[16,32,1664]{2,1,0:T(8,128)(2,1)}), bf16[16,32,1664]{2,1,0:T(8,128)(2,1)S(1)}, u32[]{:S(2)}, u32[]{:S(2)}) %all-to-all-start.2) | async-done | bytes 1703968 | tf_op jit(solution)/shard_map/all_to_all | solution.py:170
  203.6 0.9 reduce_sum.139
  204.5 1.1 convolution_convert_fusion.3
  205.6 1.6 pad_maximum_fusion
  207.2 4.4 %all-to-all-start.3 = ((bf16[8,9,1664]{2,1,0:T(8,128)(2,1)}), bf16[8,9,1664]{2,1,0:T(8,128)(2,1)S(1)}, u32[]{:S(2)}, u32[]{:S(2)}) async-start(bf16[8,9,1664]{2,1,0:T(8,128)(2,1)} %pad_maximum_fusion), calls=%async_computation.3 | async-start | bytes 851968 | tf_op jit(solution)/shard_map/all_to_all | solution.py:192
  211.9 9.0 %all-to-all-done.3 = bf16[8,9,1664]{2,1,0:T(8,128)(2,1)S(1)} async-done(((bf16[8,9,1664]{2,1,0:T(8,128)(2,1)}), bf16[8,9,1664]{2,1,0:T(8,128)(2,1)S(1)}, u32[]{:S(2)}, u32[]{:S(2)}) %all-to-all-start.3) | async-done | bytes 239648 | tf_op jit(solution)/shard_map/all_to_all | solution.py:192
  221.1 0.5 multiply_reduce_fusion
  221.6 0.9 multiply_convert_fusion
  223.2 58.3 %all-gather.11.cloned.1.call-done = bf16[2048,1664]{1,0:T(8,128)(2,1)} async-done(((bf16[128,1664]{1,0:T(8,128)(2,1)}), bf16[2048,1664]{1,0:T(8,128)(2,1)}) %all-gather.11.cloned.1.call-update) | async-done | bytes 6815760 | tf_op jit(solution)/shard_map/all_gather | solution.py:212
  281.5 5.7 %convolution_convert_fusion.1 = bf16[2048,312]{0,1:T(8,128)(2,1)S(1)} fusion(bf16[2048,1664]{1,0:T(8,128)(2,1)} %all-gather.11.cloned.1.call-done, bf16[1664,312]{0,1:T(8,128)(2,1)} %bitcast.190), kind=kOutput, calls=%fused_computation.37 | convolution fusion | flops 2127151104 | bytes 9132032 | tf_op jit(solution)/shard_map/dot_general | solution.py:52
  287.2 0.4 fusion.53
  287.8 0.3 fusion.30
  288.3 0.7 fusion.52
  289.0 0.4 fusion.22
  289.3 0.5 fusion.29
  290.0 1.0 fusion.51
  291.0 0.5 fusion.17
  291.5 0.6 fusion.28
  292.2 1.3 fusion.50
  293.5 0.6 fusion.14
  294.2 0.8 fusion.27
  295.2 15.5 %all_to_all.40 = bf16[16,128,104]{1,2,0:T(8,128)(2,1)S(1)} all-to-all(bf16[16,128,104]{1,2,0:T(8,128)(2,1)S(1)} %copy.36), channel_id=1, replica_groups=mesh['seq'=16,'grp'=8] {'seq'}, dimensions={0} | all-to-all | bytes 851968 | tf_op jit(solution)/shard_map/all_to_all | solution.py:89
  310.7 1.9 convolution_add_fusion
  (68 shorter events, 2.6 us)
Async XLA Ops:
  6.5 154.2 %copy-start = (bf16[416,1664]{1,0:T(8,128)(2,1)S(1)}, bf16[416,1664]{1,0:T(8,128)(2,1)}, u32[]{:S(2)}) copy-start(bf16[416,1664]{1,0:T(8,128)(2,1)} %param.21) | copy-start | bytes 4153348
  6.5 69.0 %all-gather.5.cloned.1.call-start = ((), (), s32[]{:S(2)}) async-start(), calls=%async_computation.5 | async-start | bytes 7241728 | tf_op jit(solution)/shard_map/all_gather | solution.py:145
  8.8 127.9 %all-gather.7.cloned.1.call-start = ((), (), s32[]{:S(2)}) async-start(), calls=%async_computation.6 | async-start | bytes 5883904 | tf_op jit(solution)/shard_map/all_gather | solution.py:143
  9.5 213.0 %all-gather.9.cloned.1.call-start = ((), (), s32[]{:S(2)}) async-start(), calls=%async_computation.7 | async-start | bytes 5883904 | tf_op jit(solution)/shard_map/all_gather | solution.py:158
  98.3 38.4 %copy-start.1 = (bf16[128,1664]{1,0:T(8,128)(2,1)S(1)}, bf16[128,1664]{1,0:T(8,128)(2,1)}, u32[]{:S(2)}) copy-start(bf16[128,1664]{1,0:T(8,128)(2,1)} %x_ref.1) | copy-start | bytes 1277956
  99.5 37.2 %all-to-all-start = ((bf16[16,128,104]{1,2,0:T(8,128)(2,1)}), bf16[16,128,104]{1,2,0:T(8,128)(2,1)S(1)}, u32[]{:S(2)}, u32[]{:S(2)}) async-start(bf16[16,128,104]{1,2,0:T(8,128)(2,1)} %copy_bitcast_fusion), calls=%async_computation | async-start | bytes 851968 | tf_op jit(solution)/shard_map/all_to_all | solution.py:89
  136.6 4.0 %copy-start.3 = (f32[1664]{0:T(1024)S(1)}, f32[1664]{0:T(1024)}, u32[]{:S(2)}) copy-start(f32[1664]{0:T(1024)} %param.20) | copy-start | bytes 19972
  163.1 3.9 %copy-start.7 = (s32[32,1]{0,1:T(1,128)S(1)}, s32[32,1]{0,1:T(1,128)}, u32[]{:S(2)}) copy-start(s32[32,1]{0,1:T(1,128)} %param.23) | copy-start | bytes 388
  163.1 58.0 %copy-start.2 = (bf16[128,1664]{1,0:T(8,128)(2,1)S(1)}, bf16[128,1664]{1,0:T(8,128)(2,1)}, u32[]{:S(2)}) copy-start(bf16[128,1664]{1,0:T(8,128)(2,1)} %param.26) | copy-start | bytes 1277956
  163.1 40.5 %all-to-all-start.2 = ((bf16[16,32,1664]{2,1,0:T(8,128)(2,1)}), bf16[16,32,1664]{2,1,0:T(8,128)(2,1)S(1)}, u32[]{:S(2)}, u32[]{:S(2)}) async-start(bf16[16,32,1664]{2,1,0:T(8,128)(2,1)} %bitcast.178), calls=%async_computation.2 | async-start | bytes 3407872 | tf_op jit(solution)/shard_map/all_to_all | solution.py:170
  166.9 54.7 %copy-start.4 = (f32[1664]{0:T(1024)S(1)}, f32[1664]{0:T(1024)}, u32[]{:S(2)}) copy-start(f32[1664]{0:T(1024)} %param.27) | copy-start | bytes 19972
  167.1 44.8 %copy-start.8 = (s32[1,1,128]{2,1,0:T(1,128)S(1)}, s32[1,1,128]{2,1,0:T(1,128)}, u32[]{:S(2)}) copy-start(s32[1,1,128]{2,1,0:T(1,128)} %param.24) | copy-start | bytes 1540
  207.2 13.7 %all-to-all-start.3 = ((bf16[8,9,1664]{2,1,0:T(8,128)(2,1)}), bf16[8,9,1664]{2,1,0:T(8,128)(2,1)S(1)}, u32[]{:S(2)}, u32[]{:S(2)}) async-start(bf16[8,9,1664]{2,1,0:T(8,128)(2,1)} %pad_maximum_fusion), calls=%async_computation.3 | async-start | bytes 851968 | tf_op jit(solution)/shard_map/all_to_all | solution.py:192
  211.6 69.9 %all-gather.11.cloned.1.call-start = ((), (), s32[]{:S(2)}) async-start(), calls=%async_computation.8 | async-start | bytes 7241728 | tf_op jit(solution)/shard_map/all_gather | solution.py:212
  223.2 64.0 %copy-start.5 = (pred[2048]{0:T(1024)(128)(4,1)}, pred[2048]{0:T(1024)(128)(4,1)S(1)}, u32[]{:S(2)}) copy-start(pred[2048]{0:T(1024)(128)(4,1)S(1)} %iota_compare_fusion.4) | copy-start | bytes 6148
  287.6 0.7 slice-start.2
  289.3 0.7 copy-start.6
  293.5 17.2 %slice-start = ((s8[5537792]{0:T(1024)(128)(4,1)}), s8[1343488]{0:T(1024)(128)(4,1)S(1)}, s32[]{:S(2)}) async-start(s8[5537792]{0:T(1024)(128)(4,1)} %bitcast.175), calls=%async_computation.9 | async-start | bytes 2686976
  294.2 16.5 %slice-start.1 = ((s8[5537792]{0:T(1024)(128)(4,1)}), s8[4194304]{0:T(1024)(128)(4,1)S(1)}, s32[]{:S(2)}) async-start(s8[5537792]{0:T(1024)(128)(4,1)} %bitcast.175), calls=%async_computation.10 | async-start | bytes 8388608
Sparse Core Ops, SparseCore 0:
  9.5 66.0 all-gather.4
  77.7 58.9 all-gather.6
  138.8 70.9 all-gather.8
  222.7 58.8 all-gather.10

commit v13 on v12

--- a/solution.py
+++ b/solution.py
@@ -184,14 +184,21 @@
         (dest_rows[None, None, :] == jnp.arange(groups, dtype=jnp.int32)[:, None, None])
         & (slot_rank[None, None, :] == jnp.arange(capacity, dtype=jnp.int32)[None, :, None])
     ).astype(jnp.bfloat16)
+    arrived_flags = jnp.sum(selector.astype(jnp.float32), axis=2).astype(jnp.bfloat16)
+    selector_ext = jnp.concatenate(
+        [
+            jnp.pad(selector, ((0, 0), (0, 0), (0, capacity))),
+            jnp.pad(arrived_flags, ((0, 0), (merged_rows, 0)))[:, None, :],
+        ],
+        axis=1,
+    )
+    visual_ext = jnp.concatenate(
+        [visual, jnp.eye(capacity, model_width, dtype=jnp.bfloat16)], axis=0
+    )
     outgoing = jnp.einsum(
-        "gct,td->gcd", selector, visual, preferred_element_type=jnp.float32
+        "gct,td->gcd", selector_ext, visual_ext, preferred_element_type=jnp.float32
     ).astype(jnp.bfloat16)
-    arrived_flags = jnp.sum(selector.astype(jnp.float32), axis=2).astype(jnp.bfloat16)
-    flag_row = jnp.pad(arrived_flags, ((0, 0), (0, model_width - capacity)))[:, None, :]
-    payload = lax.all_to_all(
-        jnp.concatenate([outgoing, flag_row], axis=1), "grp", split_axis=0, concat_axis=0, tiled=True
-    )
+    payload = lax.all_to_all(outgoing, "grp", split_axis=0, concat_axis=0, tiled=True)
     incoming = payload[:, :capacity, :]
     arrived = payload[:, capacity, :capacity]
     prompt_rows = text_emb.shape[0]

time: 320 us -> 319 us (level)
  no operation moved by 1% of the time
where the time goes in v13:
time: 319 us; the launch traced here: 318 us
  waiting for transfers between devices  199 us (62%)
  matrix products  35.6 us (11%)
  blocking collectives  34.5 us (11%)
  between operations  14.1 us (4%)
  starting transfers between devices  13.8 us (4%)
  other arithmetic  13.2 us (4%)
  local copies, waits for them, and re-layouts  6.24 us (2%)
    all_gather x1, waiting for transfers between devices, per_device(): lax.all_gather(vis_normed, 'seq', axis=0, tiled=True)  65 us
    all_gather x1, waiting for transfers between devices, per_device(): lax.all_gather(txt_normed, 'seq', axis=0, tiled=True)  58.3 us
    all_to_all x1, waiting for transfers between devices, per_device(): lax.all_to_all(merge_partial.astype(jnp.bfloat16).reshape(seq_count, -1,...  34.2 us
    all_gather x1, waiting for transfers between devices, per_device(): vis_out_full = lax.all_gather(vis_out, 'seq', axis=0, tiled=True)  31.9 us
    all_to_all x1, blocking collectives, per_device(): lax.all_to_all(merged_in, 'seq', split_axis=1, concat_axis=0, tiled=True)  19 us
    all_to_all x1, blocking collectives, heads_to_rows(): lax.all_to_all(blocks, 'seq', split_axis=0, concat_axis=0, tiled=True)  15.5 us
    dot_general x2, matrix products, projector(): jnp.dot(shard_piece, packed, preferred_element_type=jnp.float32)  11.4 us
    all_to_all x1, waiting for transfers between devices, per_device(): lax.all_to_all(outgoing, 'grp', split_axis=0, concat_axis=0, tiled=True)  8.38 us
  transfers between devices with their start and end apart: 7, of which 5 were waited for; matrix products, arithmetic and copies ran while one was open for 12% of the time, Pallas kernels for 0%

profile of v13, /device:TPU:0, one launch (start us, length us, event | category | flops | bytes accessed | tf_op | source)
XLA Modules:
  0.0 318.2 jit_solution(1220994451754508729)
XLA Ops:
  6.5 2.2 shard_map.136
  8.8 0.7 all-gather.7.cloned.1.call-update
  9.6 0.8 reduce-window.4
  10.5 65.0 %all-gather.5.cloned.1.call-done = bf16[2048,1664]{1,0:T(8,128)(2,1)} async-done(((bf16[128,1664]{1,0:T(8,128)(2,1)}), bf16[2048,1664]{1,0:T(8,128)(2,1)}) %all-gather.5.cloned.1.call-update) | async-done | bytes 6815760 | tf_op jit(solution)/shard_map/all_gather | solution.py:145
  75.5 5.7 %convolution_convert_fusion.2 = bf16[2048,312]{0,1:T(8,128)(2,1)S(1)} fusion(bf16[2048,1664]{1,0:T(8,128)(2,1)} %all-gather.5.cloned.1.call-done, bf16[1664,312]{0,1:T(8,128)(2,1)} %bitcast.189), kind=kOutput, calls=%fused_computation.38 | convolution fusion | flops 2127151104 | bytes 9132032 | tf_op jit(solution)/shard_map/dot_general | solution.py:52
  81.4 0.3 reshape_squeeze.12
  81.8 16.5 %while.12 = (s32[]{:T(128)}, bf16[4,512,1,104]{1,3,2,0:T(8,128)(2,1)S(1)}, s32[4]{0:T(128)S(1)}, s32[3]{0:T(128)S(1)}, s32[2048]{0:T(1024)S(1)}, /*index=5*/bf16...) while((s32[]{:T(128)}, ...), condition=%wide.region_9.10_spmd, body=%wide.region_5.9_spmd.sunk | while | flops 445709312 | bytes 13674625 | solution.py:81
  81.8 0.6 dynamic_slice.23
  82.4 0.7 add_select_fusion.3
  83.1 1.0 fusion.79
  84.1 0.7 fusion.80
  84.8 1.1 fusion.81
  85.9 0.6 dynamic_slice.23
  86.5 0.7 add_select_fusion.3
  87.2 1.0 fusion.79
  88.2 0.7 fusion.80
  88.9 1.1 fusion.81
  90.0 0.6 dynamic_slice.23
  90.6 0.7 add_select_fusion.3
  91.4 1.0 fusion.79
  92.3 0.7 fusion.80
  93.0 1.1 fusion.81
  94.2 0.6 dynamic_slice.23
  94.7 0.7 add_select_fusion.3
  95.5 1.0 fusion.79
  96.5 0.7 fusion.80
  97.2 1.1 fusion.81
  98.3 0.2 copy.30
  98.6 0.8 copy_bitcast_fusion
  99.5 5.3 %all-to-all-start = ((bf16[16,128,104]{1,2,0:T(8,128)(2,1)}), bf16[16,128,104]{1,2,0:T(8,128)(2,1)S(1)}, u32[]{:S(2)}, u32[]{:S(2)}) async-start(bf16[16,128,104]{1,2,0:T(8,128)(2,1)} %copy_bitcast_fusion), calls=%async_computation | async-start | bytes 851968 | tf_op jit(solution)/shard_map/all_to_all | solution.py:89
  104.7 31.9 %all-gather.7.cloned.1.call-done = bf16[1664,1664]{1,0:T(8,128)(2,1)} async-done(((bf16[104,1664]{1,0:T(8,128)(2,1)}), bf16[1664,1664]{1,0:T(8,128)(2,1)}) %all-gather.7.cloned.1.call-update) | async-done | bytes 5537808 | tf_op jit(solution)/shard_map/all_gather | solution.py:143
  136.6 3.7 %fusion.58 = (f32[128]{0:T(128)S(1)}, f32[128,1664]{1,0:T(8,128)S(1)}) fusion(bf16[128,1664]{0,1:T(8,128)(2,1)S(1)} %bitcast.177, bf16[1664,1664]{1,0:T(8,128)(2,1)} %all-gather.7.cloned.1.call-done, bf16[128,1664]{1,0:T(8,128)(2,1)S(1)} %copy-done.1), kind=kOutput, calls=%fused_computation.140 | convolution fusion | flops 709476224 | bytes 7242240 | tf_op jit(solution)/shard_map/dot_general | solution.py:159
  140.4 0.2 multiply_reduce_fusion.1
  140.8 0.6 all_to_all.27
  141.4 0.3 copy.32
  141.7 19.0 %all_to_all.39 = bf16[32,16,416]{2,0,1:T(8,128)(2,1)S(1)} all-to-all(bf16[32,16,416]{2,0,1:T(8,128)(2,1)S(1)} %copy.32), channel_id=1, replica_groups=mesh['seq'=16,'grp'=8] {'seq'}, dimensions={1} | all-to-all | bytes 851968 | tf_op jit(solution)/shard_map/all_to_all | solution.py:168
  160.8 2.3 convolution_convert_fusion
  163.1 3.8 %all-to-all-start.2 = ((bf16[16,32,1664]{2,1,0:T(8,128)(2,1)}), bf16[16,32,1664]{2,1,0:T(8,128)(2,1)S(1)}, u32[]{:S(2)}, u32[]{:S(2)}) async-start(bf16[16,32,1664]{2,1,0:T(8,128)(2,1)} %bitcast.178), calls=%async_computation.2 | async-start | bytes 3407872 | tf_op jit(solution)/shard_map/all_to_all | solution.py:170
  167.1 0.8 select_reduce_fusion
  167.9 0.7 iota_compare_fusion.7
  168.8 0.6 and_convert_fusion
  169.4 34.2 %all-to-all-done.2 = bf16[16,32,1664]{2,1,0:T(8,128)(2,1)S(1)} async-done(((bf16[16,32,1664]{2,1,0:T(8,128)(2,1)}), bf16[16,32,1664]{2,1,0:T(8,128)(2,1)S(1)}, u32[]{:S(2)}, u32[]{:S(2)}) %all-to-all-start.2) | async-done | bytes 1703968 | tf_op jit(solution)/shard_map/all_to_all | solution.py:170
  203.6 0.9 reduce_sum.140
  204.5 1.9 convolution_convert_fusion.3
  206.4 4.4 %all-to-all-start.3 = ((bf16[8,9,1664]{2,1,0:T(8,128)(2,1)}), bf16[8,9,1664]{2,1,0:T(8,128)(2,1)S(1)}, u32[]{:S(2)}, u32[]{:S(2)}) async-start(bf16[8,9,1664]{2,1,0:T(8,128)(2,1)} %convolution_convert_fusion.3), calls=%async_computation.3 | async-start | bytes 851968 | tf_op jit(solution)/shard_map/all_to_all | solution.py:201
  211.0 0.7 slice_bitcast_fusion.29
  211.7 8.4 %all-to-all-done.3 = bf16[8,9,1664]{2,1,0:T(8,128)(2,1)S(1)} async-done(((bf16[8,9,1664]{2,1,0:T(8,128)(2,1)}), bf16[8,9,1664]{2,1,0:T(8,128)(2,1)S(1)}, u32[]{:S(2)}, u32[]{:S(2)}) %all-to-all-start.3) | async-done | bytes 239648 | tf_op jit(solution)/shard_map/all_to_all | solution.py:201
  220.3 0.5 multiply_reduce_fusion
  220.8 0.9 multiply_convert_fusion
  222.4 58.3 %all-gather.11.cloned.1.call-done = bf16[2048,1664]{1,0:T(8,128)(2,1)} async-done(((bf16[128,1664]{1,0:T(8,128)(2,1)}), bf16[2048,1664]{1,0:T(8,128)(2,1)}) %all-gather.11.cloned.1.call-update) | async-done | bytes 6815760 | tf_op jit(solution)/shard_map/all_gather | solution.py:219
  280.7 5.7 %convolution_convert_fusion.1 = bf16[2048,312]{0,1:T(8,128)(2,1)S(1)} fusion(bf16[2048,1664]{1,0:T(8,128)(2,1)} %all-gather.11.cloned.1.call-done, bf16[1664,312]{0,1:T(8,128)(2,1)} %bitcast.190), kind=kOutput, calls=%fused_computation.37 | convolution fusion | flops 2127151104 | bytes 9132032 | tf_op jit(solution)/shard_map/dot_general | solution.py:52
  286.4 0.4 fusion.62
  287.0 0.3 fusion.30
  287.4 0.7 fusion.61
  288.1 0.4 fusion.22
  288.5 0.5 fusion.29
  289.1 1.0 fusion.60
  290.1 0.5 fusion.17
  290.6 0.6 fusion.28
  291.3 1.3 fusion.59
  292.6 0.6 fusion.14
  293.3 0.8 fusion.27
  294.3 15.5 %all_to_all.40 = bf16[16,128,104]{1,2,0:T(8,128)(2,1)S(1)} all-to-all(bf16[16,128,104]{1,2,0:T(8,128)(2,1)S(1)} %copy.36), channel_id=1, replica_groups=mesh['seq'=16,'grp'=8] {'seq'}, dimensions={0} | all-to-all | bytes 851968 | tf_op jit(solution)/shard_map/all_to_all | solution.py:89
  309.8 1.9 convolution_add_fusion
  (67 shorter events, 2.6 us)
Async XLA Ops:
  6.5 154.2 %copy-start = (bf16[416,1664]{1,0:T(8,128)(2,1)S(1)}, bf16[416,1664]{1,0:T(8,128)(2,1)}, u32[]{:S(2)}) copy-start(bf16[416,1664]{1,0:T(8,128)(2,1)} %param.21) | copy-start | bytes 4153348
  6.5 69.0 %all-gather.5.cloned.1.call-start = ((), (), s32[]{:S(2)}) async-start(), calls=%async_computation.5 | async-start | bytes 7241728 | tf_op jit(solution)/shard_map/all_gather | solution.py:145
  8.8 127.9 %all-gather.7.cloned.1.call-start = ((), (), s32[]{:S(2)}) async-start(), calls=%async_computation.6 | async-start | bytes 5883904 | tf_op jit(solution)/shard_map/all_gather | solution.py:143
  9.5 212.2 %all-gather.9.cloned.1.call-start = ((), (), s32[]{:S(2)}) async-start(), calls=%async_computation.7 | async-start | bytes 5883904 | tf_op jit(solution)/shard_map/all_gather | solution.py:158
  98.3 38.4 %copy-start.1 = (bf16[128,1664]{1,0:T(8,128)(2,1)S(1)}, bf16[128,1664]{1,0:T(8,128)(2,1)}, u32[]{:S(2)}) copy-start(bf16[128,1664]{1,0:T(8,128)(2,1)} %x_ref.1) | copy-start | bytes 1277956
  99.5 37.2 %all-to-all-start = ((bf16[16,128,104]{1,2,0:T(8,128)(2,1)}), bf16[16,128,104]{1,2,0:T(8,128)(2,1)S(1)}, u32[]{:S(2)}, u32[]{:S(2)}) async-start(bf16[16,128,104]{1,2,0:T(8,128)(2,1)} %copy_bitcast_fusion), calls=%async_computation | async-start | bytes 851968 | tf_op jit(solution)/shard_map/all_to_all | solution.py:89
  136.6 4.0 %copy-start.3 = (f32[1664]{0:T(1024)S(1)}, f32[1664]{0:T(1024)}, u32[]{:S(2)}) copy-start(f32[1664]{0:T(1024)} %param.20) | copy-start | bytes 19972
  163.1 3.9 %copy-start.7 = (s32[32,1]{0,1:T(1,128)S(1)}, s32[32,1]{0,1:T(1,128)}, u32[]{:S(2)}) copy-start(s32[32,1]{0,1:T(1,128)} %param.23) | copy-start | bytes 388
  163.1 57.2 %copy-start.2 = (bf16[128,1664]{1,0:T(8,128)(2,1)S(1)}, bf16[128,1664]{1,0:T(8,128)(2,1)}, u32[]{:S(2)}) copy-start(bf16[128,1664]{1,0:T(8,128)(2,1)} %param.26) | copy-start | bytes 1277956
  163.1 40.5 %all-to-all-start.2 = ((bf16[16,32,1664]{2,1,0:T(8,128)(2,1)}), bf16[16,32,1664]{2,1,0:T(8,128)(2,1)S(1)}, u32[]{:S(2)}, u32[]{:S(2)}) async-start(bf16[16,32,1664]{2,1,0:T(8,128)(2,1)} %bitcast.178), calls=%async_computation.2 | async-start | bytes 3407872 | tf_op jit(solution)/shard_map/all_to_all | solution.py:170
  166.9 53.9 %copy-start.4 = (f32[1664]{0:T(1024)S(1)}, f32[1664]{0:T(1024)}, u32[]{:S(2)}) copy-start(f32[1664]{0:T(1024)} %param.27) | copy-start | bytes 19972
  206.4 13.7 %all-to-all-start.3 = ((bf16[8,9,1664]{2,1,0:T(8,128)(2,1)}), bf16[8,9,1664]{2,1,0:T(8,128)(2,1)S(1)}, u32[]{:S(2)}, u32[]{:S(2)}) async-start(bf16[8,9,1664]{2,1,0:T(8,128)(2,1)} %convolution_convert_fusion.3), calls=%async_computation.3 | async-start | bytes 851968 | tf_op jit(solution)/shard_map/all_to_all | solution.py:201
  210.8 69.9 %all-gather.11.cloned.1.call-start = ((), (), s32[]{:S(2)}) async-start(), calls=%async_computation.8 | async-start | bytes 7241728 | tf_op jit(solution)/shard_map/all_gather | solution.py:219
  222.4 64.0 %copy-start.5 = (pred[2048]{0:T(1024)(128)(4,1)}, pred[2048]{0:T(1024)(128)(4,1)S(1)}, u32[]{:S(2)}) copy-start(pred[2048]{0:T(1024)(128)(4,1)S(1)} %iota_compare_fusion.6) | copy-start | bytes 6148
  286.8 0.6 slice-start.2
  288.5 0.6 copy-start.6
  292.6 17.1 %slice-start = ((s8[5537792]{0:T(1024)(128)(4,1)}), s8[1343488]{0:T(1024)(128)(4,1)S(1)}, s32[]{:S(2)}) async-start(s8[5537792]{0:T(1024)(128)(4,1)} %bitcast.175), calls=%async_computation.9 | async-start | bytes 2686976
  293.2 16.5 %slice-start.1 = ((s8[5537792]{0:T(1024)(128)(4,1)}), s8[4194304]{0:T(1024)(128)(4,1)S(1)}, s32[]{:S(2)}) async-start(s8[5537792]{0:T(1024)(128)(4,1)} %bitcast.175), calls=%async_computation.10 | async-start | bytes 8388608
Sparse Core Ops, SparseCore 0:
  9.5 66.0 all-gather.4
  77.7 58.9 all-gather.6
  138.8 70.9 all-gather.8
  221.9 58.8 all-gather.10
